TPU v7x, 32 devices: a whole 2x2x4 slice. The times are simulated.
32 devices in a mesh: sect: 4 (over z), slab: 8 (over y, x, core).
Axes of the slice: x: 2, y: 2, z: 4, core: 2. Of those that a mesh axis runs over, the one named last changes fastest.
Arguments:
- vapor: float32 [30, 128, 4096], P(None, 'slab', 'sect'), may hold values from 0 to 0.05
- gas_temp: float32 [128, 4096], P('slab', 'sect'), may hold values from 1 to 2
- masses: float32 [30, 131072], P(None, ('sect', 'slab')), may hold values from 0.1 to 1
- drop_temp: float32 [131072], P(('sect', 'slab')), may hold values from 0.6 to 1.2
- cells: int32 [131072], P(('sect', 'slab')), may hold values from 0 to 65535
- flags: int32 [131072], P(('sect', 'slab')), may hold values 0 or 1
- moves: int32 [131072], P(('sect', 'slab')), may hold values from 0 to 2, as said below
- volat_a: float32 [30], replicated, may hold values from 1 to 3
- volat_b: float32 [30], replicated, may hold values from 1 to 4
- latent: float32 [30], replicated, may hold values from 0.5 to 5
Outputs:
- gas_next: float32 [31, 128, 4096], P(None, 'slab', 'sect')
- kept: float32 [31, 131072], P(None, ('sect', 'slab'))
- arrivals: float32 [31, 65536], P(None, ('sect', 'slab'))
Inputs may be any that keep to these rules, and one draw needn't show every extreme that they name: In each device's 4096 parcels at most 1024 have moves 1 and at most 1024 have moves 2; some device has exactly 1024 with moves 1 and some device has exactly 1024 with moves 2.
All inputs are finite; a program needn't handle non-finite values. No bound on the sum of `flags` on one device may be relied on, other than what follows from the above.
Results may differ from a plain program's by a relative error of at most 0.0001.
Values sent between devices are 32-bit elements; how exact they have to be, the bound alone decides.
No kernel may reach another device: no remote copies, remote signals or barrier semaphores. Data moves between devices by JAX's collectives and lax.ppermute only.
A program may use at most 128 MiB of HBM per device.

v0:
```python
import jax
import jax.numpy as jnp
from jax import lax
from jax.sharding import PartitionSpec as P

NC = 30
RR_ITERS = 4
MOVE_CAP = 1024


def with_halo(block, sides, width):
    for axis, dim in sides:
        count = lax.axis_size(axis)
        forward = [(i, i + 1) for i in range(count - 1)]
        backward = [(target, source) for source, target in forward]
        low = lax.ppermute(
            lax.slice_in_dim(block, block.shape[dim] - width, None, axis=dim), axis, forward
        )
        high = lax.ppermute(lax.slice_in_dim(block, 0, width, axis=dim), axis, backward)
        block = jnp.concatenate([low, block, high], axis=dim)
    return block


def shifted(shard, axis, by):
    length = lax.axis_size(axis)
    pairs = [(i, i + by) for i in range(length) if 0 <= i + by < length]
    return lax.ppermute(shard, axis, pairs)


def parcel_update(masses, drop_temp, flags, vap_p, temp_p, volat_a, volat_b, latent):
    total = jnp.sum(masses, axis=0)
    frac = masses / total[None]
    surf = 0.5 * (drop_temp + temp_p)
    ratio = jnp.exp(volat_a[:, None] - volat_b[:, None] / surf[None])
    excess = ratio - 1.0
    share = jnp.full(total.shape, 0.5, jnp.float32)
    for sweep in range(RR_ITERS):
        denom = 1.0 + share[None] * excess
        residue = jnp.sum(frac * excess / denom, axis=0)
        slope = jnp.sum(frac * excess * excess / (denom * denom), axis=0) + 0.1
        share = jnp.clip(share + residue / slope, 0.02, 0.98)
    effect = flags.astype(jnp.float32) * share
    vap_eq = frac * ratio / (1.0 + effect[None] * excess)
    evap = 0.02 * total[None] * (vap_eq - vap_p)
    new_mass = masses - evap
    new_temp = (
        drop_temp
        + 0.2 * (temp_p - drop_temp)
        - 0.5 * jnp.sum(latent[:, None] * evap, axis=0) / total
    )
    heat = total * (drop_temp - temp_p)
    state = jnp.concatenate([new_mass, new_temp[None]], axis=0)
    terms = jnp.concatenate([0.1 * evap, 0.05 * heat[None]], axis=0)
    return (state, terms)


def pack_slots(state, chosen):
    slot = jnp.cumsum(chosen.astype(jnp.int32)) - 1
    slot = jnp.where(chosen, slot, MOVE_CAP)
    buffer = jnp.zeros((MOVE_CAP, state.shape[0]), jnp.float32)
    return buffer.at[slot].set(state.T, mode="drop").T


def body(vapor, gas_temp, masses, drop_temp, cells, flags, moves, volat_a, volat_b, latent):
    gas_block = jnp.concatenate([vapor, gas_temp[None]], axis=0)
    fields, width_x, width_yz = gas_block.shape
    sections = lax.axis_size("sect")
    own_sect = lax.axis_index("sect")
    plane = sections * width_yz
    all_cells = lax.all_gather(cells, "sect", axis=0, tiled=True)
    cell_row = all_cells // plane
    cell_col = all_cells % plane
    owner_sect = cell_col // width_yz
    local_cell = cell_row * width_yz + cell_col % width_yz
    picked = jnp.take(gas_block.reshape(fields, width_x * width_yz), local_cell, axis=1)
    picked = jnp.where((owner_sect == own_sect)[None], picked, 0.0)
    at_parcel = lax.psum_scatter(picked, "sect", scatter_dimension=1, tiled=True)
    state, terms = parcel_update(
        masses, drop_temp, flags, at_parcel[:NC], at_parcel[NC], volat_a, volat_b, latent
    )
    padded = with_halo(gas_block, (("slab", 1),), 1)
    down = padded[:, :-2]
    upper = padded[:, 2:]
    flowed = gas_block + 0.2 * (upper - 2.0 * gas_block + down) - 0.3 * (gas_block - down)
    all_terms, all_cells = (
        lax.all_gather(terms, "sect", axis=1, tiled=True),
        lax.all_gather(cells, "sect", axis=0, tiled=True),
    )
    cell_row = all_cells // plane
    cell_col = all_cells % plane
    owner_sect = cell_col // width_yz
    local_cell = cell_row * width_yz + cell_col % width_yz
    segment_ids = jnp.where(owner_sect == own_sect, local_cell, width_x * width_yz).astype(
        jnp.int32
    )
    summed = jax.ops.segment_sum(all_terms.T, segment_ids, width_x * width_yz + 1)
    source = summed[: width_x * width_yz].T.reshape(fields, width_x, width_yz)
    gas_next = flowed + source
    kept = jnp.where(moves[None] == 0, state, 0.0)
    from_prev = shifted(pack_slots(state, moves == 2), "slab", 1)
    from_next = shifted(pack_slots(state, moves == 1), "slab", -1)
    arrivals = jnp.concatenate([from_prev, from_next], axis=1)
    return (gas_next, kept, arrivals)


def solution(mesh):
    in_specs = (
        P(None, "slab", "sect"),
        P("slab", "sect"),
        P(None, ("sect", "slab")),
        P(("sect", "slab")),
        P(("sect", "slab")),
        P(("sect", "slab")),
        P(("sect", "slab")),
        P(),
        P(),
        P(),
    )
    out_specs = (P(None, "slab", "sect"), P(None, ("sect", "slab")), P(None, ("sect", "slab")))
    return jax.shard_map(body, mesh=mesh, in_specs=in_specs, out_specs=out_specs, check_vma=False)
```

profile of v0, /device:TPU:3, one launch (start us, length us, event | category | flops | bytes accessed | tf_op | source)
XLA Modules:
  0.0 312.2 jit_solution(2320441178170594106)
XLA Ops:
  7.2 11.1 %all_gather.7 = s32[16384]{0:T(1024)S(1)} all-gather(s32[4096]{0:T(1024)} %param.14), channel_id=1, replica_groups=mesh['sect'=4,'slab'=8] {'sect'}, dimensions={0}, use_global_device_ids=true | all-gather | bytes 81920 | tf_op jit(solution)/shard_map/all_gather | solution.py:87
  19.4 1.7 pad.23
  21.1 1.2 copy.66
  22.5 4.7 %copy.57 = f32[31,16384]{0,1:T(8,128)} copy(f32[31,16384]{1,0:T(8,128)S(1)} %pad_maximum_fusion.5) | data formatting | bytes 4063232 | tf_op jit(solution)/shard_map/concatenate | solution.py:65
  28.0 57.8 %gather_fusion = f32[16384,31]{1,0:T(8,128)} fusion(f32[31,16384]{0,1:T(8,128)} %copy.57, s32[16384]{0:T(1024)S(1)} %get-tuple-element.42), kind=kCustom, calls=%fused_computation | custom fusion | bytes 4128768 | tf_op jit(solution)/shard_map/jit(_take)/gather | solution.py:75
  85.7 5.2 %copy.58 = f32[16384,31]{0,1:T(8,128)S(1)} copy(f32[16384,31]{1,0:T(8,128)} %gather_fusion) | data formatting | bytes 4063232 | tf_op jit(solution)/shard_map/jit(_take)/gather | solution.py:75
  91.0 1.6 select_bitcast_fusion
  93.7 45.9 %reduce-scatter.2.cloned.1.call-done = f32[31,4096]{1,0:T(8,128)} async-done(((f32[31,16384]{1,0:T(8,128)}), f32[31,4096]{1,0:T(8,128)}) %reduce-scatter.2.cloned.1.call-update) | async-done | bytes 507920 | tf_op jit(solution)/shard_map/reduce_scatter | solution.py:77
  139.6 1.0 slice.54
  146.6 11.4 %scatter_custom_fusion.2 = f32[1024,31]{1,0:T(8,128)} fusion(s32[4096]{0:T(1024)S(1)} %get-tuple-element.48, f32[4096,31]{1,0:T(8,128)S(1)} %copy.61, f32[]{:T(128)} %constant.98.clone.1), kind=kCustom, calls=%fused_computation.51 | custom fusion | bytes 126980 | tf_op jit(solution)/shard_map/scatter | solution.py:61
  158.0 3.0 collective-permute-start.3
  161.0 11.4 %scatter_custom_fusion.1 = f32[1024,31]{1,0:T(8,128)} fusion(s32[4096]{0:T(1024)S(1)} %get-tuple-element.49, f32[4096,31]{1,0:T(8,128)S(1)} %copy.61, f32[]{:T(128)} %constant.98.clone.1), kind=kCustom, calls=%fused_computation.53 | custom fusion | bytes 126980 | tf_op jit(solution)/shard_map/scatter | solution.py:61
  172.4 3.6 %collective-permute-start.2 = (f32[31,1024]{0,1:T(8,128)}, f32[31,1024]{0,1:T(8,128)}, u32[]{:S(2)}, u32[]{:S(2)}) collective-permute-start(f32[31,1024]{0,1:T(8,128)} %bitcast.11), channel_id=1, source_target_pairs={{0,1},{1,2},{2,3},{3,4},{4,5},{5,6},{6,7},{8,9},{9,10},{10,11},{11... | collective-permute-start | bytes 380936 | tf_op jit(solution)/shard_map/ppermute | solution.py:27
  176.0 2.7 copy.55
  178.8 1.9 collective-permute-start
  180.7 4.7 %collective-permute-start.1 = (f32[31,1,1024]{2,0,1:T(8,128)S(1)}, f32[31,1,1024]{2,0,1:T(8,128)S(1)}, u32[]{:S(2)}, u32[]{:S(2)}) collective-permute-start(f32[31,1,1024]{2,0,1:T(8,128)S(1)} %get-tuple-element.36), channel_id=1, source_target_pairs={{0,1},{1,2},{2,3},{3,4},{4,5},{5,6},{6,7},{8,9},{9,10},{10,11},{11... | collective-permute-start | bytes 380936 | tf_op jit(solution)/shard_map/ppermute | solution.py:16
  185.7 1.2 copy.63
  187.7 1.5 all-gather.2.cloned.1.call-done
  189.1 6.3 %copy.59 = f32[16384,31]{1,0:T(8,128)} copy(f32[16384,31]{0,1:T(8,128)} %bitcast.35) | data formatting | bytes 4063232 | tf_op jit(solution)/shard_map/transpose | solution.py:96
  195.4 93.1 %scatter_custom_fusion = f32[16385,31]{1,0:T(8,128)} fusion(s32[16384]{0:T(1024)} %get-tuple-element.34, f32[16384,31]{1,0:T(8,128)} %copy.59, f32[]{:T(128)} %constant.98.clone.1), kind=kCustom, calls=%fused_computation.4 | custom fusion | flops 507904 | bytes 2032252 | tf_op jit(solution)/shard_map/scatter-add | solution.py:96
  288.6 5.7 %slice.56 = f32[16384,31]{1,0:T(8,128)} slice(f32[16385,31]{1,0:T(8,128)} %scatter_custom_fusion), slice={[0:16384], [0:31]} | slice | bytes 4063232 | tf_op jit(solution)/shard_map/slice | solution.py:97
  294.2 6.4 %copy.60 = f32[31,16,1024]{2,0,1:T(8,128)} copy(f32[31,16,1024]{0,2,1:T(8,128)} %bitcast.32) | data formatting | bytes 4063232 | tf_op jit(solution)/shard_map/reshape | solution.py:97
  300.6 2.3 fusion.7
  302.9 2.5 copy.65
  (61 shorter events, 9.9 us)
Async XLA Ops:
  7.2 132.5 %reduce-scatter.2.cloned.1.call-start = ((), (), s32[]{:S(2)}) async-start(), calls=%async_computation.1 | async-start | bytes 2621440 | tf_op jit(solution)/shard_map/reduce_scatter | solution.py:77
  92.6 1.0 copy-start
  92.6 48.0 %copy-start.3 = (f32[4096]{0:T(1024)S(1)}, f32[4096]{0:T(1024)}, u32[]{:S(2)}) copy-start(f32[4096]{0:T(1024)} %param.13) | copy-start | bytes 49156
  92.6 48.1 %copy-start.6 = (f32[30]{0:T(128)S(1)}, f32[30]{0:T(128)}, u32[]{:S(2)}) copy-start(f32[30]{0:T(128)} %param.18) | copy-start | bytes 364
  92.6 48.1 %copy-start.7 = (f32[30]{0:T(128)S(1)}, f32[30]{0:T(128)}, u32[]{:S(2)}) copy-start(f32[30]{0:T(128)} %param.17) | copy-start | bytes 364
  92.6 49.9 %copy-start.4 = (s32[4096]{0:T(1024)S(1)}, s32[4096]{0:T(1024)}, u32[]{:S(2)}) copy-start(s32[4096]{0:T(1024)} %param.15) | copy-start | bytes 49156
  92.6 96.5 %all-gather.2.cloned.1.call-start = ((), (), s32[]{:S(2)}) async-start(), calls=%async_computation.2 | async-start | bytes 2621440 | tf_op jit(solution)/shard_map/all_gather | solution.py:86
  139.6 2.9 copy-start.1
  141.1 1.7 copy-start.8
  142.5 1.4 copy-start.5
  158.0 27.5 %collective-permute-start.3 = (f32[31,1024]{0,1:T(8,128)}, f32[31,1024]{0,1:T(8,128)S(1)}, u32[]{:S(2)}, u32[]{:S(2)}) collective-permute-start(f32[31,1024]{0,1:T(8,128)} %bitcast.14), channel_id=1, source_target_pairs={{1,0},{2,1},{3,2},{4,3},{5,4},{6,5},{7,6},{9,8},{10,9},{11,10},{12... | collective-permute-start | bytes 380936 | tf_op jit(solution)/shard_map/ppermute | solution.py:27
  172.4 6.3 %copy-start.2 = (f32[16,1024]{1,0:T(8,128)S(1)}, f32[16,1024]{1,0:T(8,128)}, u32[]{:S(2)}) copy-start(f32[16,1024]{1,0:T(8,128)} %param.11) | copy-start | bytes 196612
  172.4 13.3 %collective-permute-start.2 = (f32[31,1024]{0,1:T(8,128)}, f32[31,1024]{0,1:T(8,128)}, u32[]{:S(2)}, u32[]{:S(2)}) collective-permute-start(f32[31,1024]{0,1:T(8,128)} %bitcast.11), channel_id=1, source_target_pairs={{0,1},{1,2},{2,3},{3,4},{4,5},{5,6},{6,7},{8,9},{9,10},{10,11},{11... | collective-permute-start | bytes 380936 | tf_op jit(solution)/shard_map/ppermute | solution.py:27
  178.8 121.8 %collective-permute-start = (f32[31,1,1024]{2,0,1:T(8,128)S(1)}, f32[31,1,1024]{2,0,1:T(8,128)S(1)}, u32[]{:S(2)}, u32[]{:S(2)}) collective-permute-start(f32[31,1,1024]{2,0,1:T(8,128)S(1)} %get-tuple-element.37), channel_id=1, source_target_pairs={{1,0},{2,1},{3,2},{4,3},{5,4},{6,5},{7,6},{9,8},{10,9},{11,10},{12... | collective-permute-start | bytes 380936 | tf_op jit(solution)/shard_map/ppermute | solution.py:19
  180.7 119.9 %collective-permute-start.1 = (f32[31,1,1024]{2,0,1:T(8,128)S(1)}, f32[31,1,1024]{2,0,1:T(8,128)S(1)}, u32[]{:S(2)}, u32[]{:S(2)}) collective-permute-start(f32[31,1,1024]{2,0,1:T(8,128)S(1)} %get-tuple-element.36), channel_id=1, source_target_pairs={{0,1},{1,2},{2,3},{3,4},{4,5},{5,6},{6,7},{8,9},{9,10},{10,11},{11... | collective-permute-start | bytes 380936 | tf_op jit(solution)/shard_map/ppermute | solution.py:16
Sparse Core Ops, SparseCore 0:
  92.7 46.8 reduce-scatter.1
  144.0 45.0 all-gather.1
where the time goes:
time: 314 us; the launch traced here: 312 us
  local copies, waits for them, and re-layouts  122 us (39%)
  other arithmetic  104 us (33%)
  waiting for transfers between devices  47.5 us (15%)
  between operations  14.4 us (5%)
  starting transfers between devices  13.3 us (4%)
  blocking collectives  11.1 us (4%)
    scatter-add x1, other arithmetic, body(): jax.ops.segment_sum(all_terms.T, segment_ids, width_x * width_yz + 1)  93.1 us
    gather x2, local copies, waits for them, and re-layouts, body(): jnp.take(gas_block.reshape(fields, width_x * width_yz), local_cell, axis=1)  63 us
    reduce_scatter x1, waiting for transfers between devices, body(): lax.psum_scatter(picked, 'sect', scatter_dimension=1, tiled=True)  45.9 us
    scatter x2, local copies, waits for them, and re-layouts, pack_slots(): return buffer.at[slot].set(state.T, mode='drop').T  22.8 us
    all_gather x1, blocking collectives, body(): lax.all_gather(cells, 'sect', axis=0, tiled=True)  11.1 us
    unnamed x23, local copies, waits for them, and re-layouts  10 us
    ppermute x2, starting transfers between devices, shifted(): return lax.ppermute(shard, axis, pairs)  6.57 us
    reshape x1, local copies, waits for them, and re-layouts, body(): source = summed[:width_x * width_yz].T.reshape(fields, width_x, width_yz)  6.35 us
  transfers between devices with their start and end apart: 6, of which 2 were waited for; matrix products, arithmetic and copies ran while one was open for 45% of the time, Pallas kernels for 0%

commit v1 on v0

--- a/solution.py
+++ b/solution.py
@@ -1,11 +1,14 @@
 import jax
 import jax.numpy as jnp
 from jax import lax
+from jax.experimental import pallas as pl
+from jax.experimental.pallas import tpu as pltpu
 from jax.sharding import PartitionSpec as P
 
 NC = 30
 RR_ITERS = 4
 MOVE_CAP = 1024
+UNROLL = 8
 
 
 def with_halo(block, sides, width):
@@ -61,19 +64,85 @@
     return buffer.at[slot].set(state.T, mode="drop").T
 
 
+def _gather_kernel(count_ref, order_ref, local_ref, table_ref, out_ref):
+    out_ref[...] = jnp.zeros(out_ref.shape, out_ref.dtype)
+
+    def step(i, carry):
+        base = i * UNROLL
+        for j in range(UNROLL):
+            p = order_ref[base + j]
+            out_ref[pl.ds(p, 1), :] = table_ref[pl.ds(local_ref[p], 1), :]
+        return carry
+
+    lax.fori_loop(0, (count_ref[0] + UNROLL - 1) // UNROLL, step, 0)
+
+
+def _scatter_kernel(count_ref, order_ref, seg_ref, rows_ref, out_ref, acc_ref):
+    acc_ref[...] = jnp.zeros(acc_ref.shape, acc_ref.dtype)
+
+    def step(i, carry):
+        base = i * UNROLL
+        for j in range(UNROLL):
+            p = order_ref[base + j]
+            s = seg_ref[p]
+            acc_ref[pl.ds(s, 1), :] += rows_ref[pl.ds(p, 1), :]
+        return carry
+
+    lax.fori_loop(0, (count_ref[0] + UNROLL - 1) // UNROLL, step, 0)
+    out_ref[...] = acc_ref[pl.ds(0, out_ref.shape[0]), :]
+
+
+def row_gather(count, order, local, table):
+    n_out = order.shape[0]
+    n_tab, width = table.shape
+    spec = pltpu.PrefetchScalarGridSpec(
+        num_scalar_prefetch=3,
+        grid=(1,),
+        in_specs=[pl.BlockSpec((n_tab, width), lambda i, *_: (0, 0))],
+        out_specs=pl.BlockSpec((n_out, width), lambda i, *_: (0, 0)),
+    )
+    return pl.pallas_call(
+        _gather_kernel,
+        grid_spec=spec,
+        out_shape=jax.ShapeDtypeStruct((n_out, width), table.dtype),
+    )(count, order, local, table)
+
+
+def row_scatter_add(count, order, seg, rows, n_cells):
+    n_rows, width = rows.shape
+    spec = pltpu.PrefetchScalarGridSpec(
+        num_scalar_prefetch=3,
+        grid=(1,),
+        in_specs=[pl.BlockSpec((n_rows, width), lambda i, *_: (0, 0))],
+        out_specs=pl.BlockSpec((n_cells, width), lambda i, *_: (0, 0)),
+        scratch_shapes=[pltpu.VMEM((n_cells + UNROLL, width), jnp.float32)],
+    )
+    return pl.pallas_call(
+        _scatter_kernel,
+        grid_spec=spec,
+        out_shape=jax.ShapeDtypeStruct((n_cells, width), rows.dtype),
+    )(count, order, seg, rows)
+
+
 def body(vapor, gas_temp, masses, drop_temp, cells, flags, moves, volat_a, volat_b, latent):
     gas_block = jnp.concatenate([vapor, gas_temp[None]], axis=0)
     fields, width_x, width_yz = gas_block.shape
+    n_cells = width_x * width_yz
     sections = lax.axis_size("sect")
     own_sect = lax.axis_index("sect")
     plane = sections * width_yz
     all_cells = lax.all_gather(cells, "sect", axis=0, tiled=True)
+    n_all = all_cells.shape[0]
     cell_row = all_cells // plane
     cell_col = all_cells % plane
-    owner_sect = cell_col // width_yz
-    local_cell = cell_row * width_yz + cell_col % width_yz
-    picked = jnp.take(gas_block.reshape(fields, width_x * width_yz), local_cell, axis=1)
-    picked = jnp.where((owner_sect == own_sect)[None], picked, 0.0)
+    owned = (cell_col // width_yz) == own_sect
+    local_cell = (cell_row * width_yz + cell_col % width_yz).astype(jnp.int32)
+    seg = jnp.where(owned, local_cell, n_cells).astype(jnp.int32)
+    position = jnp.arange(n_all, dtype=jnp.int32)
+    order = lax.sort(jnp.where(owned, 0, n_all).astype(jnp.int32) + position) % n_all
+    count = jnp.sum(owned.astype(jnp.int32)).reshape(1)
+    table = gas_block.reshape(fields, n_cells).T
+    picked = jnp.where(owned[None, :], row_gather(count, order, local_cell, table).T, 0.0)
     at_parcel = lax.psum_scatter(picked, "sect", scatter_dimension=1, tiled=True)
     state, terms = parcel_update(
         masses, drop_temp, flags, at_parcel[:NC], at_parcel[NC], volat_a, volat_b, latent
@@ -82,19 +151,9 @@
     down = padded[:, :-2]
     upper = padded[:, 2:]
     flowed = gas_block + 0.2 * (upper - 2.0 * gas_block + down) - 0.3 * (gas_block - down)
-    all_terms, all_cells = (
-        lax.all_gather(terms, "sect", axis=1, tiled=True),
-        lax.all_gather(cells, "sect", axis=0, tiled=True),
-    )
-    cell_row = all_cells // plane
-    cell_col = all_cells % plane
-    owner_sect = cell_col // width_yz
-    local_cell = cell_row * width_yz + cell_col % width_yz
-    segment_ids = jnp.where(owner_sect == own_sect, local_cell, width_x * width_yz).astype(
-        jnp.int32
-    )
-    summed = jax.ops.segment_sum(all_terms.T, segment_ids, width_x * width_yz + 1)
-    source = summed[: width_x * width_yz].T.reshape(fields, width_x, width_yz)
+    all_terms = lax.all_gather(terms, "sect", axis=1, tiled=True)
+    summed = row_scatter_add(count, order, seg, all_terms.T, n_cells)
+    source = summed.T.reshape(fields, width_x, width_yz)
     gas_next = flowed + source
     kept = jnp.where(moves[None] == 0, state, 0.0)
     from_prev = shifted(pack_slots(state, moves == 2), "slab", 1)

time: 314 us -> 436 us (1.39)
  waiting for transfers between devices: 47.5 us -> 253 us
  local copies, waits for them, and re-layouts: 122 us -> 51.8 us
  other arithmetic: 104 us -> 47.1 us
  Pallas kernels: 0 us -> 43.8 us
    all_gather x1, waiting for transfers between devices: 1.49 us -> 106 us  [body(): all_terms = lax.all_gather(terms, 'sect', axis=1, tiled=True)]
    reduce_scatter x1, waiting for transfers between devices: 45.9 us -> 146 us  [body(): lax.psum_scatter(picked, 'sect', scatter_dimension=1, tiled=True)]
    scatter-add x1 -> x0, other arithmetic: 93.1 us -> none  [body(): jax.ops.segment_sum(all_terms.T, segment_ids, width_x * width_yz + 1)]
    gather x2 -> x0, local copies, waits for them, and re-layouts: 63 us -> none  [body(): jnp.take(gas_block.reshape(fields, width_x * width_yz), local_cell, axis=1)]
    pallas_call x0 -> x2, Pallas kernels: none -> 43.8 us  [the longest x1 25.2 us: row_scatter_add(): pl.pallas_call(_scatter_kernel, grid_spec=spec, out_shape=jax.ShapeDtypeS...]
    select_n x2 -> x3, other arithmetic: 2.31 us -> 14.5 us  [the longest x1 13.1 us: body(): jnp.where(owned[None, :], row_gather(count, order, local_cell, table).T,...]
    reduce_sum x4, other arithmetic: 1.72 us -> 10.7 us  [parcel_update(): slope = jnp.sum(frac * excess * excess / (denom * denom), axis=0) + 0.1]
    sort x0 -> x1, other arithmetic: none -> 7.75 us  [body(): lax.sort(jnp.where(owned, 0, n_all).astype(jnp.int32) + position) % n_all]
  transfers between devices with their start and end apart: 6 -> 6, of which waited for: 2 -> 3; matrix products, arithmetic and copies ran while one was open for 45% -> 9% of each run, Pallas kernels for 0% -> 6%
where the time goes in v1:
time: 436 us; the launch traced here: 434 us
  waiting for transfers between devices  253 us (58%)
  local copies, waits for them, and re-layouts  51.8 us (12%)
  other arithmetic  47.1 us (11%)
  Pallas kernels  43.8 us (10%)
  between operations  14.4 us (3%)
  starting transfers between devices  12.9 us (3%)
  blocking collectives  11.1 us (3%)
    reduce_scatter x1, waiting for transfers between devices, body(): lax.psum_scatter(picked, 'sect', scatter_dimension=1, tiled=True)  146 us
    all_gather x1, waiting for transfers between devices, body(): all_terms = lax.all_gather(terms, 'sect', axis=1, tiled=True)  106 us
    pallas_call x1, Pallas kernels, row_scatter_add(): pl.pallas_call(_scatter_kernel, grid_spec=spec, out_shape=jax.ShapeDtypeS...  25.2 us
    scatter x2, local copies, waits for them, and re-layouts, pack_slots(): return buffer.at[slot].set(state.T, mode='drop').T  22.8 us
    pallas_call x1, Pallas kernels, row_gather(): pl.pallas_call(_gather_kernel, grid_spec=spec, out_shape=jax.ShapeDtypeSt...  18.6 us
    select_n x1, other arithmetic, body(): jnp.where(owned[None, :], row_gather(count, order, local_cell, table).T,...  13.1 us
    all_gather x1, blocking collectives, body(): all_cells = lax.all_gather(cells, 'sect', axis=0, tiled=True)  11.1 us
    reduce_sum x4, other arithmetic, parcel_update(): slope = jnp.sum(frac * excess * excess / (denom * denom), axis=0) + 0.1  10.7 us
  transfers between devices with their start and end apart: 6, of which 3 were waited for; matrix products, arithmetic and copies ran while one was open for 9% of the time, Pallas kernels for 6%

profile of v1, /device:TPU:3, one launch (start us, length us, event | category | flops | bytes accessed | tf_op | source)
XLA Modules:
  0.0 434.0 jit_solution(16081118978985707559)
XLA Ops:
  7.2 11.1 %all_gather.6 = s32[16384]{0:T(1024)S(1)} all-gather(s32[4096]{0:T(1024)} %param.14), channel_id=1, replica_groups=mesh['sect'=4,'slab'=8] {'sect'}, dimensions={0}, use_global_device_ids=true | all-gather | bytes 81920 | tf_op jit(solution)/shard_map/all_gather | solution.py:134
  19.8 7.7 %sort.14 = (s32[16384]{0:T(1024)S(1)}, s32[16384]{0:T(1024)}) sort(s32[16384]{0:T(1024)S(1)} %get-tuple-element.53, s32[16384]{0:T(1024)S(1)} %iota.7), dimensions={0}, to_apply=%region_1.2 | sort | flops 229376 | bytes 262144 | tf_op jit(solution)/shard_map/sort | solution.py:142
  31.5 4.7 %copy.71 = f32[31,16384]{0,1:T(8,128)} copy(f32[31,16384]{1,0:T(8,128)S(1)} %pad_maximum_fusion.5) | data formatting | bytes 4063232 | tf_op jit(solution)/shard_map/concatenate | solution.py:128
  36.2 18.6 %shard_map.121 = f32[16384,31]{1,0:T(8,128)} custom-call(s32[1]{0:T(128)} %bitcast.1.count_ref, s32[16384]{0:T(1024)} %add_select_fusion.2.order_ref, s32[16384]{0:T(1024)} %get-tuple-element.40.local_ref, f32[16384,31]{1,0:T(8,128)} %bitcast.34), custom_call_target="tpu_custom_call" | custom-call | tf_op jit(solution)/shard_map/pallas_call | solution.py:104
  54.8 13.1 %select_bitcast_fusion = f32[31,16384]{0,1:T(8,128)} fusion(f32[16384,31]{1,0:T(8,128)} %shard_map.121, pred[16384]{0:T(1024)(128)(4,1)S(1)} %get-tuple-element.41), kind=kLoop, calls=%fused_computation.2 | loop fusion | flops 507904 | bytes 4079616 | tf_op jit(solution)/shard_map/jit(_where)/select_n | solution.py:145
  69.7 146.0 %reduce-scatter.2.cloned.1.call-done = f32[31,4096]{0,1:T(8,128)} async-done(((f32[31,16384]{0,1:T(8,128)}), f32[31,4096]{0,1:T(8,128)}) %reduce-scatter.2.cloned.1.call-update) | async-done | bytes 507920 | tf_op jit(solution)/shard_map/reduce_scatter | solution.py:146
  215.8 2.8 slice_reduce_fusion
  218.6 2.7 fusion.8
  221.3 2.7 fusion.9
  224.0 2.7 fusion.10
  226.7 2.7 fusion.11
  229.4 4.2 fusion.28
  236.3 3.6 pad_maximum_fusion.6
  243.6 11.4 %scatter_custom_fusion = f32[1024,31]{1,0:T(8,128)} fusion(s32[4096]{0:T(1024)S(1)} %get-tuple-element.56, f32[4096,31]{1,0:T(8,128)S(1)} %copy.77, f32[]{:T(128)} %constant.96.clone.1), kind=kCustom, calls=%fused_computation.52 | custom fusion | bytes 126980 | tf_op jit(solution)/shard_map/scatter | solution.py:64
  255.0 4.0 collective-permute-start.2
  259.1 11.4 %scatter_custom_fusion.1 = f32[1024,31]{1,0:T(8,128)} fusion(s32[4096]{0:T(1024)S(1)} %get-tuple-element.55, f32[4096,31]{1,0:T(8,128)S(1)} %copy.77, f32[]{:T(128)} %constant.96.clone.1), kind=kCustom, calls=%fused_computation.50 | custom fusion | bytes 126980 | tf_op jit(solution)/shard_map/scatter | solution.py:64
  272.4 2.7 copy.68
  275.2 2.8 collective-permute-start
  278.0 3.9 collective-permute-start.1
  284.4 106.4 %all-gather.2.cloned.1.call-done = f32[31,16384]{0,1:T(8,128)} async-done(((f32[31,4096]{0,1:T(8,128)}), f32[31,16384]{0,1:T(8,128)}) %all-gather.2.cloned.1.call-update) | async-done | bytes 2031632 | tf_op jit(solution)/shard_map/all_gather | solution.py:154
  390.9 25.2 %shard_map.122 = f32[16384,31]{1,0:T(8,128)} custom-call(s32[1]{0:T(128)} %bitcast.1.count_ref, s32[16384]{0:T(1024)} %add_select_fusion.2.order_ref, s32[16384]{0:T(1024)} %get-tuple-element.39.seg_ref, f32[16384,31]{1,0:T(8,128)} %bitcast.35), custom_call_target="tpu_custom_call" | custom-call | tf_op jit(solution)/shard_map/pallas_call | solution.py:120
  416.1 6.4 %copy.74 = f32[31,16,1024]{2,0,1:T(8,128)} copy(f32[31,16,1024]{0,2,1:T(8,128)} %bitcast.33) | data formatting | bytes 4063232 | tf_op jit(solution)/shard_map/reshape | solution.py:156
  422.4 2.3 fusion.7
  424.7 2.5 copy.81
  (66 shorter events, 18.1 us)
Async XLA Ops:
  7.2 208.6 %reduce-scatter.2.cloned.1.call-start = ((), (), s32[]{:S(2)}) async-start(), calls=%async_computation.1 | async-start | bytes 10485760 | tf_op jit(solution)/shard_map/reduce_scatter | solution.py:146
  30.0 1.2 copy-start.3
  67.9 1.0 copy-start.2
  67.9 322.9 %all-gather.2.cloned.1.call-start = ((), (), s32[]{:S(2)}) async-start(), calls=%async_computation.2 | async-start | bytes 10485760 | tf_op jit(solution)/shard_map/all_gather | solution.py:154
  69.0 149.5 %copy-start.4 = (f32[4096]{0:T(1024)S(1)}, f32[4096]{0:T(1024)}, u32[]{:S(2)}) copy-start(f32[4096]{0:T(1024)} %param.13) | copy-start | bytes 49156
  69.0 149.5 %copy-start.7 = (f32[30]{0:T(128)S(1)}, f32[30]{0:T(128)}, u32[]{:S(2)}) copy-start(f32[30]{0:T(128)} %param.18) | copy-start | bytes 364
  69.0 149.5 %copy-start.8 = (f32[30]{0:T(128)S(1)}, f32[30]{0:T(128)}, u32[]{:S(2)}) copy-start(f32[30]{0:T(128)} %param.17) | copy-start | bytes 364
  224.0 5.4 %copy-start.5 = (s32[4096]{0:T(1024)S(1)}, s32[4096]{0:T(1024)}, u32[]{:S(2)}) copy-start(s32[4096]{0:T(1024)} %param.15) | copy-start | bytes 49156
  224.0 5.4 %copy-start.1 = (f32[31,4096]{0,1:T(8,128)S(1)}, f32[31,4096]{0,1:T(8,128)}, u32[]{:S(2)}) copy-start(f32[31,4096]{0,1:T(8,128)} %reduce-scatter.2.cloned.1.call-done) | copy-start | bytes 1523716
  229.4 4.2 copy-start.9
  236.3 3.6 copy-start.6
  239.9 1.6 copy-start
  255.0 26.9 %collective-permute-start.2 = (f32[31,1024]{0,1:T(8,128)}, f32[31,1024]{0,1:T(8,128)S(1)}, u32[]{:S(2)}, u32[]{:S(2)}) collective-permute-start(f32[31,1024]{0,1:T(8,128)} %bitcast.12), channel_id=1, source_target_pairs={{0,1},{1,2},{2,3},{3,4},{4,5},{5,6},{6,7},{8,9},{9,10},{10,11},{11... | collective-permute-start | bytes 380936 | tf_op jit(solution)/shard_map/ppermute | solution.py:30
  270.5 12.0 %collective-permute-start.3 = (f32[31,1024]{0,1:T(8,128)}, f32[31,1024]{0,1:T(8,128)}, u32[]{:S(2)}, u32[]{:S(2)}) collective-permute-start(f32[31,1024]{0,1:T(8,128)} %bitcast.15), channel_id=1, source_target_pairs={{1,0},{2,1},{3,2},{4,3},{5,4},{6,5},{7,6},{9,8},{10,9},{11,10},{12... | collective-permute-start | bytes 380936 | tf_op jit(solution)/shard_map/ppermute | solution.py:30
  275.2 147.2 %collective-permute-start = (f32[31,1,1024]{2,0,1:T(8,128)S(1)}, f32[31,1,1024]{2,0,1:T(8,128)S(1)}, u32[]{:S(2)}, u32[]{:S(2)}) collective-permute-start(f32[31,1,1024]{2,0,1:T(8,128)S(1)} %get-tuple-element.43), channel_id=1, source_target_pairs={{1,0},{2,1},{3,2},{4,3},{5,4},{6,5},{7,6},{9,8},{10,9},{11,10},{12... | collective-permute-start | bytes 380936 | tf_op jit(solution)/shard_map/ppermute | solution.py:22
  278.0 144.4 %collective-permute-start.1 = (f32[31,1,1024]{2,0,1:T(8,128)S(1)}, f32[31,1,1024]{2,0,1:T(8,128)S(1)}, u32[]{:S(2)}, u32[]{:S(2)}) collective-permute-start(f32[31,1,1024]{2,0,1:T(8,128)S(1)} %get-tuple-element.42), channel_id=1, source_target_pairs={{0,1},{1,2},{2,3},{3,4},{4,5},{5,6},{6,7},{8,9},{9,10},{10,11},{11... | collective-permute-start | bytes 380936 | tf_op jit(solution)/shard_map/ppermute | solution.py:19
Sparse Core Ops, SparseCore 0:
  68.1 147.6 reduce-scatter.1
  240.0 150.7 all-gather.1

commit v2 on v1

--- a/solution.py
+++ b/solution.py
@@ -3,6 +3,7 @@
 from jax import lax
 from jax.experimental import pallas as pl
 from jax.experimental.pallas import tpu as pltpu
+from jax.experimental.layout import Layout, with_layout_constraint
 from jax.sharding import PartitionSpec as P
 
 NC = 30
@@ -143,7 +144,9 @@
     count = jnp.sum(owned.astype(jnp.int32)).reshape(1)
     table = gas_block.reshape(fields, n_cells).T
     picked = jnp.where(owned[None, :], row_gather(count, order, local_cell, table).T, 0.0)
+    picked = with_layout_constraint(picked, Layout(major_to_minor=(0, 1)))
     at_parcel = lax.psum_scatter(picked, "sect", scatter_dimension=1, tiled=True)
+    at_parcel = with_layout_constraint(at_parcel, Layout(major_to_minor=(0, 1)))
     state, terms = parcel_update(
         masses, drop_temp, flags, at_parcel[:NC], at_parcel[NC], volat_a, volat_b, latent
     )
@@ -151,7 +154,9 @@
     down = padded[:, :-2]
     upper = padded[:, 2:]
     flowed = gas_block + 0.2 * (upper - 2.0 * gas_block + down) - 0.3 * (gas_block - down)
+    terms = with_layout_constraint(terms, Layout(major_to_minor=(0, 1)))
     all_terms = lax.all_gather(terms, "sect", axis=1, tiled=True)
+    all_terms = with_layout_constraint(all_terms, Layout(major_to_minor=(0, 1)))
     summed = row_scatter_add(count, order, seg, all_terms.T, n_cells)
     source = summed.T.reshape(fields, width_x, width_yz)
     gas_next = flowed + source

time: 436 us -> 211 us (0.48)
  waiting for transfers between devices: 253 us -> 47.9 us
  other arithmetic: 47.1 us -> 19.4 us
  local copies, waits for them, and re-layouts: 51.8 us -> 58.8 us
    all_gather x1, waiting for transfers between devices: 106 us -> 1.67 us  [body(): all_terms = lax.all_gather(terms, 'sect', axis=1, tiled=True)]
    reduce_scatter x1, waiting for transfers between devices: 146 us -> 46.2 us  [body(): lax.psum_scatter(picked, 'sect', scatter_dimension=1, tiled=True)]
    select_n x1, other arithmetic: 13.1 us -> 1.53 us  [body(): jnp.where(owned[None, :], row_gather(count, order, local_cell, table).T,...]
    reduce_sum x4, other arithmetic: 10.7 us -> 1.72 us  [parcel_update(): slope = jnp.sum(frac * excess * excess / (denom * denom), axis=0) + 0.1]
    another operation x3 -> x4, local copies, waits for them, and re-layouts: 0.3 us -> 6.59 us  [the longest x1 6.3 us: body(): all_terms = with_layout_constraint(all_terms, Layout(major_to_minor=(0, 1)))]
    pallas_call x0 -> x1, local copies, waits for them, and re-layouts: none -> 5.25 us  [row_gather(): pl.pallas_call(_gather_kernel, grid_spec=spec, out_shape=jax.ShapeDtypeSt...]
    unnamed x26 -> x23, local copies, waits for them, and re-layouts: 10.1 us -> 9.83 us
  transfers between devices with their start and end apart: 6 -> 6, of which waited for: 3 -> 2; matrix products, arithmetic and copies ran while one was open for 9% -> 21% of each run, Pallas kernels for 6% -> 12%
where the time goes in v2:
time: 211 us; the launch traced here: 208 us
  local copies, waits for them, and re-layouts  58.8 us (28%)
  waiting for transfers between devices  47.9 us (23%)
  Pallas kernels  43.3 us (21%)
  other arithmetic  19.4 us (9%)
  between operations  14.4 us (7%)
  starting transfers between devices  13.3 us (6%)
  blocking collectives  11.1 us (5%)
    reduce_scatter x1, waiting for transfers between devices, body(): lax.psum_scatter(picked, 'sect', scatter_dimension=1, tiled=True)  46.2 us
    pallas_call x1, Pallas kernels, row_scatter_add(): pl.pallas_call(_scatter_kernel, grid_spec=spec, out_shape=jax.ShapeDtypeS...  25 us
    scatter x2, local copies, waits for them, and re-layouts, pack_slots(): return buffer.at[slot].set(state.T, mode='drop').T  22.8 us
    pallas_call x1, Pallas kernels, row_gather(): pl.pallas_call(_gather_kernel, grid_spec=spec, out_shape=jax.ShapeDtypeSt...  18.3 us
    all_gather x1, blocking collectives, body(): all_cells = lax.all_gather(cells, 'sect', axis=0, tiled=True)  11.1 us
    unnamed x23, local copies, waits for them, and re-layouts  9.83 us
    sort x1, other arithmetic, body(): lax.sort(jnp.where(owned, 0, n_all).astype(jnp.int32) + position) % n_all  7.75 us
    ppermute x2, starting transfers between devices, shifted(): return lax.ppermute(shard, axis, pairs)  6.57 us
  transfers between devices with their start and end apart: 6, of which 2 were waited for; matrix products, arithmetic and copies ran while one was open for 21% of the time, Pallas kernels for 12%

profile of v2, /device:TPU:3, one launch (start us, length us, event | category | flops | bytes accessed | tf_op | source)
XLA Modules:
  0.0 208.1 jit_solution(13434814191002672165)
XLA Ops:
  7.2 11.1 %all_gather.6 = s32[16384]{0:T(1024)S(1)} all-gather(s32[4096]{0:T(1024)} %param.14), channel_id=1, replica_groups=mesh['sect'=4,'slab'=8] {'sect'}, dimensions={0}, use_global_device_ids=true | all-gather | bytes 81920 | tf_op jit(solution)/shard_map/all_gather | solution.py:135
  19.8 7.7 %sort.14 = (s32[16384]{0:T(1024)S(1)}, s32[16384]{0:T(1024)}) sort(s32[16384]{0:T(1024)S(1)} %get-tuple-element.46, s32[16384]{0:T(1024)S(1)} %iota.7), dimensions={0}, to_apply=%region_1.2 | sort | flops 229376 | bytes 262144 | tf_op jit(solution)/shard_map/sort | solution.py:143
  29.1 1.7 pad.22
  30.9 1.2 copy.49
  32.3 4.7 %copy.40 = f32[31,16384]{0,1:T(8,128)} copy(f32[31,16384]{1,0:T(8,128)S(1)} %pad_maximum_fusion.5) | data formatting | bytes 4063232 | tf_op jit(solution)/shard_map/concatenate | solution.py:129
  37.0 18.3 %shard_map.121 = f32[16384,31]{1,0:T(8,128)} custom-call(s32[1]{0:T(128)} %bitcast.1.count_ref, s32[16384]{0:T(1024)} %add_select_fusion.2.order_ref, s32[16384]{0:T(1024)} %get-tuple-element.33.local_ref, f32[16384,31]{1,0:T(8,128)} %bitcast.36), custom_call_target="tpu_custom_call" | custom-call | tf_op jit(solution)/shard_map/pallas_call | solution.py:105
  55.4 5.2 %copy.41 = f32[16384,31]{0,1:T(8,128)S(1)} copy(f32[16384,31]{1,0:T(8,128)} %shard_map.121) | data formatting | bytes 4063232 | tf_op jit(solution)/shard_map/pallas_call | solution.py:105
  60.6 1.5 select_bitcast_fusion
  63.3 46.2 %reduce-scatter.2.cloned.1.call-done = f32[31,4096]{1,0:T(8,128)} async-done(((f32[31,16384]{1,0:T(8,128)}), f32[31,4096]{1,0:T(8,128)}) %reduce-scatter.2.cloned.1.call-update) | async-done | bytes 507920 | tf_op jit(solution)/shard_map/reduce_scatter | solution.py:148
  109.4 1.0 slice.48
  116.4 11.4 %scatter_custom_fusion.1 = f32[1024,31]{1,0:T(8,128)} fusion(s32[4096]{0:T(1024)S(1)} %get-tuple-element.48, f32[4096,31]{1,0:T(8,128)S(1)} %copy.44, f32[]{:T(128)} %constant.96.clone.1), kind=kCustom, calls=%fused_computation.47 | custom fusion | bytes 126980 | tf_op jit(solution)/shard_map/scatter | solution.py:65
  127.8 2.9 %collective-permute-start.3 = (f32[31,1024]{0,1:T(8,128)}, f32[31,1024]{0,1:T(8,128)S(1)}, u32[]{:S(2)}, u32[]{:S(2)}) collective-permute-start(f32[31,1024]{0,1:T(8,128)} %bitcast.16), channel_id=1, source_target_pairs={{1,0},{2,1},{3,2},{4,3},{5,4},{6,5},{7,6},{9,8},{10,9},{11,10},{12... | collective-permute-start | bytes 380936 | tf_op jit(solution)/shard_map/ppermute | solution.py:31
  130.7 11.4 %scatter_custom_fusion = f32[1024,31]{1,0:T(8,128)} fusion(s32[4096]{0:T(1024)S(1)} %get-tuple-element.49, f32[4096,31]{1,0:T(8,128)S(1)} %copy.44, f32[]{:T(128)} %constant.96.clone.1), kind=kCustom, calls=%fused_computation.49 | custom fusion | bytes 126980 | tf_op jit(solution)/shard_map/scatter | solution.py:65
  142.1 3.6 %collective-permute-start.2 = (f32[31,1024]{0,1:T(8,128)}, f32[31,1024]{0,1:T(8,128)}, u32[]{:S(2)}, u32[]{:S(2)}) collective-permute-start(f32[31,1024]{0,1:T(8,128)} %bitcast.13), channel_id=1, source_target_pairs={{0,1},{1,2},{2,3},{3,4},{4,5},{5,6},{6,7},{8,9},{9,10},{10,11},{11... | collective-permute-start | bytes 380936 | tf_op jit(solution)/shard_map/ppermute | solution.py:31
  145.8 2.7 %copy.38 = f32[30,16,1024]{2,0,1:T(8,128)S(1)} copy(f32[30,16,1024]{2,1,0:T(8,128)} %param.10) | data formatting | bytes 3932160 | tf_op args[0]
  148.6 1.9 collective-permute-start
  150.5 4.5 %collective-permute-start.1 = (f32[31,1,1024]{2,0,1:T(8,128)S(1)}, f32[31,1,1024]{2,0,1:T(8,128)S(1)}, u32[]{:S(2)}, u32[]{:S(2)}) collective-permute-start(f32[31,1,1024]{2,0,1:T(8,128)S(1)} %get-tuple-element.35), channel_id=1, source_target_pairs={{0,1},{1,2},{2,3},{3,4},{4,5},{5,6},{6,7},{8,9},{9,10},{10,11},{11... | collective-permute-start | bytes 380936 | tf_op jit(solution)/shard_map/ppermute | solution.py:20
  155.3 1.2 copy.46
  157.3 1.7 all-gather.2.cloned.1.call-done
  158.9 6.3 %copy.42 = f32[31,16384]{0,1:T(8,128)} copy(f32[31,16384]{1,0:T(8,128)} %all-gather.2.cloned.1.call-done) | data formatting | bytes 4063232 | tf_op jit(solution)/shard_map/layout_constraint | solution.py:159
  165.2 25.0 %shard_map.122 = f32[16384,31]{1,0:T(8,128)} custom-call(s32[1]{0:T(128)} %bitcast.1.count_ref, s32[16384]{0:T(1024)} %add_select_fusion.2.order_ref, s32[16384]{0:T(1024)} %get-tuple-element.32.seg_ref, f32[16384,31]{1,0:T(8,128)} %bitcast.34), custom_call_target="tpu_custom_call" | custom-call | tf_op jit(solution)/shard_map/pallas_call | solution.py:121
  190.2 6.4 %copy.43 = f32[31,16,1024]{2,0,1:T(8,128)} copy(f32[31,16,1024]{0,2,1:T(8,128)} %bitcast.35) | data formatting | bytes 4063232 | tf_op jit(solution)/shard_map/reshape | solution.py:161
  196.5 2.3 %fusion.5 = f32[31,16,1024]{2,0,1:T(8,128)S(1)} fusion(f32[31,16,1024]{2,0,1:T(8,128)} %copy.43, f32[31,1,1024]{2,0,1:T(8,128)S(1)} %collective-permute-done, f32[1,16,1024]{2,0,1:T(1,128)S(1)} %copy.39, f32[30,16,1024]{2,0,1:T(8,128)S(1)} %copy.38, f32[31,1,1024]{2,0,1:T(8,128)S(1)} %collective-permute-done.1), kind=kLoop, calls=%fused_computation.13 | loop fusion | flops 7110656 | bytes 6348800 | tf_op jit(solution)/shard_map/add | solution.py:162
  198.8 2.5 %copy.48 = f32[31,16,1024]{2,1,0:T(8,128)} copy(f32[31,16,1024]{2,0,1:T(8,128)S(1)} %fusion.5) | data formatting | bytes 4063232
  (63 shorter events, 11.2 us)
Async XLA Ops:
  7.2 102.2 %reduce-scatter.2.cloned.1.call-start = ((), (), s32[]{:S(2)}) async-start(), calls=%async_computation.1 | async-start | bytes 2621440 | tf_op jit(solution)/shard_map/reduce_scatter | solution.py:148
  62.1 1.0 copy-start
  62.1 48.3 %copy-start.3 = (f32[4096]{0:T(1024)S(1)}, f32[4096]{0:T(1024)}, u32[]{:S(2)}) copy-start(f32[4096]{0:T(1024)} %param.13) | copy-start | bytes 49156
  62.1 48.3 %copy-start.6 = (f32[30]{0:T(128)S(1)}, f32[30]{0:T(128)}, u32[]{:S(2)}) copy-start(f32[30]{0:T(128)} %param.18) | copy-start | bytes 364
  62.1 48.3 %copy-start.7 = (f32[30]{0:T(128)S(1)}, f32[30]{0:T(128)}, u32[]{:S(2)}) copy-start(f32[30]{0:T(128)} %param.17) | copy-start | bytes 364
  62.2 50.1 %copy-start.4 = (s32[4096]{0:T(1024)S(1)}, s32[4096]{0:T(1024)}, u32[]{:S(2)}) copy-start(s32[4096]{0:T(1024)} %param.15) | copy-start | bytes 49156
  62.2 96.7 %all-gather.2.cloned.1.call-start = ((), (), s32[]{:S(2)}) async-start(), calls=%async_computation.2 | async-start | bytes 2621440 | tf_op jit(solution)/shard_map/all_gather | solution.py:158
  109.4 2.9 %copy-start.1 = (f32[31,4096]{1,0:T(8,128)S(1)}, f32[31,4096]{1,0:T(8,128)}, u32[]{:S(2)}) copy-start(f32[31,4096]{1,0:T(8,128)} %reduce-scatter.2.cloned.1.call-done) | copy-start | bytes 1523716
  110.9 1.7 copy-start.8
  112.3 1.4 copy-start.5
  127.8 27.3 %collective-permute-start.3 = (f32[31,1024]{0,1:T(8,128)}, f32[31,1024]{0,1:T(8,128)S(1)}, u32[]{:S(2)}, u32[]{:S(2)}) collective-permute-start(f32[31,1024]{0,1:T(8,128)} %bitcast.16), channel_id=1, source_target_pairs={{1,0},{2,1},{3,2},{4,3},{5,4},{6,5},{7,6},{9,8},{10,9},{11,10},{12... | collective-permute-start | bytes 380936 | tf_op jit(solution)/shard_map/ppermute | solution.py:31
  142.1 6.3 %copy-start.2 = (f32[16,1024]{1,0:T(8,128)S(1)}, f32[16,1024]{1,0:T(8,128)}, u32[]{:S(2)}) copy-start(f32[16,1024]{1,0:T(8,128)} %param.11) | copy-start | bytes 196612
  142.1 13.1 %collective-permute-start.2 = (f32[31,1024]{0,1:T(8,128)}, f32[31,1024]{0,1:T(8,128)}, u32[]{:S(2)}, u32[]{:S(2)}) collective-permute-start(f32[31,1024]{0,1:T(8,128)} %bitcast.13), channel_id=1, source_target_pairs={{0,1},{1,2},{2,3},{3,4},{4,5},{5,6},{6,7},{8,9},{9,10},{10,11},{11... | collective-permute-start | bytes 380936 | tf_op jit(solution)/shard_map/ppermute | solution.py:31
  148.6 47.9 %collective-permute-start = (f32[31,1,1024]{2,0,1:T(8,128)S(1)}, f32[31,1,1024]{2,0,1:T(8,128)S(1)}, u32[]{:S(2)}, u32[]{:S(2)}) collective-permute-start(f32[31,1,1024]{2,0,1:T(8,128)S(1)} %get-tuple-element.36), channel_id=1, source_target_pairs={{1,0},{2,1},{3,2},{4,3},{5,4},{6,5},{7,6},{9,8},{10,9},{11,10},{12... | collective-permute-start | bytes 380936 | tf_op jit(solution)/shard_map/ppermute | solution.py:23
  150.5 46.0 %collective-permute-start.1 = (f32[31,1,1024]{2,0,1:T(8,128)S(1)}, f32[31,1,1024]{2,0,1:T(8,128)S(1)}, u32[]{:S(2)}, u32[]{:S(2)}) collective-permute-start(f32[31,1,1024]{2,0,1:T(8,128)S(1)} %get-tuple-element.35), channel_id=1, source_target_pairs={{0,1},{1,2},{2,3},{3,4},{4,5},{5,6},{6,7},{8,9},{9,10},{10,11},{11... | collective-permute-start | bytes 380936 | tf_op jit(solution)/shard_map/ppermute | solution.py:20
Sparse Core Ops, SparseCore 0:
  62.3 47.0 reduce-scatter.1
  113.8 45.0 all-gather.1

commit v3 on v2

--- a/solution.py
+++ b/solution.py
@@ -59,10 +59,16 @@
 
 
 def pack_slots(state, chosen):
-    slot = jnp.cumsum(chosen.astype(jnp.int32)) - 1
-    slot = jnp.where(chosen, slot, MOVE_CAP)
-    buffer = jnp.zeros((MOVE_CAP, state.shape[0]), jnp.float32)
-    return buffer.at[slot].set(state.T, mode="drop").T
+    slot = jnp.where(chosen, jnp.cumsum(chosen.astype(jnp.int32)) - 1, -1)
+    onehot = (slot[:, None] == jnp.arange(MOVE_CAP, dtype=jnp.int32)[None, :]).astype(jnp.bfloat16)
+    high = lax.reduce_precision(state, exponent_bits=8, mantissa_bits=7)
+    rest = state - high
+    middle = lax.reduce_precision(rest, exponent_bits=8, mantissa_bits=7)
+    low = rest - middle
+    parts = jnp.concatenate([high, middle, low], axis=0).astype(jnp.bfloat16)
+    out = jnp.dot(parts, onehot, preferred_element_type=jnp.float32)
+    rows = state.shape[0]
+    return (out[:rows] + out[rows : 2 * rows]) + out[2 * rows :]
 
 
 def _gather_kernel(count_ref, order_ref, local_ref, table_ref, out_ref):
@@ -132,7 +138,8 @@
     sections = lax.axis_size("sect")
     own_sect = lax.axis_index("sect")
     plane = sections * width_yz
-    all_cells = lax.all_gather(cells, "sect", axis=0, tiled=True)
+    all_cells = lax.all_gather(cells.astype(jnp.float32), "sect", axis=0, tiled=True)
+    all_cells = all_cells.astype(jnp.int32)
     n_all = all_cells.shape[0]
     cell_row = all_cells // plane
     cell_col = all_cells % plane

time: 211 us -> 211 us (level)
  local copies, waits for them, and re-layouts: 58.8 us -> 32.4 us
  waiting for transfers between devices: 47.9 us -> 66.4 us
  matrix products: 0 us -> 7.19 us
    scatter x2 -> x0, local copies, waits for them, and re-layouts: 22.8 us -> none  [pack_slots(): return buffer.at[slot].set(state.T, mode='drop').T]
    all_gather x1, waiting for transfers between devices: 1.67 us -> 20.5 us  [body(): all_terms = lax.all_gather(terms, 'sect', axis=1, tiled=True)]
    dot_general x0 -> x2, matrix products: none -> 7.19 us  [pack_slots(): out = jnp.dot(parts, onehot, preferred_element_type=jnp.float32)]
    unnamed x23 -> x25, local copies, waits for them, and re-layouts: 9.83 us -> 8.29 us
  transfers between devices with their start and end apart: 6 -> 6, of which waited for: 2 -> 2; matrix products, arithmetic and copies ran while one was open for 21% -> 12% of each run, Pallas kernels for 12% -> 12%
where the time goes in v3:
time: 211 us; the launch traced here: 208 us
  waiting for transfers between devices  66.4 us (31%)
  Pallas kernels  43.3 us (21%)
  local copies, waits for them, and re-layouts  32.4 us (15%)
  other arithmetic  20.3 us (10%)
  between operations  14.4 us (7%)
  starting transfers between devices  13.5 us (6%)
  blocking collectives  10.9 us (5%)
  matrix products  7.19 us (3%)
    reduce_scatter x1, waiting for transfers between devices, body(): lax.psum_scatter(picked, 'sect', scatter_dimension=1, tiled=True)  45.9 us
    pallas_call x1, Pallas kernels, row_scatter_add(): pl.pallas_call(_scatter_kernel, grid_spec=spec, out_shape=jax.ShapeDtypeS...  24.9 us
    all_gather x1, waiting for transfers between devices, body(): all_terms = lax.all_gather(terms, 'sect', axis=1, tiled=True)  20.5 us
    pallas_call x1, Pallas kernels, row_gather(): pl.pallas_call(_gather_kernel, grid_spec=spec, out_shape=jax.ShapeDtypeSt...  18.4 us
    all_gather x1, blocking collectives, body(): lax.all_gather(cells.astype(jnp.float32), 'sect', axis=0, tiled=True)  10.9 us
    unnamed x25, local copies, waits for them, and re-layouts  8.29 us
    sort x1, other arithmetic, body(): lax.sort(jnp.where(owned, 0, n_all).astype(jnp.int32) + position) % n_all  7.75 us
    dot_general x2, matrix products, pack_slots(): out = jnp.dot(parts, onehot, preferred_element_type=jnp.float32)  7.19 us
  transfers between devices with their start and end apart: 6, of which 2 were waited for; matrix products, arithmetic and copies ran while one was open for 12% of the time, Pallas kernels for 12%

profile of v3, /device:TPU:3, one launch (start us, length us, event | category | flops | bytes accessed | tf_op | source)
XLA Modules:
  0.0 208.4 jit_solution(17354392963506430955)
XLA Ops:
  7.9 10.9 %all_gather.6 = f32[16384]{0:T(1024)S(1)} all-gather(f32[4096]{0:T(1024)S(1)} %convert_element_type.8), channel_id=1, replica_groups=mesh['sect'=4,'slab'=8] {'sect'}, dimensions={0}, use_global_device_ids=true | all-gather | bytes 81920 | tf_op jit(solution)/shard_map/all_gather | solution.py:141
  20.3 7.7 %sort.14 = (s32[16384]{0:T(1024)S(1)}, s32[16384]{0:T(1024)}) sort(s32[16384]{0:T(1024)S(1)} %get-tuple-element.42, s32[16384]{0:T(1024)S(1)} %iota.12), dimensions={0}, to_apply=%region_1.2 | sort | flops 229376 | bytes 262144 | tf_op jit(solution)/shard_map/sort | solution.py:150
  29.6 1.7 pad.25
  31.4 1.2 copy.35
  32.8 4.7 %copy.30 = f32[31,16384]{0,1:T(8,128)} copy(f32[31,16384]{1,0:T(8,128)S(1)} %pad_maximum_fusion.5) | data formatting | bytes 4063232 | tf_op jit(solution)/shard_map/concatenate | solution.py:135
  37.5 18.4 %shard_map.121 = f32[16384,31]{1,0:T(8,128)} custom-call(s32[1]{0:T(128)} %bitcast.1.count_ref, s32[16384]{0:T(1024)} %add_select_fusion.2.order_ref, s32[16384]{0:T(1024)} %get-tuple-element.27.local_ref, f32[16384,31]{1,0:T(8,128)} %bitcast.28), custom_call_target="tpu_custom_call" | custom-call | tf_op jit(solution)/shard_map/pallas_call | solution.py:111
  55.9 5.2 %copy.31 = f32[16384,31]{0,1:T(8,128)S(1)} copy(f32[16384,31]{1,0:T(8,128)} %shard_map.121) | data formatting | bytes 4063232 | tf_op jit(solution)/shard_map/pallas_call | solution.py:111
  61.2 1.5 select_bitcast_fusion
  63.8 45.9 %reduce-scatter.2.cloned.1.call-done = f32[31,4096]{1,0:T(8,128)} async-done(((f32[31,16384]{1,0:T(8,128)}), f32[31,4096]{1,0:T(8,128)}) %reduce-scatter.2.cloned.1.call-update) | async-done | bytes 507920 | tf_op jit(solution)/shard_map/reduce_scatter | solution.py:155
  109.7 1.0 slice.72
  115.2 1.0 reduce-precision_convert_fusion.1
  116.2 3.6 %fusion.1 = f32[93,1024]{1,0:T(8,128)S(1)} fusion(s32[4096]{0:T(1024)S(1)} %get-tuple-element.44, bf16[31,4096]{1,0:T(8,128)(2,1)S(1)} %get-tuple-element.33, bf16[31,4096]{1,0:T(8,128)(2,1)S(1)} %get-tuple-element.32, bf16[31,4096]{1,0:T(8,128)(2,1)S(1)} %get-tuple-element.31), kind=kOutput, calls=%fused_computation.3 | convolution fusion | flops 786620416 | bytes 1159168 | tf_op jit(solution)/shard_map/dot_general | solution.py:69
  119.8 3.0 %collective-permute-start.3 = (f32[31,1024]{1,0:T(8,128)S(1)}, f32[31,1024]{1,0:T(8,128)S(1)}, u32[]{:S(2)}, u32[]{:S(2)}) collective-permute-start(f32[31,1024]{1,0:T(8,128)S(1)} %slice_add_fusion), channel_id=1, source_target_pairs={{1,0},{2,1},{3,2},{4,3},{5,4},{6,5},{7,6},{9,8},{10,9},{11,10},{12... | collective-permute-start | bytes 380936 | tf_op jit(solution)/shard_map/ppermute | solution.py:31
  122.8 3.6 %fusion = f32[93,1024]{1,0:T(8,128)S(1)} fusion(s32[4096]{0:T(1024)S(1)} %get-tuple-element.45, bf16[31,4096]{1,0:T(8,128)(2,1)S(1)} %get-tuple-element.33, bf16[31,4096]{1,0:T(8,128)(2,1)S(1)} %get-tuple-element.32, bf16[31,4096]{1,0:T(8,128)(2,1)S(1)} %get-tuple-element.31), kind=kOutput, calls=%fused_computation.2 | convolution fusion | flops 786620416 | bytes 1159168 | tf_op jit(solution)/shard_map/dot_general | solution.py:69
  126.4 3.6 %collective-permute-start.2 = (f32[31,1024]{1,0:T(8,128)S(1)}, f32[31,1024]{1,0:T(8,128)S(1)}, u32[]{:S(2)}, u32[]{:S(2)}) collective-permute-start(f32[31,1024]{1,0:T(8,128)S(1)} %slice_add_fusion.2), channel_id=1, source_target_pairs={{0,1},{1,2},{2,3},{3,4},{4,5},{5,6},{6,7},{8,9},{9,10},{10,11},{11... | collective-permute-start | bytes 380936 | tf_op jit(solution)/shard_map/ppermute | solution.py:31
  130.1 1.1 copy.28
  131.3 1.9 collective-permute-start
  133.3 4.8 %collective-permute-start.1 = (f32[31,1,1024]{2,0,1:T(8,128)S(1)}, f32[31,1,1024]{2,0,1:T(8,128)S(1)}, u32[]{:S(2)}, u32[]{:S(2)}) collective-permute-start(f32[31,1,1024]{2,0,1:T(8,128)S(1)} %get-tuple-element.29), channel_id=1, source_target_pairs={{0,1},{1,2},{2,3},{3,4},{4,5},{5,6},{6,7},{8,9},{9,10},{10,11},{11... | collective-permute-start | bytes 380936 | tf_op jit(solution)/shard_map/ppermute | solution.py:20
  138.8 20.5 %all-gather.2.cloned.1.call-done = f32[31,16384]{1,0:T(8,128)} async-done(((f32[31,4096]{1,0:T(8,128)}), f32[31,16384]{1,0:T(8,128)}) %all-gather.2.cloned.1.call-update) | async-done | bytes 2031632 | tf_op jit(solution)/shard_map/all_gather | solution.py:165
  159.3 6.3 %copy.32 = f32[31,16384]{0,1:T(8,128)} copy(f32[31,16384]{1,0:T(8,128)} %all-gather.2.cloned.1.call-done) | data formatting | bytes 4063232 | tf_op jit(solution)/shard_map/layout_constraint | solution.py:166
  165.6 24.9 %shard_map.122 = f32[16384,31]{1,0:T(8,128)} custom-call(s32[1]{0:T(128)} %bitcast.1.count_ref, s32[16384]{0:T(1024)} %add_select_fusion.2.order_ref, s32[16384]{0:T(1024)} %get-tuple-element.26.seg_ref, f32[16384,31]{1,0:T(8,128)} %bitcast.26), custom_call_target="tpu_custom_call" | custom-call | tf_op jit(solution)/shard_map/pallas_call | solution.py:127
  190.5 6.4 %copy.33 = f32[31,16,1024]{2,0,1:T(8,128)} copy(f32[31,16,1024]{0,2,1:T(8,128)} %bitcast.27) | data formatting | bytes 4063232 | tf_op jit(solution)/shard_map/reshape | solution.py:168
  196.8 2.3 %fusion.9 = f32[31,16,1024]{2,0,1:T(8,128)S(1)} fusion(f32[31,16,1024]{2,0,1:T(8,128)} %copy.33, f32[31,1,1024]{2,0,1:T(8,128)S(1)} %collective-permute-done, f32[1,16,1024]{2,0,1:T(1,128)S(1)} %copy.29, f32[30,16,1024]{2,0,1:T(8,128)S(1)} %copy.28, f32[31,1,1024]{2,0,1:T(8,128)S(1)} %collective-permute-done.1), kind=kLoop, calls=%fused_computation.17 | loop fusion | flops 7110656 | bytes 6348800 | tf_op jit(solution)/shard_map/add | solution.py:169
  199.1 2.5 %copy.34 = f32[31,16,1024]{2,1,0:T(8,128)} copy(f32[31,16,1024]{2,0,1:T(8,128)S(1)} %fusion.9) | data formatting | bytes 4063232
  (65 shorter events, 10.2 us)
Async XLA Ops:
  7.2 102.6 %reduce-scatter.2.cloned.1.call-start = ((), (), s32[]{:S(2)}) async-start(), calls=%async_computation.1 | async-start | bytes 2621440 | tf_op jit(solution)/shard_map/reduce_scatter | solution.py:155
  62.7 1.0 copy-start
  62.7 48.0 %copy-start.4 = (f32[4096]{0:T(1024)S(1)}, f32[4096]{0:T(1024)}, u32[]{:S(2)}) copy-start(f32[4096]{0:T(1024)} %param.13) | copy-start | bytes 49156
  62.7 48.0 %copy-start.7 = (f32[30]{0:T(128)S(1)}, f32[30]{0:T(128)}, u32[]{:S(2)}) copy-start(f32[30]{0:T(128)} %param.18) | copy-start | bytes 364
  62.7 48.0 %copy-start.8 = (f32[30]{0:T(128)S(1)}, f32[30]{0:T(128)}, u32[]{:S(2)}) copy-start(f32[30]{0:T(128)} %param.17) | copy-start | bytes 364
  62.8 49.8 %copy-start.5 = (s32[4096]{0:T(1024)S(1)}, s32[4096]{0:T(1024)}, u32[]{:S(2)}) copy-start(s32[4096]{0:T(1024)} %param.15) | copy-start | bytes 49156
  62.8 96.5 %all-gather.2.cloned.1.call-start = ((), (), s32[]{:S(2)}) async-start(), calls=%async_computation.2 | async-start | bytes 2621440 | tf_op jit(solution)/shard_map/all_gather | solution.py:165
  109.7 2.9 %copy-start.2 = (f32[31,4096]{1,0:T(8,128)S(1)}, f32[31,4096]{1,0:T(8,128)}, u32[]{:S(2)}) copy-start(f32[31,4096]{1,0:T(8,128)} %reduce-scatter.2.cloned.1.call-done) | copy-start | bytes 1523716
  111.2 1.7 copy-start.9
  112.6 1.4 copy-start.6
  119.8 18.3 %collective-permute-start.3 = (f32[31,1024]{1,0:T(8,128)S(1)}, f32[31,1024]{1,0:T(8,128)S(1)}, u32[]{:S(2)}, u32[]{:S(2)}) collective-permute-start(f32[31,1024]{1,0:T(8,128)S(1)} %slice_add_fusion), channel_id=1, source_target_pairs={{1,0},{2,1},{3,2},{4,3},{5,4},{6,5},{7,6},{9,8},{10,9},{11,10},{12... | collective-permute-start | bytes 380936 | tf_op jit(solution)/shard_map/ppermute | solution.py:31
  122.8 7.3 %copy-start.1 = (f32[30,16,1024]{2,1,0:T(8,128)S(1)}, f32[30,16,1024]{2,1,0:T(8,128)}, u32[]{:S(2)}) copy-start(f32[30,16,1024]{2,1,0:T(8,128)} %param.10) | copy-start | bytes 5898244
  126.4 4.8 %copy-start.3 = (f32[16,1024]{1,0:T(8,128)S(1)}, f32[16,1024]{1,0:T(8,128)}, u32[]{:S(2)}) copy-start(f32[16,1024]{1,0:T(8,128)} %param.11) | copy-start | bytes 196612
  126.4 11.6 %collective-permute-start.2 = (f32[31,1024]{1,0:T(8,128)S(1)}, f32[31,1024]{1,0:T(8,128)S(1)}, u32[]{:S(2)}, u32[]{:S(2)}) collective-permute-start(f32[31,1024]{1,0:T(8,128)S(1)} %slice_add_fusion.2), channel_id=1, source_target_pairs={{0,1},{1,2},{2,3},{3,4},{4,5},{5,6},{6,7},{8,9},{9,10},{10,11},{11... | collective-permute-start | bytes 380936 | tf_op jit(solution)/shard_map/ppermute | solution.py:31
  131.3 65.5 %collective-permute-start = (f32[31,1,1024]{2,0,1:T(8,128)S(1)}, f32[31,1,1024]{2,0,1:T(8,128)S(1)}, u32[]{:S(2)}, u32[]{:S(2)}) collective-permute-start(f32[31,1,1024]{2,0,1:T(8,128)S(1)} %get-tuple-element.30), channel_id=1, source_target_pairs={{1,0},{2,1},{3,2},{4,3},{5,4},{6,5},{7,6},{9,8},{10,9},{11,10},{12... | collective-permute-start | bytes 380936 | tf_op jit(solution)/shard_map/ppermute | solution.py:23
  133.3 63.5 %collective-permute-start.1 = (f32[31,1,1024]{2,0,1:T(8,128)S(1)}, f32[31,1,1024]{2,0,1:T(8,128)S(1)}, u32[]{:S(2)}, u32[]{:S(2)}) collective-permute-start(f32[31,1,1024]{2,0,1:T(8,128)S(1)} %get-tuple-element.29), channel_id=1, source_target_pairs={{0,1},{1,2},{2,3},{3,4},{4,5},{5,6},{6,7},{8,9},{9,10},{10,11},{11... | collective-permute-start | bytes 380936 | tf_op jit(solution)/shard_map/ppermute | solution.py:20
Sparse Core Ops, SparseCore 0:
  62.9 46.8 reduce-scatter.1
  114.1 45.0 all-gather.1

commit v4 on v3

--- a/solution.py
+++ b/solution.py
@@ -131,6 +131,10 @@
     )(count, order, seg, rows)
 
 
+def field_major(x):
+    return with_layout_constraint(x, Layout(major_to_minor=(0, 1)))
+
+
 def body(vapor, gas_temp, masses, drop_temp, cells, flags, moves, volat_a, volat_b, latent):
     gas_block = jnp.concatenate([vapor, gas_temp[None]], axis=0)
     fields, width_x, width_yz = gas_block.shape
@@ -138,6 +142,10 @@
     sections = lax.axis_size("sect")
     own_sect = lax.axis_index("sect")
     plane = sections * width_yz
+    parcel_in = jnp.concatenate(
+        [masses, drop_temp[None], flags.astype(jnp.float32)[None]], axis=0
+    )
+    all_in = field_major(lax.all_gather(field_major(parcel_in), "sect", axis=1, tiled=True))
     all_cells = lax.all_gather(cells.astype(jnp.float32), "sect", axis=0, tiled=True)
     all_cells = all_cells.astype(jnp.int32)
     n_all = all_cells.shape[0]
@@ -150,21 +158,18 @@
     order = lax.sort(jnp.where(owned, 0, n_all).astype(jnp.int32) + position) % n_all
     count = jnp.sum(owned.astype(jnp.int32)).reshape(1)
     table = gas_block.reshape(fields, n_cells).T
-    picked = jnp.where(owned[None, :], row_gather(count, order, local_cell, table).T, 0.0)
-    picked = with_layout_constraint(picked, Layout(major_to_minor=(0, 1)))
-    at_parcel = lax.psum_scatter(picked, "sect", scatter_dimension=1, tiled=True)
-    at_parcel = with_layout_constraint(at_parcel, Layout(major_to_minor=(0, 1)))
-    state, terms = parcel_update(
-        masses, drop_temp, flags, at_parcel[:NC], at_parcel[NC], volat_a, volat_b, latent
+    at_parcel = jnp.where(owned[None, :], row_gather(count, order, local_cell, table).T, 0.0)
+    state_all, terms_all = parcel_update(
+        all_in[:NC], all_in[NC], all_in[NC + 1], at_parcel[:NC], at_parcel[NC],
+        volat_a, volat_b, latent,
     )
+    state_own = field_major(jnp.where(owned[None, :], state_all, 0.0))
+    state = field_major(lax.psum_scatter(state_own, "sect", scatter_dimension=1, tiled=True))
     padded = with_halo(gas_block, (("slab", 1),), 1)
     down = padded[:, :-2]
     upper = padded[:, 2:]
     flowed = gas_block + 0.2 * (upper - 2.0 * gas_block + down) - 0.3 * (gas_block - down)
-    terms = with_layout_constraint(terms, Layout(major_to_minor=(0, 1)))
-    all_terms = lax.all_gather(terms, "sect", axis=1, tiled=True)
-    all_terms = with_layout_constraint(all_terms, Layout(major_to_minor=(0, 1)))
-    summed = row_scatter_add(count, order, seg, all_terms.T, n_cells)
+    summed = row_scatter_add(count, order, seg, terms_all.T, n_cells)
     source = summed.T.reshape(fields, width_x, width_yz)
     gas_next = flowed + source
     kept = jnp.where(moves[None] == 0, state, 0.0)

time: 211 us -> 160 us (0.76)
  waiting for transfers between devices: 66.4 us -> 2.1 us
  other arithmetic: 20.3 us -> 35.8 us
    reduce_scatter x1, waiting for transfers between devices: 45.9 us -> 0.01 us  [body(): lax.psum_scatter(state_own, 'sect', scatter_dimension=1, tiled=True)]
    all_gather x1, waiting for transfers between devices: 20.5 us -> 0.02 us  [body(): lax.all_gather(field_major(parcel_in), 'sect', axis=1, tiled=True)]
    transpose x0 -> x1, local copies, waits for them, and re-layouts: none -> 6.34 us  [body(): summed = row_scatter_add(count, order, seg, terms_all.T, n_cells)]
    another operation x5 -> x4, local copies, waits for them, and re-layouts: 6.6 us -> 0.3 us  [the longest x1 6.3 us: body(): all_terms = with_layout_constraint(all_terms, Layout(major_to_minor=(0, 1)))]
    reduce_sum x4, other arithmetic: 1.72 us -> 6.15 us  [parcel_update(): slope = jnp.sum(frac * excess * excess / (denom * denom), axis=0) + 0.1]
    ppermute x1, starting transfers between devices: 1.92 us -> 5.22 us  [with_halo(): lax.ppermute(lax.slice_in_dim(block, 0, width, axis=dim), axis, backward)]
    transpose x0 -> x1, other arithmetic: none -> 3.16 us  [body(): summed = row_scatter_add(count, order, seg, terms_all.T, n_cells)]
    unnamed x25 -> x21, local copies, waits for them, and re-layouts: 8.29 us -> 6.96 us
  transfers between devices with their start and end apart: 6 -> 6, of which waited for: 2 -> 1; matrix products, arithmetic and copies ran while one was open for 12% -> 36% of each run, Pallas kernels for 12% -> 28%
where the time goes in v4:
time: 160 us; the launch traced here: 159 us
  Pallas kernels  43.7 us (27%)
  other arithmetic  35.8 us (22%)
  local copies, waits for them, and re-layouts  31.2 us (20%)
  between operations  14.4 us (9%)
  starting transfers between devices  13.6 us (8%)
  blocking collectives  10.9 us (7%)
  matrix products  7.19 us (4%)
  waiting for transfers between devices  2.1 us (1%)
    pallas_call x1, Pallas kernels, row_scatter_add(): pl.pallas_call(_scatter_kernel, grid_spec=spec, out_shape=jax.ShapeDtypeS...  25 us
    pallas_call x1, Pallas kernels, row_gather(): pl.pallas_call(_gather_kernel, grid_spec=spec, out_shape=jax.ShapeDtypeSt...  18.7 us
    all_gather x1, blocking collectives, body(): lax.all_gather(cells.astype(jnp.float32), 'sect', axis=0, tiled=True)  10.9 us
    sort x1, other arithmetic, body(): lax.sort(jnp.where(owned, 0, n_all).astype(jnp.int32) + position) % n_all  7.73 us
    dot_general x2, matrix products, pack_slots(): out = jnp.dot(parts, onehot, preferred_element_type=jnp.float32)  7.19 us
    unnamed x21, local copies, waits for them, and re-layouts  6.96 us
    reshape x1, local copies, waits for them, and re-layouts, body(): source = summed.T.reshape(fields, width_x, width_yz)  6.35 us
    pallas_call x1, local copies, waits for them, and re-layouts, row_gather(): pl.pallas_call(_gather_kernel, grid_spec=spec, out_shape=jax.ShapeDtypeSt...  6.34 us
  transfers between devices with their start and end apart: 6, of which 1 were waited for; matrix products, arithmetic and copies ran while one was open for 36% of the time, Pallas kernels for 28%

profile of v4, /device:TPU:3, one launch (start us, length us, event | category | flops | bytes accessed | tf_op | source)
XLA Modules:
  0.0 158.9 jit_solution(12326604012246014580)
XLA Ops:
  8.1 1.9 %pad_maximum_fusion.7 = f32[32,4096]{1,0:T(8,128)} fusion(f32[1,4096]{1,0:T(1,128)S(1)} %bitcast.47, f32[1,4096]{1,0:T(1,128)} %bitcast.48, f32[30,4096]{1,0:T(8,128)} %param.12), kind=kLoop, calls=%fused_computation.58 | loop fusion | flops 262144 | bytes 1048576 | tf_op jit(solution)/shard_map/concatenate | solution.py:145
  10.8 10.9 %all_gather.6 = f32[16384]{0:T(1024)S(1)} all-gather(f32[4096]{0:T(1024)S(1)} %convert_element_type.8), channel_id=1, replica_groups=mesh['sect'=4,'slab'=8] {'sect'}, dimensions={0}, use_global_device_ids=true | all-gather | bytes 81920 | tf_op jit(solution)/shard_map/all_gather | solution.py:149
  23.2 7.7 %sort.14 = (s32[16384]{0:T(1024)S(1)}, s32[16384]{0:T(1024)}) sort(s32[16384]{0:T(1024)S(1)} %get-tuple-element.42, s32[16384]{0:T(1024)S(1)} %iota.12), dimensions={0}, to_apply=%region_1.2 | sort | flops 229376 | bytes 262144 | tf_op jit(solution)/shard_map/sort | solution.py:158
  33.3 4.8 %copy.30 = f32[31,16384]{0,1:T(8,128)} copy(f32[31,16384]{1,0:T(8,128)S(1)} %pad_maximum_fusion.5) | data formatting | bytes 4063232 | tf_op jit(solution)/shard_map/concatenate | solution.py:139
  38.1 18.7 %shard_map.121 = f32[16384,31]{1,0:T(8,128)} custom-call(s32[1]{0:T(128)} %bitcast.1.count_ref, s32[16384]{0:T(1024)} %add_select_fusion.2.order_ref, s32[16384]{0:T(1024)} %get-tuple-element.27.local_ref, f32[16384,31]{1,0:T(8,128)} %bitcast.32), custom_call_target="tpu_custom_call" | custom-call | tf_op jit(solution)/shard_map/pallas_call | solution.py:111
  56.8 6.3 %copy.31 = f32[16384,31]{0,1:T(8,128)} copy(f32[16384,31]{1,0:T(8,128)} %shard_map.121) | data formatting | bytes 4063232 | tf_op jit(solution)/shard_map/pallas_call | solution.py:111
  63.1 1.8 %select_bitcast_fusion = f32[31,16384]{1,0:T(8,128)S(1)} fusion(f32[16384,31]{0,1:T(8,128)} %copy.31, pred[16384]{0:T(1024)(128)(4,1)S(1)} %get-tuple-element.28), kind=kLoop, calls=%fused_computation.35 | loop fusion | flops 507904 | bytes 4079616 | tf_op jit(solution)/shard_map/jit(_where)/select_n | solution.py:161
  64.9 2.0 %slice_reduce_fusion = f32[16384]{0:T(1024)S(1)} fusion(f32[32,16384]{1,0:T(8,128)} %all-gather.2.cloned.1.call-done), kind=kLoop, calls=%fused_computation.48 | loop fusion | flops 475136 | bytes 2031616 | tf_op jit(solution)/shard_map/reduce_sum | solution.py:35
  74.9 1.6 %multiply_reduce_fusion = (f32[16384]{0:T(1024)S(1)}, f32[30,16384]{1,0:T(8,128)}) fusion(f32[30,16384]{1,0:T(8,128)S(1)} %get-tuple-element.25, f32[30]{0:T(128)S(1)} %copy-done.7), kind=kLoop, calls=%fused_computation.26 | loop fusion | flops 1458176 | bytes 3997816 | tf_op jit(solution)/shard_map/reduce_sum | solution.py:53
  76.8 1.6 %maximum_select_fusion = f32[31,16384]{1,0:T(8,128)} fusion(f32[1,16384]{1,0:T(1,128)S(1)} %get-tuple-element.29, f32[30,16384]{1,0:T(8,128)S(1)} %get-tuple-element.24, pred[16384]{0:T(1024)(128)(4,1)S(1)} %get-tuple-element.28), kind=kLoop, calls=%fused_computation.25 | loop fusion | flops 1015808 | bytes 4079616 | tf_op jit(solution)/shard_map/jit(_where)/select_n | solution.py:166
  78.4 2.7 %copy.28 = f32[30,16,1024]{2,0,1:T(8,128)S(1)} copy(f32[30,16,1024]{2,1,0:T(8,128)} %param.10) | data formatting | bytes 3932160 | tf_op args[0]
  81.2 5.2 %collective-permute-start = (f32[31,1,1024]{2,0,1:T(8,128)S(1)}, f32[31,1,1024]{2,0,1:T(8,128)S(1)}, u32[]{:S(2)}, u32[]{:S(2)}) collective-permute-start(f32[31,1,1024]{2,0,1:T(8,128)S(1)} %get-tuple-element.32), channel_id=1, source_target_pairs={{1,0},{2,1},{3,2},{4,3},{5,4},{6,5},{7,6},{9,8},{10,9},{11,10},{12... | collective-permute-start | bytes 380936 | tf_op jit(solution)/shard_map/ppermute | solution.py:23
  86.4 3.5 %collective-permute-start.1 = (f32[31,1,1024]{2,0,1:T(8,128)S(1)}, f32[31,1,1024]{2,0,1:T(8,128)S(1)}, u32[]{:S(2)}, u32[]{:S(2)}) collective-permute-start(f32[31,1,1024]{2,0,1:T(8,128)S(1)} %get-tuple-element.31), channel_id=1, source_target_pairs={{0,1},{1,2},{2,3},{3,4},{4,5},{5,6},{6,7},{8,9},{9,10},{10,11},{11... | collective-permute-start | bytes 380936 | tf_op jit(solution)/shard_map/ppermute | solution.py:20
  91.1 3.2 %maximum_bitcast_fusion = f32[16384,31]{0,1:T(8,128)} fusion(f32[1,16384]{1,0:T(1,128)S(1)} %get-tuple-element.30, f32[30,16384]{1,0:T(8,128)} %get-tuple-element.34), kind=kLoop, calls=%fused_computation.24 | loop fusion | flops 507904 | bytes 4063232 | tf_op jit(solution)/shard_map/transpose | solution.py:172
  94.3 6.3 %copy.32.rows_ref = f32[16384,31]{1,0:T(8,128)} copy(f32[16384,31]{0,1:T(8,128)} %maximum_bitcast_fusion) | data formatting | bytes 4063232 | tf_op jit(solution)/shard_map/transpose | solution.py:172
  100.6 25.0 %shard_map.122 = f32[16384,31]{1,0:T(8,128)} custom-call(s32[1]{0:T(128)} %bitcast.1.count_ref, s32[16384]{0:T(1024)} %add_select_fusion.2.order_ref, s32[16384]{0:T(1024)} %get-tuple-element.26.seg_ref, f32[16384,31]{1,0:T(8,128)} %copy.32.rows_ref), custom_call_target="tpu_custom_call" | custom-call | tf_op jit(solution)/shard_map/pallas_call | solution.py:127
  125.7 6.4 %copy.33 = f32[31,16,1024]{2,0,1:T(8,128)} copy(f32[31,16,1024]{0,2,1:T(8,128)} %bitcast.31) | data formatting | bytes 4063232 | tf_op jit(solution)/shard_map/reshape | solution.py:173
  132.0 2.0 %reduce-precision_convert_fusion.1 = (bf16[31,4096]{1,0:T(8,128)(2,1)S(1)}, bf16[31,4096]{1,0:T(8,128)(2,1)S(1)}, f32[31,4096]{1,0:T(8,128)}, bf16[31,4096]{1,0:T(8,128)(2,1)S(1)}) fusion(f32[31,4096]{1,0:T(8,128)} %reduce-scatter.2.cloned.1.call-done, pred[4096]{0:T(1024)(128)(4,1)S(1)} %get-tuple-element.39), kind=kLoop, calls=%fused_computation.56 | loop fusion | flops 1015808 | bytes 1781760 | tf_op jit(solution)/shard_map/convert.2
  134.0 3.6 %fusion = f32[93,1024]{1,0:T(8,128)S(1)} fusion(s32[4096]{0:T(1024)S(1)} %get-tuple-element.45, bf16[31,4096]{1,0:T(8,128)(2,1)S(1)} %get-tuple-element.36, bf16[31,4096]{1,0:T(8,128)(2,1)S(1)} %get-tuple-element.38, bf16[31,4096]{1,0:T(8,128)(2,1)S(1)} %get-tuple-element.35), kind=kOutput, calls=%fused_computation.2 | convolution fusion | flops 786620416 | bytes 1159168 | tf_op jit(solution)/shard_map/dot_general | solution.py:69
  137.6 2.8 %collective-permute-start.2 = (f32[31,1024]{1,0:T(8,128)S(1)}, f32[31,1024]{1,0:T(8,128)S(1)}, u32[]{:S(2)}, u32[]{:S(2)}) collective-permute-start(f32[31,1024]{1,0:T(8,128)S(1)} %slice_add_fusion.2), channel_id=1, source_target_pairs={{0,1},{1,2},{2,3},{3,4},{4,5},{5,6},{6,7},{8,9},{9,10},{10,11},{11... | collective-permute-start | bytes 380936 | tf_op jit(solution)/shard_map/ppermute | solution.py:31
  140.5 3.6 %fusion.1 = f32[93,1024]{1,0:T(8,128)S(1)} fusion(s32[4096]{0:T(1024)S(1)} %get-tuple-element.44, bf16[31,4096]{1,0:T(8,128)(2,1)S(1)} %get-tuple-element.36, bf16[31,4096]{1,0:T(8,128)(2,1)S(1)} %get-tuple-element.38, bf16[31,4096]{1,0:T(8,128)(2,1)S(1)} %get-tuple-element.35), kind=kOutput, calls=%fused_computation.3 | convolution fusion | flops 786620416 | bytes 1159168 | tf_op jit(solution)/shard_map/dot_general | solution.py:69
  144.1 1.9 %collective-permute-start.3 = (f32[31,1024]{1,0:T(8,128)S(1)}, f32[31,1024]{1,0:T(8,128)S(1)}, u32[]{:S(2)}, u32[]{:S(2)}) collective-permute-start(f32[31,1024]{1,0:T(8,128)S(1)} %slice_add_fusion), channel_id=1, source_target_pairs={{1,0},{2,1},{3,2},{4,3},{5,4},{6,5},{7,6},{9,8},{10,9},{11,10},{12... | collective-permute-start | bytes 380936 | tf_op jit(solution)/shard_map/ppermute | solution.py:31
  146.8 2.5 %copy.34 = f32[31,16,1024]{2,1,0:T(8,128)} copy(f32[31,16,1024]{2,0,1:T(8,128)S(1)} %fusion.11) | data formatting | bytes 4063232
  149.3 2.0 %collective-permute-done.3 = f32[31,1024]{1,0:T(8,128)S(1)} collective-permute-done((f32[31,1024]{1,0:T(8,128)S(1)}, f32[31,1024]{1,0:T(8,128)S(1)}, u32[]{:S(2)}, u32[]{:S(2)}) %collective-permute-start.3) | collective-permute-done | bytes 127008 | tf_op jit(solution)/shard_map/ppermute | solution.py:31
  (65 shorter events, 16.4 us)
Async XLA Ops:
  7.2 24.4 %copy-start.2 = (f32[30,16,1024]{2,1,0:T(8,128)S(1)}, f32[30,16,1024]{2,1,0:T(8,128)}, u32[]{:S(2)}) copy-start(f32[30,16,1024]{2,1,0:T(8,128)} %param.10) | copy-start | bytes 5898244
  7.2 57.7 %all-gather.2.cloned.1.call-start = ((), (), s32[]{:S(2)}) async-start(), calls=%async_computation.1 | async-start | bytes 2621440 | tf_op jit(solution)/shard_map/all_gather | solution.py:148
  10.0 122.0 %reduce-scatter.2.cloned.1.call-start = ((), (), s32[]{:S(2)}) async-start(), calls=%async_computation.2 | async-start | bytes 2621440 | tf_op jit(solution)/shard_map/reduce_scatter | solution.py:167
  31.8 1.2 copy-start.3
  64.9 2.4 %copy-start.5 = (f32[30]{0:T(128)S(1)}, f32[30]{0:T(128)}, u32[]{:S(2)}) copy-start(f32[30]{0:T(128)} %param.18) | copy-start | bytes 364
  64.9 2.4 %copy-start.6 = (f32[30]{0:T(128)S(1)}, f32[30]{0:T(128)}, u32[]{:S(2)}) copy-start(f32[30]{0:T(128)} %param.17) | copy-start | bytes 364
  64.9 2.2 %copy-start = (f32[32,16384]{1,0:T(8,128)S(1)}, f32[32,16384]{1,0:T(8,128)}, u32[]{:S(2)}) copy-start(f32[32,16384]{1,0:T(8,128)} %all-gather.2.cloned.1.call-done) | copy-start | bytes 6291460
  73.7 1.2 copy-start.7
  81.1 8.9 %copy-start.4 = (s32[4096]{0:T(1024)S(1)}, s32[4096]{0:T(1024)}, u32[]{:S(2)}) copy-start(s32[4096]{0:T(1024)} %param.16) | copy-start | bytes 49156
  81.2 64.8 %collective-permute-start = (f32[31,1,1024]{2,0,1:T(8,128)S(1)}, f32[31,1,1024]{2,0,1:T(8,128)S(1)}, u32[]{:S(2)}, u32[]{:S(2)}) collective-permute-start(f32[31,1,1024]{2,0,1:T(8,128)S(1)} %get-tuple-element.32), channel_id=1, source_target_pairs={{1,0},{2,1},{3,2},{4,3},{5,4},{6,5},{7,6},{9,8},{10,9},{11,10},{12... | collective-permute-start | bytes 380936 | tf_op jit(solution)/shard_map/ppermute | solution.py:23
  86.4 59.6 %collective-permute-start.1 = (f32[31,1,1024]{2,0,1:T(8,128)S(1)}, f32[31,1,1024]{2,0,1:T(8,128)S(1)}, u32[]{:S(2)}, u32[]{:S(2)}) collective-permute-start(f32[31,1,1024]{2,0,1:T(8,128)S(1)} %get-tuple-element.31), channel_id=1, source_target_pairs={{0,1},{1,2},{2,3},{3,4},{4,5},{5,6},{6,7},{8,9},{9,10},{10,11},{11... | collective-permute-start | bytes 380936 | tf_op jit(solution)/shard_map/ppermute | solution.py:20
  137.6 11.6 %collective-permute-start.2 = (f32[31,1024]{1,0:T(8,128)S(1)}, f32[31,1024]{1,0:T(8,128)S(1)}, u32[]{:S(2)}, u32[]{:S(2)}) collective-permute-start(f32[31,1024]{1,0:T(8,128)S(1)} %slice_add_fusion.2), channel_id=1, source_target_pairs={{0,1},{1,2},{2,3},{3,4},{4,5},{5,6},{6,7},{8,9},{9,10},{10,11},{11... | collective-permute-start | bytes 380936 | tf_op jit(solution)/shard_map/ppermute | solution.py:31
  140.5 5.6 %copy-start.1 = (f32[31,16,1024]{2,0,1:T(8,128)S(1)}, f32[31,16,1024]{2,0,1:T(8,128)}, u32[]{:S(2)}) copy-start(f32[31,16,1024]{2,0,1:T(8,128)} %copy.33) | copy-start | bytes 6094852
  144.1 7.2 %collective-permute-start.3 = (f32[31,1024]{1,0:T(8,128)S(1)}, f32[31,1024]{1,0:T(8,128)S(1)}, u32[]{:S(2)}, u32[]{:S(2)}) collective-permute-start(f32[31,1024]{1,0:T(8,128)S(1)} %slice_add_fusion), channel_id=1, source_target_pairs={{1,0},{2,1},{3,2},{4,3},{5,4},{6,5},{7,6},{9,8},{10,9},{11,10},{12... | collective-permute-start | bytes 380936 | tf_op jit(solution)/shard_map/ppermute | solution.py:31
Sparse Core Ops, SparseCore 0:
  10.1 46.8 all-gather.1
  78.5 47.2 reduce-scatter.1

commit v5 on v4

--- a/solution.py
+++ b/solution.py
@@ -71,32 +71,32 @@
     return (out[:rows] + out[rows : 2 * rows]) + out[2 * rows :]
 
 
-def _gather_kernel(count_ref, order_ref, local_ref, table_ref, out_ref):
+def _gather_kernel(count_ref, dst_ref, src_ref, table_ref, out_ref):
     out_ref[...] = jnp.zeros(out_ref.shape, out_ref.dtype)
 
     def step(i, carry):
         base = i * UNROLL
         for j in range(UNROLL):
-            p = order_ref[base + j]
-            out_ref[pl.ds(p, 1), :] = table_ref[pl.ds(local_ref[p], 1), :]
+            out_ref[pl.ds(dst_ref[base + j], 1), :] = table_ref[pl.ds(src_ref[base + j], 1), :]
         return carry
 
     lax.fori_loop(0, (count_ref[0] + UNROLL - 1) // UNROLL, step, 0)
 
 
-def _scatter_kernel(count_ref, order_ref, seg_ref, rows_ref, out_ref, acc_ref):
-    acc_ref[...] = jnp.zeros(acc_ref.shape, acc_ref.dtype)
+def _scatter_kernel(count_ref, src_ref, seg_ref, rows_ref, out_ref, even_ref, odd_ref):
+    even_ref[...] = jnp.zeros(even_ref.shape, even_ref.dtype)
+    odd_ref[...] = jnp.zeros(odd_ref.shape, odd_ref.dtype)
 
     def step(i, carry):
         base = i * UNROLL
         for j in range(UNROLL):
-            p = order_ref[base + j]
-            s = seg_ref[p]
-            acc_ref[pl.ds(s, 1), :] += rows_ref[pl.ds(p, 1), :]
+            acc = even_ref if j % 2 == 0 else odd_ref
+            acc[pl.ds(seg_ref[base + j], 1), :] += rows_ref[pl.ds(src_ref[base + j], 1), :]
         return carry
 
     lax.fori_loop(0, (count_ref[0] + UNROLL - 1) // UNROLL, step, 0)
-    out_ref[...] = acc_ref[pl.ds(0, out_ref.shape[0]), :]
+    rows = out_ref.shape[0]
+    out_ref[...] = even_ref[pl.ds(0, rows), :] + odd_ref[pl.ds(0, rows), :]
 
 
 def row_gather(count, order, local, table):
@@ -122,7 +122,7 @@
         grid=(1,),
         in_specs=[pl.BlockSpec((n_rows, width), lambda i, *_: (0, 0))],
         out_specs=pl.BlockSpec((n_cells, width), lambda i, *_: (0, 0)),
-        scratch_shapes=[pltpu.VMEM((n_cells + UNROLL, width), jnp.float32)],
+        scratch_shapes=[pltpu.VMEM((n_cells + UNROLL, width), jnp.float32)] * 2,
     )
     return pl.pallas_call(
         _scatter_kernel,
@@ -155,10 +155,15 @@
     local_cell = (cell_row * width_yz + cell_col % width_yz).astype(jnp.int32)
     seg = jnp.where(owned, local_cell, n_cells).astype(jnp.int32)
     position = jnp.arange(n_all, dtype=jnp.int32)
-    order = lax.sort(jnp.where(owned, 0, n_all).astype(jnp.int32) + position) % n_all
+    keys = jnp.where(owned, 0, n_all).astype(jnp.int32) + position
+    _, order, local_sorted, seg_sorted = lax.sort(
+        (keys, position, local_cell, seg), num_keys=1
+    )
     count = jnp.sum(owned.astype(jnp.int32)).reshape(1)
     table = gas_block.reshape(fields, n_cells).T
-    at_parcel = jnp.where(owned[None, :], row_gather(count, order, local_cell, table).T, 0.0)
+    at_parcel = jnp.where(
+        owned[None, :], row_gather(count, order, local_sorted, table).T, 0.0
+    )
     state_all, terms_all = parcel_update(
         all_in[:NC], all_in[NC], all_in[NC + 1], at_parcel[:NC], at_parcel[NC],
         volat_a, volat_b, latent,
@@ -169,7 +174,7 @@
     down = padded[:, :-2]
     upper = padded[:, 2:]
     flowed = gas_block + 0.2 * (upper - 2.0 * gas_block + down) - 0.3 * (gas_block - down)
-    summed = row_scatter_add(count, order, seg, terms_all.T, n_cells)
+    summed = row_scatter_add(count, order, seg_sorted, terms_all.T, n_cells)
     source = summed.T.reshape(fields, width_x, width_yz)
     gas_next = flowed + source
     kept = jnp.where(moves[None] == 0, state, 0.0)

time: 160 us -> 155 us (0.969)
  Pallas kernels: 43.7 us -> 39.8 us
    pallas_call x1, Pallas kernels: 25 us -> 21.8 us  [row_scatter_add(): pl.pallas_call(_scatter_kernel, grid_spec=spec, out_shape=jax.ShapeDtypeS...]
  transfers between devices with their start and end apart: 6 -> 6, of which waited for: 1 -> 1; matrix products, arithmetic and copies ran while one was open for 36% -> 37% of each run, Pallas kernels for 28% -> 26%
where the time goes in v5:
time: 155 us; the launch traced here: 154 us
  Pallas kernels  39.8 us (26%)
  other arithmetic  35.1 us (23%)
  local copies, waits for them, and re-layouts  31.2 us (20%)
  between operations  14.4 us (9%)
  starting transfers between devices  13.2 us (9%)
  blocking collectives  10.9 us (7%)
  matrix products  7.19 us (5%)
  waiting for transfers between devices  2.1 us (1%)
    pallas_call x1, Pallas kernels, row_scatter_add(): pl.pallas_call(_scatter_kernel, grid_spec=spec, out_shape=jax.ShapeDtypeS...  21.8 us
    pallas_call x1, Pallas kernels, row_gather(): pl.pallas_call(_gather_kernel, grid_spec=spec, out_shape=jax.ShapeDtypeSt...  18 us
    all_gather x1, blocking collectives, body(): lax.all_gather(cells.astype(jnp.float32), 'sect', axis=0, tiled=True)  10.9 us
    sort x1, other arithmetic, body(): lax.sort((keys, position, local_cell, seg), num_keys=1)  8.29 us
    dot_general x2, matrix products, pack_slots(): out = jnp.dot(parts, onehot, preferred_element_type=jnp.float32)  7.19 us
    unnamed x21, local copies, waits for them, and re-layouts  6.96 us
    reshape x1, local copies, waits for them, and re-layouts, body(): source = summed.T.reshape(fields, width_x, width_yz)  6.41 us
    pallas_call x1, local copies, waits for them, and re-layouts, row_gather(): pl.pallas_call(_gather_kernel, grid_spec=spec, out_shape=jax.ShapeDtypeSt...  6.37 us
  transfers between devices with their start and end apart: 6, of which 1 were waited for; matrix products, arithmetic and copies ran while one was open for 37% of the time, Pallas kernels for 26%

profile of v5, /device:TPU:3, one launch (start us, length us, event | category | flops | bytes accessed | tf_op | source)
XLA Modules:
  0.0 153.8 jit_solution(13802851862648650786)
XLA Ops:
  8.1 1.9 %pad_maximum_fusion.7 = f32[32,4096]{1,0:T(8,128)} fusion(f32[1,4096]{1,0:T(1,128)S(1)} %bitcast.47, f32[1,4096]{1,0:T(1,128)} %bitcast.48, f32[30,4096]{1,0:T(8,128)} %param.12), kind=kLoop, calls=%fused_computation.58 | loop fusion | flops 262144 | bytes 1048576 | tf_op jit(solution)/shard_map/concatenate | solution.py:145
  10.8 10.9 %all_gather.6 = f32[16384]{0:T(1024)S(1)} all-gather(f32[4096]{0:T(1024)S(1)} %convert_element_type.8), channel_id=1, replica_groups=mesh['sect'=4,'slab'=8] {'sect'}, dimensions={0}, use_global_device_ids=true | all-gather | bytes 81920 | tf_op jit(solution)/shard_map/all_gather | solution.py:149
  24.3 4.7 %copy.30 = f32[31,16384]{0,1:T(8,128)} copy(f32[31,16384]{1,0:T(8,128)S(1)} %pad_maximum_fusion.5) | data formatting | bytes 4063232 | tf_op jit(solution)/shard_map/concatenate | solution.py:139
  29.0 8.3 %sort.27 = (s32[16384]{0:T(1024)}, s32[16384]{0:T(1024)}, s32[16384]{0:T(1024)}, s32[16384]{0:T(1024)}) sort(s32[16384]{0:T(1024)S(1)} %get-tuple-element.45, s32[16384]{0:T(1024)S(1)} %iota.11, s32[16384]{0:T(1024)S(1)} %get-tuple-element.30, s32[16384]{0:T(1024)S(1)} %get-tuple-element.29), dimensions={0}, to_apply=%region_1.2 | sort | flops 229376 | bytes 524288 | tf_op jit(solution)/shard_map/sort | solution.py:159
  37.3 18.0 %shard_map.121 = f32[16384,31]{1,0:T(8,128)} custom-call(s32[1]{0:T(128)} %bitcast.1.count_ref, s32[16384]{0:T(1024)} %get-tuple-element.6.dst_ref.src_ref, s32[16384]{0:T(1024)} %get-tuple-element.8.src_ref, f32[16384,31]{1,0:T(8,128)} %bitcast.31), custom_call_target="tpu_custom_call" | custom-call | tf_op jit(solution)/shard_map/pallas_call | solution.py:111
  55.3 6.4 %copy.31 = f32[16384,31]{0,1:T(8,128)} copy(f32[16384,31]{1,0:T(8,128)} %shard_map.121) | data formatting | bytes 4063232 | tf_op jit(solution)/shard_map/pallas_call | solution.py:111
  61.6 1.8 %select_bitcast_fusion = f32[31,16384]{1,0:T(8,128)S(1)} fusion(f32[16384,31]{0,1:T(8,128)} %copy.31, pred[16384]{0:T(1024)(128)(4,1)S(1)} %get-tuple-element.31), kind=kLoop, calls=%fused_computation.35 | loop fusion | flops 507904 | bytes 4079616 | tf_op jit(solution)/shard_map/jit(_where)/select_n | solution.py:164
  63.5 2.0 %slice_reduce_fusion = f32[16384]{0:T(1024)S(1)} fusion(f32[32,16384]{1,0:T(8,128)} %all-gather.2.cloned.1.call-done), kind=kLoop, calls=%fused_computation.48 | loop fusion | flops 475136 | bytes 2031616 | tf_op jit(solution)/shard_map/reduce_sum | solution.py:35
  73.4 1.6 %multiply_reduce_fusion = (f32[16384]{0:T(1024)S(1)}, f32[30,16384]{1,0:T(8,128)}) fusion(f32[30,16384]{1,0:T(8,128)S(1)} %get-tuple-element.28, f32[30]{0:T(128)S(1)} %copy-done.7), kind=kLoop, calls=%fused_computation.26 | loop fusion | flops 1458176 | bytes 3997816 | tf_op jit(solution)/shard_map/reduce_sum | solution.py:53
  75.3 1.6 %maximum_select_fusion = f32[31,16384]{1,0:T(8,128)} fusion(f32[1,16384]{1,0:T(1,128)S(1)} %get-tuple-element.32, f32[30,16384]{1,0:T(8,128)S(1)} %get-tuple-element.27, pred[16384]{0:T(1024)(128)(4,1)S(1)} %get-tuple-element.31), kind=kLoop, calls=%fused_computation.25 | loop fusion | flops 1015808 | bytes 4079616 | tf_op jit(solution)/shard_map/jit(_where)/select_n | solution.py:171
  76.9 2.7 %copy.28 = f32[30,16,1024]{2,0,1:T(8,128)S(1)} copy(f32[30,16,1024]{2,1,0:T(8,128)} %param.10) | data formatting | bytes 3932160 | tf_op args[0]
  79.7 5.5 %collective-permute-start = (f32[31,1,1024]{2,0,1:T(8,128)S(1)}, f32[31,1,1024]{2,0,1:T(8,128)S(1)}, u32[]{:S(2)}, u32[]{:S(2)}) collective-permute-start(f32[31,1,1024]{2,0,1:T(8,128)S(1)} %get-tuple-element.35), channel_id=1, source_target_pairs={{1,0},{2,1},{3,2},{4,3},{5,4},{6,5},{7,6},{9,8},{10,9},{11,10},{12... | collective-permute-start | bytes 380936 | tf_op jit(solution)/shard_map/ppermute | solution.py:23
  85.2 3.1 %collective-permute-start.1 = (f32[31,1,1024]{2,0,1:T(8,128)S(1)}, f32[31,1,1024]{2,0,1:T(8,128)S(1)}, u32[]{:S(2)}, u32[]{:S(2)}) collective-permute-start(f32[31,1,1024]{2,0,1:T(8,128)S(1)} %get-tuple-element.34), channel_id=1, source_target_pairs={{0,1},{1,2},{2,3},{3,4},{4,5},{5,6},{6,7},{8,9},{9,10},{10,11},{11... | collective-permute-start | bytes 380936 | tf_op jit(solution)/shard_map/ppermute | solution.py:20
  89.5 3.2 %maximum_bitcast_fusion = f32[16384,31]{0,1:T(8,128)} fusion(f32[1,16384]{1,0:T(1,128)S(1)} %get-tuple-element.33, f32[30,16384]{1,0:T(8,128)} %get-tuple-element.37), kind=kLoop, calls=%fused_computation.24 | loop fusion | flops 507904 | bytes 4063232 | tf_op jit(solution)/shard_map/transpose | solution.py:177
  92.7 6.3 %copy.32.rows_ref = f32[16384,31]{1,0:T(8,128)} copy(f32[16384,31]{0,1:T(8,128)} %maximum_bitcast_fusion) | data formatting | bytes 4063232 | tf_op jit(solution)/shard_map/transpose | solution.py:177
  99.0 21.8 %shard_map.122 = f32[16384,31]{1,0:T(8,128)} custom-call(s32[1]{0:T(128)} %bitcast.1.count_ref, s32[16384]{0:T(1024)} %get-tuple-element.6.dst_ref.src_ref, s32[16384]{0:T(1024)} %get-tuple-element.7.seg_ref, f32[16384,31]{1,0:T(8,128)} %copy.32.rows_ref), custom_call_target="tpu_custom_call" | custom-call | tf_op jit(solution)/shard_map/pallas_call | solution.py:127
  120.8 6.4 %copy.33 = f32[31,16,1024]{2,0,1:T(8,128)} copy(f32[31,16,1024]{0,2,1:T(8,128)} %bitcast.32) | data formatting | bytes 4063232 | tf_op jit(solution)/shard_map/reshape | solution.py:178
  127.2 2.0 %reduce-precision_convert_fusion.1 = (bf16[31,4096]{1,0:T(8,128)(2,1)S(1)}, bf16[31,4096]{1,0:T(8,128)(2,1)S(1)}, f32[31,4096]{1,0:T(8,128)}, bf16[31,4096]{1,0:T(8,128)(2,1)S(1)}) fusion(f32[31,4096]{1,0:T(8,128)} %reduce-scatter.2.cloned.1.call-done, pred[4096]{0:T(1024)(128)(4,1)S(1)} %get-tuple-element.42), kind=kLoop, calls=%fused_computation.56 | loop fusion | flops 1015808 | bytes 1781760 | tf_op jit(solution)/shard_map/convert.2
  129.2 3.6 %fusion = f32[93,1024]{1,0:T(8,128)S(1)} fusion(s32[4096]{0:T(1024)S(1)} %get-tuple-element.48, bf16[31,4096]{1,0:T(8,128)(2,1)S(1)} %get-tuple-element.39, bf16[31,4096]{1,0:T(8,128)(2,1)S(1)} %get-tuple-element.41, bf16[31,4096]{1,0:T(8,128)(2,1)S(1)} %get-tuple-element.38), kind=kOutput, calls=%fused_computation.2 | convolution fusion | flops 786620416 | bytes 1159168 | tf_op jit(solution)/shard_map/dot_general | solution.py:69
  132.8 2.5 %collective-permute-start.2 = (f32[31,1024]{1,0:T(8,128)S(1)}, f32[31,1024]{1,0:T(8,128)S(1)}, u32[]{:S(2)}, u32[]{:S(2)}) collective-permute-start(f32[31,1024]{1,0:T(8,128)S(1)} %slice_add_fusion.2), channel_id=1, source_target_pairs={{0,1},{1,2},{2,3},{3,4},{4,5},{5,6},{6,7},{8,9},{9,10},{10,11},{11... | collective-permute-start | bytes 380936 | tf_op jit(solution)/shard_map/ppermute | solution.py:31
  135.4 3.6 %fusion.1 = f32[93,1024]{1,0:T(8,128)S(1)} fusion(s32[4096]{0:T(1024)S(1)} %get-tuple-element.47, bf16[31,4096]{1,0:T(8,128)(2,1)S(1)} %get-tuple-element.39, bf16[31,4096]{1,0:T(8,128)(2,1)S(1)} %get-tuple-element.41, bf16[31,4096]{1,0:T(8,128)(2,1)S(1)} %get-tuple-element.38), kind=kOutput, calls=%fused_computation.3 | convolution fusion | flops 786620416 | bytes 1159168 | tf_op jit(solution)/shard_map/dot_general | solution.py:69
  139.0 1.9 %collective-permute-start.3 = (f32[31,1024]{1,0:T(8,128)S(1)}, f32[31,1024]{1,0:T(8,128)S(1)}, u32[]{:S(2)}, u32[]{:S(2)}) collective-permute-start(f32[31,1024]{1,0:T(8,128)S(1)} %slice_add_fusion), channel_id=1, source_target_pairs={{1,0},{2,1},{3,2},{4,3},{5,4},{6,5},{7,6},{9,8},{10,9},{11,10},{12... | collective-permute-start | bytes 380936 | tf_op jit(solution)/shard_map/ppermute | solution.py:31
  141.7 2.5 %copy.34 = f32[31,16,1024]{2,1,0:T(8,128)} copy(f32[31,16,1024]{2,0,1:T(8,128)S(1)} %fusion.11) | data formatting | bytes 4063232
  144.2 2.0 %collective-permute-done.3 = f32[31,1024]{1,0:T(8,128)S(1)} collective-permute-done((f32[31,1024]{1,0:T(8,128)S(1)}, f32[31,1024]{1,0:T(8,128)S(1)}, u32[]{:S(2)}, u32[]{:S(2)}) %collective-permute-start.3) | collective-permute-done | bytes 127008 | tf_op jit(solution)/shard_map/ppermute | solution.py:31
  (64 shorter events, 15.2 us)
Async XLA Ops:
  7.2 15.4 %copy-start.2 = (f32[30,16,1024]{2,1,0:T(8,128)S(1)}, f32[30,16,1024]{2,1,0:T(8,128)}, u32[]{:S(2)}) copy-start(f32[30,16,1024]{2,1,0:T(8,128)} %param.10) | copy-start | bytes 5898244
  7.2 56.3 %all-gather.2.cloned.1.call-start = ((), (), s32[]{:S(2)}) async-start(), calls=%async_computation.1 | async-start | bytes 2621440 | tf_op jit(solution)/shard_map/all_gather | solution.py:148
  10.0 117.2 %reduce-scatter.2.cloned.1.call-start = ((), (), s32[]{:S(2)}) async-start(), calls=%async_computation.2 | async-start | bytes 2621440 | tf_op jit(solution)/shard_map/reduce_scatter | solution.py:172
  22.8 1.2 copy-start.3
  63.4 2.4 %copy-start.5 = (f32[30]{0:T(128)S(1)}, f32[30]{0:T(128)}, u32[]{:S(2)}) copy-start(f32[30]{0:T(128)} %param.18) | copy-start | bytes 364
  63.4 2.4 %copy-start.6 = (f32[30]{0:T(128)S(1)}, f32[30]{0:T(128)}, u32[]{:S(2)}) copy-start(f32[30]{0:T(128)} %param.17) | copy-start | bytes 364
  63.5 2.2 %copy-start = (f32[32,16384]{1,0:T(8,128)S(1)}, f32[32,16384]{1,0:T(8,128)}, u32[]{:S(2)}) copy-start(f32[32,16384]{1,0:T(8,128)} %all-gather.2.cloned.1.call-done) | copy-start | bytes 6291460
  72.2 1.2 copy-start.7
  79.6 8.8 %copy-start.4 = (s32[4096]{0:T(1024)S(1)}, s32[4096]{0:T(1024)}, u32[]{:S(2)}) copy-start(s32[4096]{0:T(1024)} %param.16) | copy-start | bytes 49156
  79.7 61.2 %collective-permute-start = (f32[31,1,1024]{2,0,1:T(8,128)S(1)}, f32[31,1,1024]{2,0,1:T(8,128)S(1)}, u32[]{:S(2)}, u32[]{:S(2)}) collective-permute-start(f32[31,1,1024]{2,0,1:T(8,128)S(1)} %get-tuple-element.35), channel_id=1, source_target_pairs={{1,0},{2,1},{3,2},{4,3},{5,4},{6,5},{7,6},{9,8},{10,9},{11,10},{12... | collective-permute-start | bytes 380936 | tf_op jit(solution)/shard_map/ppermute | solution.py:23
  85.2 55.8 %collective-permute-start.1 = (f32[31,1,1024]{2,0,1:T(8,128)S(1)}, f32[31,1,1024]{2,0,1:T(8,128)S(1)}, u32[]{:S(2)}, u32[]{:S(2)}) collective-permute-start(f32[31,1,1024]{2,0,1:T(8,128)S(1)} %get-tuple-element.34), channel_id=1, source_target_pairs={{0,1},{1,2},{2,3},{3,4},{4,5},{5,6},{6,7},{8,9},{9,10},{10,11},{11... | collective-permute-start | bytes 380936 | tf_op jit(solution)/shard_map/ppermute | solution.py:20
  132.8 11.3 %collective-permute-start.2 = (f32[31,1024]{1,0:T(8,128)S(1)}, f32[31,1024]{1,0:T(8,128)S(1)}, u32[]{:S(2)}, u32[]{:S(2)}) collective-permute-start(f32[31,1024]{1,0:T(8,128)S(1)} %slice_add_fusion.2), channel_id=1, source_target_pairs={{0,1},{1,2},{2,3},{3,4},{4,5},{5,6},{6,7},{8,9},{9,10},{10,11},{11... | collective-permute-start | bytes 380936 | tf_op jit(solution)/shard_map/ppermute | solution.py:31
  135.4 5.6 %copy-start.1 = (f32[31,16,1024]{2,0,1:T(8,128)S(1)}, f32[31,16,1024]{2,0,1:T(8,128)}, u32[]{:S(2)}) copy-start(f32[31,16,1024]{2,0,1:T(8,128)} %copy.33) | copy-start | bytes 6094852
  139.0 7.2 %collective-permute-start.3 = (f32[31,1024]{1,0:T(8,128)S(1)}, f32[31,1024]{1,0:T(8,128)S(1)}, u32[]{:S(2)}, u32[]{:S(2)}) collective-permute-start(f32[31,1024]{1,0:T(8,128)S(1)} %slice_add_fusion), channel_id=1, source_target_pairs={{1,0},{2,1},{3,2},{4,3},{5,4},{6,5},{7,6},{9,8},{10,9},{11,10},{12... | collective-permute-start | bytes 380936 | tf_op jit(solution)/shard_map/ppermute | solution.py:31
Sparse Core Ops, SparseCore 0:
  10.1 46.8 all-gather.1
  77.0 47.5 reduce-scatter.1

commit v6 on v5

--- a/solution.py
+++ b/solution.py
@@ -131,6 +131,18 @@
     )(count, order, seg, rows)
 
 
+def gather_sect(x):
+    count = lax.axis_size("sect")
+    own = lax.axis_index("sect")
+    parts = [x] + [
+        lax.ppermute(x, "sect", [(i, (i + k) % count) for i in range(count)])
+        for k in range(1, count)
+    ]
+    stacked = jnp.stack(parts)
+    where = (own - jnp.arange(count, dtype=jnp.int32)) % count
+    return jnp.take(stacked, where, axis=0).reshape(-1)
+
+
 def field_major(x):
     return with_layout_constraint(x, Layout(major_to_minor=(0, 1)))
 
@@ -146,8 +158,7 @@
         [masses, drop_temp[None], flags.astype(jnp.float32)[None]], axis=0
     )
     all_in = field_major(lax.all_gather(field_major(parcel_in), "sect", axis=1, tiled=True))
-    all_cells = lax.all_gather(cells.astype(jnp.float32), "sect", axis=0, tiled=True)
-    all_cells = all_cells.astype(jnp.int32)
+    all_cells = gather_sect(cells)
     n_all = all_cells.shape[0]
     cell_row = all_cells // plane
     cell_col = all_cells % plane

time: 155 us -> 149 us (0.961)
  blocking collectives: 10.9 us -> 0 us
  starting transfers between devices: 13.2 us -> 15.8 us
  local copies, waits for them, and re-layouts: 31.2 us -> 33.5 us
    all_gather x1 -> x0, blocking collectives: 10.9 us -> none  [body(): lax.all_gather(cells.astype(jnp.float32), 'sect', axis=0, tiled=True)]
    ppermute x0 -> x3, starting transfers between devices: none -> 4.73 us  [gather_sect(): lax.ppermute(x, 'sect', [(i, (i + k) % count) for i in range(count)])]
    ppermute x1, starting transfers between devices: 5.47 us -> 3.14 us  [with_halo(): lax.ppermute(lax.slice_in_dim(block, 0, width, axis=dim), axis, backward)]
    unnamed x21 -> x22, local copies, waits for them, and re-layouts: 6.96 us -> 8.58 us
  transfers between devices with their start and end apart: 6 -> 9, of which waited for: 1 -> 2; matrix products, arithmetic and copies ran while one was open for 37% -> 41% of each run, Pallas kernels for 26% -> 27%
where the time goes in v6:
time: 149 us; the launch traced here: 147 us
  Pallas kernels  39.8 us (27%)
  other arithmetic  34.5 us (23%)
  local copies, waits for them, and re-layouts  33.5 us (22%)
  starting transfers between devices  15.8 us (11%)
  between operations  14.4 us (10%)
  matrix products  7.19 us (5%)
  waiting for transfers between devices  2.19 us (1%)
    pallas_call x1, Pallas kernels, row_scatter_add(): pl.pallas_call(_scatter_kernel, grid_spec=spec, out_shape=jax.ShapeDtypeS...  21.8 us
    pallas_call x1, Pallas kernels, row_gather(): pl.pallas_call(_gather_kernel, grid_spec=spec, out_shape=jax.ShapeDtypeSt...  18 us
    unnamed x22, local copies, waits for them, and re-layouts  8.58 us
    sort x1, other arithmetic, body(): lax.sort((keys, position, local_cell, seg), num_keys=1)  8.29 us
    dot_general x2, matrix products, pack_slots(): out = jnp.dot(parts, onehot, preferred_element_type=jnp.float32)  7.19 us
    pallas_call x1, local copies, waits for them, and re-layouts, row_gather(): pl.pallas_call(_gather_kernel, grid_spec=spec, out_shape=jax.ShapeDtypeSt...  6.37 us
    reshape x1, local copies, waits for them, and re-layouts, body(): source = summed.T.reshape(fields, width_x, width_yz)  6.36 us
    transpose x1, local copies, waits for them, and re-layouts, body(): summed = row_scatter_add(count, order, seg_sorted, terms_all.T, n_cells)  6.35 us
  transfers between devices with their start and end apart: 9, of which 2 were waited for; matrix products, arithmetic and copies ran while one was open for 41% of the time, Pallas kernels for 27%

profile of v6, /device:TPU:3, one launch (start us, length us, event | category | flops | bytes accessed | tf_op | source)
XLA Modules:
  0.0 147.4 jit_solution(656410419988401972)
XLA Ops:
  8.6 2.3 %collective-permute-start.3 = (s32[4096]{0:T(1024)}, s32[4096]{0:T(1024)S(1)}, u32[]{:S(2)}, u32[]{:S(2)}) collective-permute-start(s32[4096]{0:T(1024)} %param.14), channel_id=1, source_target_pairs={{0,16},{8,24},{16,0},{24,8},{1,17},{9,25},{17,1},{25,9},{2,18},{10... | collective-permute-start | bytes 49160 | tf_op jit(solution)/shard_map/ppermute | solution.py:138
  12.7 1.9 %pad_maximum_fusion.7 = f32[32,4096]{1,0:T(8,128)} fusion(f32[1,4096]{1,0:T(1,128)S(1)} %bitcast.57, f32[1,4096]{1,0:T(1,128)} %bitcast.58, f32[30,4096]{1,0:T(8,128)} %param.12), kind=kLoop, calls=%fused_computation.59 | loop fusion | flops 262144 | bytes 1048576 | tf_op jit(solution)/shard_map/concatenate | solution.py:157
  14.7 1.8 %pad.33 = f32[32,16,1024]{2,1,0:T(8,128)S(1)} pad(f32[30,16,1024]{2,1,0:T(8,128)} %param.10, f32[]{:T(128)} %constant.118.clone.1), padding=0_2x0_0x0_0 | pad | bytes 4063236
  18.0 4.8 %copy.30 = f32[31,16384]{0,1:T(8,128)} copy(f32[31,16384]{1,0:T(8,128)S(1)} %pad_maximum_fusion.5) | data formatting | bytes 4063232 | tf_op jit(solution)/shard_map/concatenate | solution.py:151
  24.6 8.3 %sort.27 = (s32[16384]{0:T(1024)}, s32[16384]{0:T(1024)}, s32[16384]{0:T(1024)}, s32[16384]{0:T(1024)}) sort(s32[16384]{0:T(1024)S(1)} %iota_add_fusion, s32[16384]{0:T(1024)S(1)} %iota.19, s32[16384]{0:T(1024)S(1)} %get-tuple-element.30, s32[16384]{0:T(1024)S(1)} %get-tuple-element.29), dimensions={0}, to_apply=%region_1.2 | sort | flops 229376 | bytes 524288 | tf_op jit(solution)/shard_map/sort | solution.py:170
  32.9 18.0 %shard_map.121 = f32[16384,31]{1,0:T(8,128)} custom-call(s32[1]{0:T(128)} %bitcast.6.count_ref, s32[16384]{0:T(1024)} %get-tuple-element.6.dst_ref.src_ref, s32[16384]{0:T(1024)} %get-tuple-element.8.src_ref, f32[16384,31]{1,0:T(8,128)} %bitcast.40), custom_call_target="tpu_custom_call" | custom-call | tf_op jit(solution)/shard_map/pallas_call | solution.py:111
  50.9 6.4 %copy.31 = f32[16384,31]{0,1:T(8,128)} copy(f32[16384,31]{1,0:T(8,128)} %shard_map.121) | data formatting | bytes 4063232 | tf_op jit(solution)/shard_map/pallas_call | solution.py:111
  57.2 1.8 %select_bitcast_fusion = f32[31,16384]{1,0:T(8,128)S(1)} fusion(f32[16384,31]{0,1:T(8,128)} %copy.31, pred[16384]{0:T(1024)(128)(4,1)S(1)} %get-tuple-element.31), kind=kLoop, calls=%fused_computation.36 | loop fusion | flops 507904 | bytes 4079616 | tf_op jit(solution)/shard_map/jit(_where)/select_n | solution.py:175
  59.4 2.0 %slice_reduce_fusion = f32[16384]{0:T(1024)S(1)} fusion(f32[32,16384]{1,0:T(8,128)} %all-gather.2.cloned.1.call-done), kind=kLoop, calls=%fused_computation.49 | loop fusion | flops 475136 | bytes 2031616 | tf_op jit(solution)/shard_map/reduce_sum | solution.py:35
  69.3 1.6 %multiply_reduce_fusion = (f32[16384]{0:T(1024)S(1)}, f32[30,16384]{1,0:T(8,128)}) fusion(f32[30,16384]{1,0:T(8,128)S(1)} %get-tuple-element.28, f32[30]{0:T(128)S(1)} %copy-done.7), kind=kLoop, calls=%fused_computation.27 | loop fusion | flops 1458176 | bytes 3997816 | tf_op jit(solution)/shard_map/reduce_sum | solution.py:53
  72.8 2.7 %copy.28 = f32[30,16,1024]{2,0,1:T(8,128)S(1)} copy(f32[30,16,1024]{2,1,0:T(8,128)} %param.10) | data formatting | bytes 3932160 | tf_op args[0]
  75.6 3.1 %collective-permute-start = (f32[31,1,1024]{2,0,1:T(8,128)S(1)}, f32[31,1,1024]{2,0,1:T(8,128)S(1)}, u32[]{:S(2)}, u32[]{:S(2)}) collective-permute-start(f32[31,1,1024]{2,0,1:T(8,128)S(1)} %get-tuple-element.35), channel_id=1, source_target_pairs={{1,0},{2,1},{3,2},{4,3},{5,4},{6,5},{7,6},{9,8},{10,9},{11,10},{12... | collective-permute-start | bytes 380936 | tf_op jit(solution)/shard_map/ppermute | solution.py:23
  78.8 3.5 %collective-permute-start.1 = (f32[31,1,1024]{2,0,1:T(8,128)S(1)}, f32[31,1,1024]{2,0,1:T(8,128)S(1)}, u32[]{:S(2)}, u32[]{:S(2)}) collective-permute-start(f32[31,1,1024]{2,0,1:T(8,128)S(1)} %get-tuple-element.34), channel_id=1, source_target_pairs={{0,1},{1,2},{2,3},{3,4},{4,5},{5,6},{6,7},{8,9},{9,10},{10,11},{11... | collective-permute-start | bytes 380936 | tf_op jit(solution)/shard_map/ppermute | solution.py:20
  83.5 3.2 %maximum_bitcast_fusion = f32[16384,31]{0,1:T(8,128)} fusion(f32[1,16384]{1,0:T(1,128)S(1)} %get-tuple-element.33, f32[30,16384]{1,0:T(8,128)} %get-tuple-element.37), kind=kLoop, calls=%fused_computation.25 | loop fusion | flops 507904 | bytes 4063232 | tf_op jit(solution)/shard_map/transpose | solution.py:188
  86.7 6.4 %copy.32.rows_ref = f32[16384,31]{1,0:T(8,128)} copy(f32[16384,31]{0,1:T(8,128)} %maximum_bitcast_fusion) | data formatting | bytes 4063232 | tf_op jit(solution)/shard_map/transpose | solution.py:188
  93.1 21.8 %shard_map.122 = f32[16384,31]{1,0:T(8,128)} custom-call(s32[1]{0:T(128)} %bitcast.6.count_ref, s32[16384]{0:T(1024)} %get-tuple-element.6.dst_ref.src_ref, s32[16384]{0:T(1024)} %get-tuple-element.7.seg_ref, f32[16384,31]{1,0:T(8,128)} %copy.32.rows_ref), custom_call_target="tpu_custom_call" | custom-call | tf_op jit(solution)/shard_map/pallas_call | solution.py:127
  114.9 6.4 %copy.33 = f32[31,16,1024]{2,0,1:T(8,128)} copy(f32[31,16,1024]{0,2,1:T(8,128)} %bitcast.41) | data formatting | bytes 4063232 | tf_op jit(solution)/shard_map/reshape | solution.py:189
  121.3 2.0 %reduce-precision_convert_fusion.1 = (bf16[31,4096]{1,0:T(8,128)(2,1)S(1)}, bf16[31,4096]{1,0:T(8,128)(2,1)S(1)}, f32[31,4096]{1,0:T(8,128)}, bf16[31,4096]{1,0:T(8,128)(2,1)S(1)}) fusion(f32[31,4096]{1,0:T(8,128)} %reduce-scatter.2.cloned.1.call-done, pred[4096]{0:T(1024)(128)(4,1)S(1)} %get-tuple-element.44), kind=kLoop, calls=%fused_computation.57 | loop fusion | flops 1015808 | bytes 1781760 | tf_op jit(solution)/shard_map/convert.2
  123.2 3.6 %fusion = f32[93,1024]{1,0:T(8,128)S(1)} fusion(s32[4096]{0:T(1024)S(1)} %get-tuple-element.48, bf16[31,4096]{1,0:T(8,128)(2,1)S(1)} %get-tuple-element.39, bf16[31,4096]{1,0:T(8,128)(2,1)S(1)} %get-tuple-element.41, bf16[31,4096]{1,0:T(8,128)(2,1)S(1)} %get-tuple-element.38), kind=kOutput, calls=%fused_computation.3 | convolution fusion | flops 786620416 | bytes 1159168 | tf_op jit(solution)/shard_map/dot_general | solution.py:69
  126.9 2.2 %collective-permute-start.5 = (f32[31,1024]{1,0:T(8,128)S(1)}, f32[31,1024]{1,0:T(8,128)S(1)}, u32[]{:S(2)}, u32[]{:S(2)}) collective-permute-start(f32[31,1024]{1,0:T(8,128)S(1)} %slice_add_fusion.2), channel_id=1, source_target_pairs={{0,1},{1,2},{2,3},{3,4},{4,5},{5,6},{6,7},{8,9},{9,10},{10,11},{11... | collective-permute-start | bytes 380936 | tf_op jit(solution)/shard_map/ppermute | solution.py:31
  129.1 3.6 %fusion.1 = f32[93,1024]{1,0:T(8,128)S(1)} fusion(s32[4096]{0:T(1024)S(1)} %get-tuple-element.47, bf16[31,4096]{1,0:T(8,128)(2,1)S(1)} %get-tuple-element.39, bf16[31,4096]{1,0:T(8,128)(2,1)S(1)} %get-tuple-element.41, bf16[31,4096]{1,0:T(8,128)(2,1)S(1)} %get-tuple-element.38), kind=kOutput, calls=%fused_computation.4 | convolution fusion | flops 786620416 | bytes 1159168 | tf_op jit(solution)/shard_map/dot_general | solution.py:69
  132.7 2.2 %collective-permute-start.6 = (f32[31,1024]{1,0:T(8,128)S(1)}, f32[31,1024]{1,0:T(8,128)S(1)}, u32[]{:S(2)}, u32[]{:S(2)}) collective-permute-start(f32[31,1024]{1,0:T(8,128)S(1)} %slice_add_fusion), channel_id=1, source_target_pairs={{1,0},{2,1},{3,2},{4,3},{5,4},{6,5},{7,6},{9,8},{10,9},{11,10},{12... | collective-permute-start | bytes 380936 | tf_op jit(solution)/shard_map/ppermute | solution.py:31
  135.6 2.5 %copy.34 = f32[31,16,1024]{2,1,0:T(8,128)} copy(f32[31,16,1024]{2,0,1:T(8,128)S(1)} %fusion.11) | data formatting | bytes 4063232
  138.1 1.8 %collective-permute-done.6 = f32[31,1024]{1,0:T(8,128)S(1)} collective-permute-done((f32[31,1024]{1,0:T(8,128)S(1)}, f32[31,1024]{1,0:T(8,128)S(1)}, u32[]{:S(2)}, u32[]{:S(2)}) %collective-permute-start.6) | collective-permute-done | bytes 127008 | tf_op jit(solution)/shard_map/ppermute | solution.py:31
  (75 shorter events, 19.3 us)
Async XLA Ops:
  7.2 52.2 %all-gather.2.cloned.1.call-start = ((), (), s32[]{:S(2)}) async-start(), calls=%async_computation.1 | async-start | bytes 2621440 | tf_op jit(solution)/shard_map/all_gather | solution.py:160
  7.2 15.6 %collective-permute-start.2 = (s32[4096]{0:T(1024)}, s32[4096]{0:T(1024)S(1)}, u32[]{:S(2)}, u32[]{:S(2)}) collective-permute-start(s32[4096]{0:T(1024)} %param.14), channel_id=1, source_target_pairs={{0,8},{8,16},{16,24},{24,0},{1,9},{9,17},{17,25},{25,1},{2,10},{10... | collective-permute-start | bytes 49160 | tf_op jit(solution)/shard_map/ppermute | solution.py:138
  8.6 14.3 %collective-permute-start.3 = (s32[4096]{0:T(1024)}, s32[4096]{0:T(1024)S(1)}, u32[]{:S(2)}, u32[]{:S(2)}) collective-permute-start(s32[4096]{0:T(1024)} %param.14), channel_id=1, source_target_pairs={{0,16},{8,24},{16,0},{24,8},{1,17},{9,25},{17,1},{25,9},{2,18},{10... | collective-permute-start | bytes 49160 | tf_op jit(solution)/shard_map/ppermute | solution.py:138
  10.9 12.0 %collective-permute-start.4 = (s32[4096]{0:T(1024)}, s32[4096]{0:T(1024)S(1)}, u32[]{:S(2)}, u32[]{:S(2)}) collective-permute-start(s32[4096]{0:T(1024)} %param.14), channel_id=1, source_target_pairs={{0,24},{8,0},{16,8},{24,16},{1,25},{9,1},{17,9},{25,17},{2,26},{10... | collective-permute-start | bytes 49160 | tf_op jit(solution)/shard_map/ppermute | solution.py:138
  14.6 106.7 %reduce-scatter.2.cloned.1.call-start = ((), (), s32[]{:S(2)}) async-start(), calls=%async_computation.2 | async-start | bytes 2621440 | tf_op jit(solution)/shard_map/reduce_scatter | solution.py:183
  16.5 1.2 copy-start.2
  18.0 4.8 %copy-start.4 = (s32[4096]{0:T(1024)S(1)}, s32[4096]{0:T(1024)}, u32[]{:S(2)}) copy-start(s32[4096]{0:T(1024)} %param.14) | copy-start | bytes 49156
  59.0 2.7 %copy-start.5 = (f32[30]{0:T(128)S(1)}, f32[30]{0:T(128)}, u32[]{:S(2)}) copy-start(f32[30]{0:T(128)} %param.18) | copy-start | bytes 364
  59.0 2.7 %copy-start.6 = (f32[30]{0:T(128)S(1)}, f32[30]{0:T(128)}, u32[]{:S(2)}) copy-start(f32[30]{0:T(128)} %param.17) | copy-start | bytes 364
  59.4 2.2 %copy-start = (f32[32,16384]{1,0:T(8,128)S(1)}, f32[32,16384]{1,0:T(8,128)}, u32[]{:S(2)}) copy-start(f32[32,16384]{1,0:T(8,128)} %all-gather.2.cloned.1.call-done) | copy-start | bytes 6291460
  68.1 1.2 copy-start.7
  75.5 6.8 %copy-start.3 = (s32[4096]{0:T(1024)S(1)}, s32[4096]{0:T(1024)}, u32[]{:S(2)}) copy-start(s32[4096]{0:T(1024)} %param.16) | copy-start | bytes 49156
  75.6 59.2 %collective-permute-start = (f32[31,1,1024]{2,0,1:T(8,128)S(1)}, f32[31,1,1024]{2,0,1:T(8,128)S(1)}, u32[]{:S(2)}, u32[]{:S(2)}) collective-permute-start(f32[31,1,1024]{2,0,1:T(8,128)S(1)} %get-tuple-element.35), channel_id=1, source_target_pairs={{1,0},{2,1},{3,2},{4,3},{5,4},{6,5},{7,6},{9,8},{10,9},{11,10},{12... | collective-permute-start | bytes 380936 | tf_op jit(solution)/shard_map/ppermute | solution.py:23
  78.8 56.1 %collective-permute-start.1 = (f32[31,1,1024]{2,0,1:T(8,128)S(1)}, f32[31,1,1024]{2,0,1:T(8,128)S(1)}, u32[]{:S(2)}, u32[]{:S(2)}) collective-permute-start(f32[31,1,1024]{2,0,1:T(8,128)S(1)} %get-tuple-element.34), channel_id=1, source_target_pairs={{0,1},{1,2},{2,3},{3,4},{4,5},{5,6},{6,7},{8,9},{9,10},{10,11},{11... | collective-permute-start | bytes 380936 | tf_op jit(solution)/shard_map/ppermute | solution.py:20
  126.9 11.2 %collective-permute-start.5 = (f32[31,1024]{1,0:T(8,128)S(1)}, f32[31,1024]{1,0:T(8,128)S(1)}, u32[]{:S(2)}, u32[]{:S(2)}) collective-permute-start(f32[31,1024]{1,0:T(8,128)S(1)} %slice_add_fusion.2), channel_id=1, source_target_pairs={{0,1},{1,2},{2,3},{3,4},{4,5},{5,6},{6,7},{8,9},{9,10},{10,11},{11... | collective-permute-start | bytes 380936 | tf_op jit(solution)/shard_map/ppermute | solution.py:31
  129.1 5.8 %copy-start.1 = (f32[31,16,1024]{2,0,1:T(8,128)S(1)}, f32[31,16,1024]{2,0,1:T(8,128)}, u32[]{:S(2)}) copy-start(f32[31,16,1024]{2,0,1:T(8,128)} %copy.33) | copy-start | bytes 6094852
  132.7 7.2 %collective-permute-start.6 = (f32[31,1024]{1,0:T(8,128)S(1)}, f32[31,1024]{1,0:T(8,128)S(1)}, u32[]{:S(2)}, u32[]{:S(2)}) collective-permute-start(f32[31,1024]{1,0:T(8,128)S(1)} %slice_add_fusion), channel_id=1, source_target_pairs={{1,0},{2,1},{3,2},{4,3},{5,4},{6,5},{7,6},{9,8},{10,9},{11,10},{12... | collective-permute-start | bytes 380936 | tf_op jit(solution)/shard_map/ppermute | solution.py:31
Sparse Core Ops, SparseCore 0:
  14.7 44.6 all-gather.1
  72.9 42.1 reduce-scatter.1

commit v7 on v6

--- a/solution.py
+++ b/solution.py
@@ -72,8 +72,6 @@
 
 
 def _gather_kernel(count_ref, dst_ref, src_ref, table_ref, out_ref):
-    out_ref[...] = jnp.zeros(out_ref.shape, out_ref.dtype)
-
     def step(i, carry):
         base = i * UNROLL
         for j in range(UNROLL):
@@ -83,20 +81,27 @@
     lax.fori_loop(0, (count_ref[0] + UNROLL - 1) // UNROLL, step, 0)
 
 
-def _scatter_kernel(count_ref, src_ref, seg_ref, rows_ref, out_ref, even_ref, odd_ref):
-    even_ref[...] = jnp.zeros(even_ref.shape, even_ref.dtype)
+def _scatter_kernel(count_ref, src_ref, seg_ref, rows_ref, out_ref, odd_ref):
+    out_ref[...] = jnp.zeros(out_ref.shape, out_ref.dtype)
     odd_ref[...] = jnp.zeros(odd_ref.shape, odd_ref.dtype)
+
+    def add_row(acc, k):
+        acc[pl.ds(seg_ref[k], 1), :] += rows_ref[pl.ds(src_ref[k], 1), :]
 
     def step(i, carry):
         base = i * UNROLL
         for j in range(UNROLL):
-            acc = even_ref if j % 2 == 0 else odd_ref
-            acc[pl.ds(seg_ref[base + j], 1), :] += rows_ref[pl.ds(src_ref[base + j], 1), :]
+            add_row(out_ref if j % 2 == 0 else odd_ref, base + j)
         return carry
 
-    lax.fori_loop(0, (count_ref[0] + UNROLL - 1) // UNROLL, step, 0)
-    rows = out_ref.shape[0]
-    out_ref[...] = even_ref[pl.ds(0, rows), :] + odd_ref[pl.ds(0, rows), :]
+    def rest(k, carry):
+        add_row(out_ref, k)
+        return carry
+
+    full = count_ref[0] // UNROLL
+    lax.fori_loop(0, full, step, 0)
+    lax.fori_loop(full * UNROLL, count_ref[0], rest, 0)
+    out_ref[...] += odd_ref[...]
 
 
 def row_gather(count, order, local, table):
@@ -122,7 +127,7 @@
         grid=(1,),
         in_specs=[pl.BlockSpec((n_rows, width), lambda i, *_: (0, 0))],
         out_specs=pl.BlockSpec((n_cells, width), lambda i, *_: (0, 0)),
-        scratch_shapes=[pltpu.VMEM((n_cells + UNROLL, width), jnp.float32)] * 2,
+        scratch_shapes=[pltpu.VMEM((n_cells, width), jnp.float32)],
     )
     return pl.pallas_call(
         _scatter_kernel,

time: 149 us -> 149 us (level)
  no operation moved by 1% of the time
where the time goes in v7:
time: 149 us; the launch traced here: 148 us
  Pallas kernels  39.8 us (27%)
  other arithmetic  34.5 us (23%)
  local copies, waits for them, and re-layouts  33.4 us (22%)
  starting transfers between devices  15.8 us (11%)
  between operations  14.4 us (10%)
  matrix products  7.2 us (5%)
  waiting for transfers between devices  2.27 us (2%)
    pallas_call x1, Pallas kernels, row_scatter_add(): pl.pallas_call(_scatter_kernel, grid_spec=spec, out_shape=jax.ShapeDtypeS...  22.2 us
    pallas_call x1, Pallas kernels, row_gather(): pl.pallas_call(_gather_kernel, grid_spec=spec, out_shape=jax.ShapeDtypeSt...  17.7 us
    unnamed x22, local copies, waits for them, and re-layouts  8.58 us
    sort x1, other arithmetic, body(): lax.sort((keys, position, local_cell, seg), num_keys=1)  8.29 us
    dot_general x2, matrix products, pack_slots(): out = jnp.dot(parts, onehot, preferred_element_type=jnp.float32)  7.2 us
    pallas_call x1, local copies, waits for them, and re-layouts, row_gather(): pl.pallas_call(_gather_kernel, grid_spec=spec, out_shape=jax.ShapeDtypeSt...  6.37 us
    transpose x1, local copies, waits for them, and re-layouts, body(): summed = row_scatter_add(count, order, seg_sorted, terms_all.T, n_cells)  6.35 us
    reshape x1, local copies, waits for them, and re-layouts, body(): source = summed.T.reshape(fields, width_x, width_yz)  6.35 us
  transfers between devices with their start and end apart: 9, of which 2 were waited for; matrix products, arithmetic and copies ran while one was open for 41% of the time, Pallas kernels for 27%

profile of v7, /device:TPU:3, one launch (start us, length us, event | category | flops | bytes accessed | tf_op | source)
XLA Modules:
  0.0 147.5 jit_solution(1150202345165845301)
XLA Ops:
  8.6 2.3 %collective-permute-start.3 = (s32[4096]{0:T(1024)}, s32[4096]{0:T(1024)S(1)}, u32[]{:S(2)}, u32[]{:S(2)}) collective-permute-start(s32[4096]{0:T(1024)} %param.14), channel_id=1, source_target_pairs={{0,16},{8,24},{16,0},{24,8},{1,17},{9,25},{17,1},{25,9},{2,18},{10... | collective-permute-start | bytes 49160 | tf_op jit(solution)/shard_map/ppermute | solution.py:143
  12.7 1.9 %pad_maximum_fusion.7 = f32[32,4096]{1,0:T(8,128)} fusion(f32[1,4096]{1,0:T(1,128)S(1)} %bitcast.57, f32[1,4096]{1,0:T(1,128)} %bitcast.58, f32[30,4096]{1,0:T(8,128)} %param.12), kind=kLoop, calls=%fused_computation.59 | loop fusion | flops 262144 | bytes 1048576 | tf_op jit(solution)/shard_map/concatenate | solution.py:162
  14.7 1.8 %pad.33 = f32[32,16,1024]{2,1,0:T(8,128)S(1)} pad(f32[30,16,1024]{2,1,0:T(8,128)} %param.10, f32[]{:T(128)} %constant.118.clone.1), padding=0_2x0_0x0_0 | pad | bytes 4063236
  18.0 4.8 %copy.30 = f32[31,16384]{0,1:T(8,128)} copy(f32[31,16384]{1,0:T(8,128)S(1)} %pad_maximum_fusion.5) | data formatting | bytes 4063232 | tf_op jit(solution)/shard_map/concatenate | solution.py:156
  24.6 8.3 %sort.27 = (s32[16384]{0:T(1024)}, s32[16384]{0:T(1024)}, s32[16384]{0:T(1024)}, s32[16384]{0:T(1024)}) sort(s32[16384]{0:T(1024)S(1)} %iota_add_fusion, s32[16384]{0:T(1024)S(1)} %iota.19, s32[16384]{0:T(1024)S(1)} %get-tuple-element.30, s32[16384]{0:T(1024)S(1)} %get-tuple-element.29), dimensions={0}, to_apply=%region_1.2 | sort | flops 229376 | bytes 524288 | tf_op jit(solution)/shard_map/sort | solution.py:175
  32.9 17.7 %shard_map.121 = f32[16384,31]{1,0:T(8,128)} custom-call(s32[1]{0:T(128)} %bitcast.6.count_ref, s32[16384]{0:T(1024)} %get-tuple-element.6.dst_ref.src_ref, s32[16384]{0:T(1024)} %get-tuple-element.8.src_ref, f32[16384,31]{1,0:T(8,128)} %bitcast.40), custom_call_target="tpu_custom_call" | custom-call | tf_op jit(solution)/shard_map/pallas_call | solution.py:116
  50.6 6.4 %copy.31 = f32[16384,31]{0,1:T(8,128)} copy(f32[16384,31]{1,0:T(8,128)} %shard_map.121) | data formatting | bytes 4063232 | tf_op jit(solution)/shard_map/pallas_call | solution.py:116
  56.9 1.8 %select_bitcast_fusion = f32[31,16384]{1,0:T(8,128)S(1)} fusion(f32[16384,31]{0,1:T(8,128)} %copy.31, pred[16384]{0:T(1024)(128)(4,1)S(1)} %get-tuple-element.31), kind=kLoop, calls=%fused_computation.36 | loop fusion | flops 507904 | bytes 4079616 | tf_op jit(solution)/shard_map/jit(_where)/select_n | solution.py:180
  59.4 2.0 %slice_reduce_fusion = f32[16384]{0:T(1024)S(1)} fusion(f32[32,16384]{1,0:T(8,128)} %all-gather.2.cloned.1.call-done), kind=kLoop, calls=%fused_computation.49 | loop fusion | flops 475136 | bytes 2031616 | tf_op jit(solution)/shard_map/reduce_sum | solution.py:35
  69.3 1.6 %multiply_reduce_fusion = (f32[16384]{0:T(1024)S(1)}, f32[30,16384]{1,0:T(8,128)}) fusion(f32[30,16384]{1,0:T(8,128)S(1)} %get-tuple-element.28, f32[30]{0:T(128)S(1)} %copy-done.7), kind=kLoop, calls=%fused_computation.27 | loop fusion | flops 1458176 | bytes 3997816 | tf_op jit(solution)/shard_map/reduce_sum | solution.py:53
  71.2 1.6 %maximum_select_fusion = f32[31,16384]{1,0:T(8,128)} fusion(f32[1,16384]{1,0:T(1,128)S(1)} %get-tuple-element.32, f32[30,16384]{1,0:T(8,128)S(1)} %get-tuple-element.27, pred[16384]{0:T(1024)(128)(4,1)S(1)} %get-tuple-element.31), kind=kLoop, calls=%fused_computation.26 | loop fusion | flops 1015808 | bytes 4079616 | tf_op jit(solution)/shard_map/jit(_where)/select_n | solution.py:187
  72.8 2.7 %copy.28 = f32[30,16,1024]{2,0,1:T(8,128)S(1)} copy(f32[30,16,1024]{2,1,0:T(8,128)} %param.10) | data formatting | bytes 3932160 | tf_op args[0]
  75.6 2.8 %collective-permute-start = (f32[31,1,1024]{2,0,1:T(8,128)S(1)}, f32[31,1,1024]{2,0,1:T(8,128)S(1)}, u32[]{:S(2)}, u32[]{:S(2)}) collective-permute-start(f32[31,1,1024]{2,0,1:T(8,128)S(1)} %get-tuple-element.35), channel_id=1, source_target_pairs={{1,0},{2,1},{3,2},{4,3},{5,4},{6,5},{7,6},{9,8},{10,9},{11,10},{12... | collective-permute-start | bytes 380936 | tf_op jit(solution)/shard_map/ppermute | solution.py:23
  78.5 3.8 %collective-permute-start.1 = (f32[31,1,1024]{2,0,1:T(8,128)S(1)}, f32[31,1,1024]{2,0,1:T(8,128)S(1)}, u32[]{:S(2)}, u32[]{:S(2)}) collective-permute-start(f32[31,1,1024]{2,0,1:T(8,128)S(1)} %get-tuple-element.34), channel_id=1, source_target_pairs={{0,1},{1,2},{2,3},{3,4},{4,5},{5,6},{6,7},{8,9},{9,10},{10,11},{11... | collective-permute-start | bytes 380936 | tf_op jit(solution)/shard_map/ppermute | solution.py:20
  83.5 3.2 %maximum_bitcast_fusion = f32[16384,31]{0,1:T(8,128)} fusion(f32[1,16384]{1,0:T(1,128)S(1)} %get-tuple-element.33, f32[30,16384]{1,0:T(8,128)} %get-tuple-element.37), kind=kLoop, calls=%fused_computation.25 | loop fusion | flops 507904 | bytes 4063232 | tf_op jit(solution)/shard_map/transpose | solution.py:193
  86.7 6.4 %copy.32.rows_ref = f32[16384,31]{1,0:T(8,128)} copy(f32[16384,31]{0,1:T(8,128)} %maximum_bitcast_fusion) | data formatting | bytes 4063232 | tf_op jit(solution)/shard_map/transpose | solution.py:193
  93.1 22.2 %shard_map.122 = f32[16384,31]{1,0:T(8,128)} custom-call(s32[1]{0:T(128)} %bitcast.6.count_ref, s32[16384]{0:T(1024)} %get-tuple-element.6.dst_ref.src_ref, s32[16384]{0:T(1024)} %get-tuple-element.7.seg_ref, f32[16384,31]{1,0:T(8,128)} %copy.32.rows_ref), custom_call_target="tpu_custom_call" | custom-call | tf_op jit(solution)/shard_map/pallas_call | solution.py:132
  115.2 6.4 %copy.33 = f32[31,16,1024]{2,0,1:T(8,128)} copy(f32[31,16,1024]{0,2,1:T(8,128)} %bitcast.41) | data formatting | bytes 4063232 | tf_op jit(solution)/shard_map/reshape | solution.py:194
  121.6 2.0 %reduce-precision_convert_fusion.1 = (bf16[31,4096]{1,0:T(8,128)(2,1)S(1)}, bf16[31,4096]{1,0:T(8,128)(2,1)S(1)}, f32[31,4096]{1,0:T(8,128)}, bf16[31,4096]{1,0:T(8,128)(2,1)S(1)}) fusion(f32[31,4096]{1,0:T(8,128)} %reduce-scatter.2.cloned.1.call-done, pred[4096]{0:T(1024)(128)(4,1)S(1)} %get-tuple-element.44), kind=kLoop, calls=%fused_computation.57 | loop fusion | flops 1015808 | bytes 1781760 | tf_op jit(solution)/shard_map/convert.2
  123.6 3.6 %fusion = f32[93,1024]{1,0:T(8,128)S(1)} fusion(s32[4096]{0:T(1024)S(1)} %get-tuple-element.48, bf16[31,4096]{1,0:T(8,128)(2,1)S(1)} %get-tuple-element.39, bf16[31,4096]{1,0:T(8,128)(2,1)S(1)} %get-tuple-element.41, bf16[31,4096]{1,0:T(8,128)(2,1)S(1)} %get-tuple-element.38), kind=kOutput, calls=%fused_computation.3 | convolution fusion | flops 786620416 | bytes 1159168 | tf_op jit(solution)/shard_map/dot_general | solution.py:69
  127.2 1.9 %collective-permute-start.5 = (f32[31,1024]{1,0:T(8,128)S(1)}, f32[31,1024]{1,0:T(8,128)S(1)}, u32[]{:S(2)}, u32[]{:S(2)}) collective-permute-start(f32[31,1024]{1,0:T(8,128)S(1)} %slice_add_fusion.2), channel_id=1, source_target_pairs={{0,1},{1,2},{2,3},{3,4},{4,5},{5,6},{6,7},{8,9},{9,10},{10,11},{11... | collective-permute-start | bytes 380936 | tf_op jit(solution)/shard_map/ppermute | solution.py:31
  129.2 3.6 %fusion.1 = f32[93,1024]{1,0:T(8,128)S(1)} fusion(s32[4096]{0:T(1024)S(1)} %get-tuple-element.47, bf16[31,4096]{1,0:T(8,128)(2,1)S(1)} %get-tuple-element.39, bf16[31,4096]{1,0:T(8,128)(2,1)S(1)} %get-tuple-element.41, bf16[31,4096]{1,0:T(8,128)(2,1)S(1)} %get-tuple-element.38), kind=kOutput, calls=%fused_computation.4 | convolution fusion | flops 786620416 | bytes 1159168 | tf_op jit(solution)/shard_map/dot_general | solution.py:69
  132.8 2.4 %collective-permute-start.6 = (f32[31,1024]{1,0:T(8,128)S(1)}, f32[31,1024]{1,0:T(8,128)S(1)}, u32[]{:S(2)}, u32[]{:S(2)}) collective-permute-start(f32[31,1024]{1,0:T(8,128)S(1)} %slice_add_fusion), channel_id=1, source_target_pairs={{1,0},{2,1},{3,2},{4,3},{5,4},{6,5},{7,6},{9,8},{10,9},{11,10},{12... | collective-permute-start | bytes 380936 | tf_op jit(solution)/shard_map/ppermute | solution.py:31
  136.0 2.5 %copy.34 = f32[31,16,1024]{2,1,0:T(8,128)} copy(f32[31,16,1024]{2,0,1:T(8,128)S(1)} %fusion.11) | data formatting | bytes 4063232
  (75 shorter events, 19.6 us)
Async XLA Ops:
  7.2 52.2 %all-gather.2.cloned.1.call-start = ((), (), s32[]{:S(2)}) async-start(), calls=%async_computation.1 | async-start | bytes 2621440 | tf_op jit(solution)/shard_map/all_gather | solution.py:165
  7.2 15.6 %collective-permute-start.2 = (s32[4096]{0:T(1024)}, s32[4096]{0:T(1024)S(1)}, u32[]{:S(2)}, u32[]{:S(2)}) collective-permute-start(s32[4096]{0:T(1024)} %param.14), channel_id=1, source_target_pairs={{0,8},{8,16},{16,24},{24,0},{1,9},{9,17},{17,25},{25,1},{2,10},{10... | collective-permute-start | bytes 49160 | tf_op jit(solution)/shard_map/ppermute | solution.py:143
  8.6 14.3 %collective-permute-start.3 = (s32[4096]{0:T(1024)}, s32[4096]{0:T(1024)S(1)}, u32[]{:S(2)}, u32[]{:S(2)}) collective-permute-start(s32[4096]{0:T(1024)} %param.14), channel_id=1, source_target_pairs={{0,16},{8,24},{16,0},{24,8},{1,17},{9,25},{17,1},{25,9},{2,18},{10... | collective-permute-start | bytes 49160 | tf_op jit(solution)/shard_map/ppermute | solution.py:143
  10.9 12.0 %collective-permute-start.4 = (s32[4096]{0:T(1024)}, s32[4096]{0:T(1024)S(1)}, u32[]{:S(2)}, u32[]{:S(2)}) collective-permute-start(s32[4096]{0:T(1024)} %param.14), channel_id=1, source_target_pairs={{0,24},{8,0},{16,8},{24,16},{1,25},{9,1},{17,9},{25,17},{2,26},{10... | collective-permute-start | bytes 49160 | tf_op jit(solution)/shard_map/ppermute | solution.py:143
  14.6 107.0 %reduce-scatter.2.cloned.1.call-start = ((), (), s32[]{:S(2)}) async-start(), calls=%async_computation.2 | async-start | bytes 2621440 | tf_op jit(solution)/shard_map/reduce_scatter | solution.py:188
  16.5 1.2 copy-start.2
  18.0 4.8 %copy-start.4 = (s32[4096]{0:T(1024)S(1)}, s32[4096]{0:T(1024)}, u32[]{:S(2)}) copy-start(s32[4096]{0:T(1024)} %param.14) | copy-start | bytes 49156
  58.7 3.0 %copy-start.5 = (f32[30]{0:T(128)S(1)}, f32[30]{0:T(128)}, u32[]{:S(2)}) copy-start(f32[30]{0:T(128)} %param.18) | copy-start | bytes 364
  58.7 3.0 %copy-start.6 = (f32[30]{0:T(128)S(1)}, f32[30]{0:T(128)}, u32[]{:S(2)}) copy-start(f32[30]{0:T(128)} %param.17) | copy-start | bytes 364
  59.4 2.2 %copy-start = (f32[32,16384]{1,0:T(8,128)S(1)}, f32[32,16384]{1,0:T(8,128)}, u32[]{:S(2)}) copy-start(f32[32,16384]{1,0:T(8,128)} %all-gather.2.cloned.1.call-done) | copy-start | bytes 6291460
  68.1 1.2 copy-start.7
  75.5 6.8 %copy-start.3 = (s32[4096]{0:T(1024)S(1)}, s32[4096]{0:T(1024)}, u32[]{:S(2)}) copy-start(s32[4096]{0:T(1024)} %param.16) | copy-start | bytes 49156
  75.6 59.6 %collective-permute-start = (f32[31,1,1024]{2,0,1:T(8,128)S(1)}, f32[31,1,1024]{2,0,1:T(8,128)S(1)}, u32[]{:S(2)}, u32[]{:S(2)}) collective-permute-start(f32[31,1,1024]{2,0,1:T(8,128)S(1)} %get-tuple-element.35), channel_id=1, source_target_pairs={{1,0},{2,1},{3,2},{4,3},{5,4},{6,5},{7,6},{9,8},{10,9},{11,10},{12... | collective-permute-start | bytes 380936 | tf_op jit(solution)/shard_map/ppermute | solution.py:23
  78.5 56.7 %collective-permute-start.1 = (f32[31,1,1024]{2,0,1:T(8,128)S(1)}, f32[31,1,1024]{2,0,1:T(8,128)S(1)}, u32[]{:S(2)}, u32[]{:S(2)}) collective-permute-start(f32[31,1,1024]{2,0,1:T(8,128)S(1)} %get-tuple-element.34), channel_id=1, source_target_pairs={{0,1},{1,2},{2,3},{3,4},{4,5},{5,6},{6,7},{8,9},{9,10},{10,11},{11... | collective-permute-start | bytes 380936 | tf_op jit(solution)/shard_map/ppermute | solution.py:20
  127.2 11.2 %collective-permute-start.5 = (f32[31,1024]{1,0:T(8,128)S(1)}, f32[31,1024]{1,0:T(8,128)S(1)}, u32[]{:S(2)}, u32[]{:S(2)}) collective-permute-start(f32[31,1024]{1,0:T(8,128)S(1)} %slice_add_fusion.2), channel_id=1, source_target_pairs={{0,1},{1,2},{2,3},{3,4},{4,5},{5,6},{6,7},{8,9},{9,10},{10,11},{11... | collective-permute-start | bytes 380936 | tf_op jit(solution)/shard_map/ppermute | solution.py:31
  129.1 6.1 %copy-start.1 = (f32[31,16,1024]{2,0,1:T(8,128)S(1)}, f32[31,16,1024]{2,0,1:T(8,128)}, u32[]{:S(2)}) copy-start(f32[31,16,1024]{2,0,1:T(8,128)} %copy.33) | copy-start | bytes 6094852
  132.8 7.2 %collective-permute-start.6 = (f32[31,1024]{1,0:T(8,128)S(1)}, f32[31,1024]{1,0:T(8,128)S(1)}, u32[]{:S(2)}, u32[]{:S(2)}) collective-permute-start(f32[31,1024]{1,0:T(8,128)S(1)} %slice_add_fusion), channel_id=1, source_target_pairs={{1,0},{2,1},{3,2},{4,3},{5,4},{6,5},{7,6},{9,8},{10,9},{11,10},{12... | collective-permute-start | bytes 380936 | tf_op jit(solution)/shard_map/ppermute | solution.py:31
Sparse Core Ops, SparseCore 0:
  14.7 44.6 all-gather.1
  72.9 42.1 reduce-scatter.1

commit v8 on v7

--- a/solution.py
+++ b/solution.py
@@ -152,6 +152,10 @@
     return with_layout_constraint(x, Layout(major_to_minor=(0, 1)))
 
 
+def plane_major(x):
+    return with_layout_constraint(x, Layout(major_to_minor=(0, 1, 2)))
+
+
 def body(vapor, gas_temp, masses, drop_temp, cells, flags, moves, volat_a, volat_b, latent):
     gas_block = jnp.concatenate([vapor, gas_temp[None]], axis=0)
     fields, width_x, width_yz = gas_block.shape
@@ -189,10 +193,12 @@
     padded = with_halo(gas_block, (("slab", 1),), 1)
     down = padded[:, :-2]
     upper = padded[:, 2:]
-    flowed = gas_block + 0.2 * (upper - 2.0 * gas_block + down) - 0.3 * (gas_block - down)
+    flowed = plane_major(
+        gas_block + 0.2 * (upper - 2.0 * gas_block + down) - 0.3 * (gas_block - down)
+    )
     summed = row_scatter_add(count, order, seg_sorted, terms_all.T, n_cells)
-    source = summed.T.reshape(fields, width_x, width_yz)
-    gas_next = flowed + source
+    source = plane_major(summed.T.reshape(fields, width_x, width_yz))
+    gas_next = plane_major(flowed + source)
     kept = jnp.where(moves[None] == 0, state, 0.0)
     from_prev = shifted(pack_slots(state, moves == 2), "slab", 1)
     from_next = shifted(pack_slots(state, moves == 1), "slab", -1)

time: 149 us -> 147 us (0.987)
  local copies, waits for them, and re-layouts: 33.4 us -> 29.7 us
  other arithmetic: 34.5 us -> 36.4 us
    unnamed x22, local copies, waits for them, and re-layouts: 8.58 us -> 4.83 us
    add x1, other arithmetic: 0.71 us -> 2.38 us  [body(): gas_next = plane_major(flowed + source)]
  transfers between devices with their start and end apart: 9 -> 9, of which waited for: 2 -> 2; matrix products, arithmetic and copies ran while one was open for 41% -> 39% of each run, Pallas kernels for 27% -> 27%
where the time goes in v8:
time: 147 us
  Pallas kernels  39.4 us (27%)
  other arithmetic  36.4 us (25%)
  local copies, waits for them, and re-layouts  29.7 us (20%)
  starting transfers between devices  15.8 us (11%)
  between operations  14.4 us (10%)
  matrix products  7.2 us (5%)
  waiting for transfers between devices  3.62 us (2%)
    pallas_call x1, Pallas kernels, row_scatter_add(): pl.pallas_call(_scatter_kernel, grid_spec=spec, out_shape=jax.ShapeDtypeS...  21.9 us
    pallas_call x1, Pallas kernels, row_gather(): pl.pallas_call(_gather_kernel, grid_spec=spec, out_shape=jax.ShapeDtypeSt...  17.5 us
    sort x1, other arithmetic, body(): lax.sort((keys, position, local_cell, seg), num_keys=1)  8.29 us
    dot_general x2, matrix products, pack_slots(): out = jnp.dot(parts, onehot, preferred_element_type=jnp.float32)  7.2 us
    reshape x1, local copies, waits for them, and re-layouts, body(): source = plane_major(summed.T.reshape(fields, width_x, width_yz))  6.47 us
    pallas_call x1, local copies, waits for them, and re-layouts, row_gather(): pl.pallas_call(_gather_kernel, grid_spec=spec, out_shape=jax.ShapeDtypeSt...  6.37 us
    transpose x1, local copies, waits for them, and re-layouts, body(): summed = row_scatter_add(count, order, seg_sorted, terms_all.T, n_cells)  6.3 us
    reduce_sum x4, other arithmetic, parcel_update(): slope = jnp.sum(frac * excess * excess / (denom * denom), axis=0) + 0.1  6.15 us
  transfers between devices with their start and end apart: 9, of which 2 were waited for; matrix products, arithmetic and copies ran while one was open for 39% of the time, Pallas kernels for 27%

profile of v8, /device:TPU:3, one launch (start us, length us, event | category | flops | bytes accessed | tf_op | source)
XLA Modules:
  0.0 146.5 jit_solution(9679147317956786181)
XLA Ops:
  8.6 2.3 %collective-permute-start.3 = (s32[4096]{0:T(1024)}, s32[4096]{0:T(1024)S(1)}, u32[]{:S(2)}, u32[]{:S(2)}) collective-permute-start(s32[4096]{0:T(1024)} %param.14), channel_id=1, source_target_pairs={{0,16},{8,24},{16,0},{24,8},{1,17},{9,25},{17,1},{25,9},{2,18},{10... | collective-permute-start | bytes 49160 | tf_op jit(solution)/shard_map/ppermute | solution.py:143
  12.7 1.9 %pad_maximum_fusion.7 = f32[32,4096]{1,0:T(8,128)} fusion(f32[1,4096]{1,0:T(1,128)S(1)} %bitcast.58, f32[1,4096]{1,0:T(1,128)} %bitcast.59, f32[30,4096]{1,0:T(8,128)} %param.12), kind=kLoop, calls=%fused_computation.59 | loop fusion | flops 262144 | bytes 1048576 | tf_op jit(solution)/shard_map/concatenate | solution.py:166
  14.7 1.7 %pad.33 = f32[32,16,1024]{2,1,0:T(8,128)S(1)} pad(f32[30,16,1024]{2,1,0:T(8,128)} %param.10, f32[]{:T(128)} %constant.118.clone.1), padding=0_2x0_0x0_0 | pad | bytes 4063236
  17.9 4.8 %copy.22 = f32[31,16384]{0,1:T(8,128)} copy(f32[31,16384]{1,0:T(8,128)S(1)} %pad_maximum_fusion.1) | data formatting | bytes 4063232 | tf_op jit(solution)/shard_map/concatenate | solution.py:160
  24.5 8.3 %sort.27 = (s32[16384]{0:T(1024)}, s32[16384]{0:T(1024)}, s32[16384]{0:T(1024)}, s32[16384]{0:T(1024)}) sort(s32[16384]{0:T(1024)S(1)} %iota_add_fusion, s32[16384]{0:T(1024)S(1)} %iota.19, s32[16384]{0:T(1024)S(1)} %get-tuple-element.24, s32[16384]{0:T(1024)S(1)} %get-tuple-element.23), dimensions={0}, to_apply=%region_1.2 | sort | flops 229376 | bytes 524288 | tf_op jit(solution)/shard_map/sort | solution.py:179
  32.8 17.5 %shard_map.121 = f32[16384,31]{1,0:T(8,128)} custom-call(s32[1]{0:T(128)} %bitcast.6.count_ref, s32[16384]{0:T(1024)} %get-tuple-element.6.dst_ref.src_ref, s32[16384]{0:T(1024)} %get-tuple-element.8.src_ref, f32[16384,31]{1,0:T(8,128)} %bitcast.40), custom_call_target="tpu_custom_call" | custom-call | tf_op jit(solution)/shard_map/pallas_call | solution.py:116
  50.3 6.4 %copy.23 = f32[16384,31]{0,1:T(8,128)} copy(f32[16384,31]{1,0:T(8,128)} %shard_map.121) | data formatting | bytes 4063232 | tf_op jit(solution)/shard_map/pallas_call | solution.py:116
  56.7 1.8 %select_bitcast_fusion = f32[31,16384]{1,0:T(8,128)S(1)} fusion(f32[16384,31]{0,1:T(8,128)} %copy.23, pred[16384]{0:T(1024)(128)(4,1)S(1)} %get-tuple-element.25), kind=kLoop, calls=%fused_computation.26 | loop fusion | flops 507904 | bytes 4079616 | tf_op jit(solution)/shard_map/jit(_where)/select_n | solution.py:184
  59.4 2.0 %slice_reduce_fusion = f32[16384]{0:T(1024)S(1)} fusion(f32[32,16384]{1,0:T(8,128)} %all-gather.2.cloned.1.call-done), kind=kLoop, calls=%fused_computation.51 | loop fusion | flops 475136 | bytes 2031616 | tf_op jit(solution)/shard_map/reduce_sum | solution.py:35
  69.3 1.6 %multiply_reduce_fusion = (f32[16384]{0:T(1024)S(1)}, f32[30,16384]{1,0:T(8,128)}) fusion(f32[30,16384]{1,0:T(8,128)S(1)} %get-tuple-element.22, f32[30]{0:T(128)S(1)} %copy-done.8), kind=kLoop, calls=%fused_computation.17 | loop fusion | flops 1458176 | bytes 3997816 | tf_op jit(solution)/shard_map/reduce_sum | solution.py:53
  71.2 1.6 %maximum_select_fusion = f32[31,16384]{1,0:T(8,128)} fusion(f32[1,16384]{1,0:T(1,128)S(1)} %get-tuple-element.26, f32[30,16384]{1,0:T(8,128)S(1)} %get-tuple-element.21, pred[16384]{0:T(1024)(128)(4,1)S(1)} %get-tuple-element.25), kind=kLoop, calls=%fused_computation.16 | loop fusion | flops 1015808 | bytes 4079616 | tf_op jit(solution)/shard_map/jit(_where)/select_n | solution.py:191
  74.6 2.7 %collective-permute-start = (f32[31,1,1024]{2,1,0:T(1,128)S(1)}, f32[31,1,1024]{2,1,0:T(1,128)S(1)}, u32[]{:S(2)}, u32[]{:S(2)}) collective-permute-start(f32[31,1,1024]{2,1,0:T(1,128)S(1)} %get-tuple-element.31), channel_id=1, source_target_pairs={{1,0},{2,1},{3,2},{4,3},{5,4},{6,5},{7,6},{9,8},{10,9},{11,10},{12... | collective-permute-start | bytes 380936 | tf_op jit(solution)/shard_map/ppermute | solution.py:23
  77.3 3.9 %collective-permute-start.1 = (f32[31,1,1024]{2,1,0:T(1,128)S(1)}, f32[31,1,1024]{2,1,0:T(1,128)S(1)}, u32[]{:S(2)}, u32[]{:S(2)}) collective-permute-start(f32[31,1,1024]{2,1,0:T(1,128)S(1)} %get-tuple-element.30), channel_id=1, source_target_pairs={{0,1},{1,2},{2,3},{3,4},{4,5},{5,6},{6,7},{8,9},{9,10},{10,11},{11... | collective-permute-start | bytes 380936 | tf_op jit(solution)/shard_map/ppermute | solution.py:20
  82.4 3.2 %maximum_bitcast_fusion = f32[16384,31]{0,1:T(8,128)} fusion(f32[1,16384]{1,0:T(1,128)S(1)} %get-tuple-element.27, f32[30,16384]{1,0:T(8,128)} %get-tuple-element.29), kind=kLoop, calls=%fused_computation.15 | loop fusion | flops 507904 | bytes 4063232 | tf_op jit(solution)/shard_map/transpose | solution.py:199
  85.6 6.3 %copy.24.rows_ref = f32[16384,31]{1,0:T(8,128)} copy(f32[16384,31]{0,1:T(8,128)} %maximum_bitcast_fusion) | data formatting | bytes 4063232 | tf_op jit(solution)/shard_map/transpose | solution.py:199
  91.9 21.9 %shard_map.122 = f32[16384,31]{1,0:T(8,128)} custom-call(s32[1]{0:T(128)} %bitcast.6.count_ref, s32[16384]{0:T(1024)} %get-tuple-element.6.dst_ref.src_ref, s32[16384]{0:T(1024)} %get-tuple-element.7.seg_ref, f32[16384,31]{1,0:T(8,128)} %copy.24.rows_ref), custom_call_target="tpu_custom_call" | custom-call | tf_op jit(solution)/shard_map/pallas_call | solution.py:132
  113.8 6.5 %copy.26 = f32[31,16,1024]{2,1,0:T(8,128)} copy(f32[31,16,1024]{0,2,1:T(8,128)} %bitcast.41) | data formatting | bytes 4063232 | tf_op jit(solution)/shard_map/reshape | solution.py:200
  120.3 2.0 %reduce-precision_convert_fusion.1 = (bf16[31,4096]{1,0:T(8,128)(2,1)S(1)}, bf16[31,4096]{1,0:T(8,128)(2,1)S(1)}, f32[31,4096]{1,0:T(8,128)}, bf16[31,4096]{1,0:T(8,128)(2,1)S(1)}) fusion(f32[31,4096]{1,0:T(8,128)} %reduce-scatter.2.cloned.1.call-done, pred[4096]{0:T(1024)(128)(4,1)S(1)} %get-tuple-element.38), kind=kLoop, calls=%fused_computation.57 | loop fusion | flops 1015808 | bytes 1781760 | tf_op jit(solution)/shard_map/convert.2
  122.2 3.6 %fusion = f32[93,1024]{1,0:T(8,128)S(1)} fusion(s32[4096]{0:T(1024)S(1)} %get-tuple-element.42, bf16[31,4096]{1,0:T(8,128)(2,1)S(1)} %get-tuple-element.33, bf16[31,4096]{1,0:T(8,128)(2,1)S(1)} %get-tuple-element.35, bf16[31,4096]{1,0:T(8,128)(2,1)S(1)} %get-tuple-element.32), kind=kOutput, calls=%fused_computation.3 | convolution fusion | flops 786620416 | bytes 1159168 | tf_op jit(solution)/shard_map/dot_general | solution.py:69
  125.9 2.2 %collective-permute-start.5 = (f32[31,1024]{1,0:T(8,128)S(1)}, f32[31,1024]{1,0:T(8,128)S(1)}, u32[]{:S(2)}, u32[]{:S(2)}) collective-permute-start(f32[31,1024]{1,0:T(8,128)S(1)} %slice_add_fusion.2), channel_id=1, source_target_pairs={{0,1},{1,2},{2,3},{3,4},{4,5},{5,6},{6,7},{8,9},{9,10},{10,11},{11... | collective-permute-start | bytes 380936 | tf_op jit(solution)/shard_map/ppermute | solution.py:31
  128.1 3.6 %fusion.1 = f32[93,1024]{1,0:T(8,128)S(1)} fusion(s32[4096]{0:T(1024)S(1)} %get-tuple-element.41, bf16[31,4096]{1,0:T(8,128)(2,1)S(1)} %get-tuple-element.33, bf16[31,4096]{1,0:T(8,128)(2,1)S(1)} %get-tuple-element.35, bf16[31,4096]{1,0:T(8,128)(2,1)S(1)} %get-tuple-element.32), kind=kOutput, calls=%fused_computation.4 | convolution fusion | flops 786620416 | bytes 1159168 | tf_op jit(solution)/shard_map/dot_general | solution.py:69
  131.8 2.1 %collective-permute-start.6 = (f32[31,1024]{1,0:T(8,128)S(1)}, f32[31,1024]{1,0:T(8,128)S(1)}, u32[]{:S(2)}, u32[]{:S(2)}) collective-permute-start(f32[31,1024]{1,0:T(8,128)S(1)} %slice_add_fusion), channel_id=1, source_target_pairs={{1,0},{2,1},{3,2},{4,3},{5,4},{6,5},{7,6},{9,8},{10,9},{11,10},{12... | collective-permute-start | bytes 380936 | tf_op jit(solution)/shard_map/ppermute | solution.py:31
  133.9 2.4 %fusion.15 = f32[31,16,1024]{2,1,0:T(8,128)} fusion(f32[31,16,1024]{2,1,0:T(8,128)S(1)} %copy-done.2, f32[31,1,1024]{2,1,0:T(1,128)S(1)} %collective-permute-done, f32[1,16,1024]{2,1,0:T(8,128)S(1)} %bitcast.52, f32[30,16,1024]{2,1,0:T(8,128)S(1)} %copy-done.1, f32[31,1,1024]{2,1,0:T(1,128)S(1)} %collective-permute-done.1), kind=kLoop, calls=%fused_computation.43 | loop fusion | flops 7110656 | bytes 6348800 | tf_op jit(solution)/shard_map/add | solution.py:201
  136.3 2.6 %collective-permute-done.6 = f32[31,1024]{1,0:T(8,128)S(1)} collective-permute-done((f32[31,1024]{1,0:T(8,128)S(1)}, f32[31,1024]{1,0:T(8,128)S(1)}, u32[]{:S(2)}, u32[]{:S(2)}) %collective-permute-start.6) | collective-permute-done | bytes 127008 | tf_op jit(solution)/shard_map/ppermute | solution.py:31
  (74 shorter events, 19.2 us)
Async XLA Ops:
  7.2 52.2 %all-gather.2.cloned.1.call-start = ((), (), s32[]{:S(2)}) async-start(), calls=%async_computation.1 | async-start | bytes 2621440 | tf_op jit(solution)/shard_map/all_gather | solution.py:169
  7.2 15.5 %collective-permute-start.2 = (s32[4096]{0:T(1024)}, s32[4096]{0:T(1024)S(1)}, u32[]{:S(2)}, u32[]{:S(2)}) collective-permute-start(s32[4096]{0:T(1024)} %param.14), channel_id=1, source_target_pairs={{0,8},{8,16},{16,24},{24,0},{1,9},{9,17},{17,25},{25,1},{2,10},{10... | collective-permute-start | bytes 49160 | tf_op jit(solution)/shard_map/ppermute | solution.py:143
  8.6 14.2 %collective-permute-start.3 = (s32[4096]{0:T(1024)}, s32[4096]{0:T(1024)S(1)}, u32[]{:S(2)}, u32[]{:S(2)}) collective-permute-start(s32[4096]{0:T(1024)} %param.14), channel_id=1, source_target_pairs={{0,16},{8,24},{16,0},{24,8},{1,17},{9,25},{17,1},{25,9},{2,18},{10... | collective-permute-start | bytes 49160 | tf_op jit(solution)/shard_map/ppermute | solution.py:143
  10.9 11.9 %collective-permute-start.4 = (s32[4096]{0:T(1024)}, s32[4096]{0:T(1024)S(1)}, u32[]{:S(2)}, u32[]{:S(2)}) collective-permute-start(s32[4096]{0:T(1024)} %param.14), channel_id=1, source_target_pairs={{0,24},{8,0},{16,8},{24,16},{1,25},{9,1},{17,9},{25,17},{2,26},{10... | collective-permute-start | bytes 49160 | tf_op jit(solution)/shard_map/ppermute | solution.py:143
  14.6 105.7 %reduce-scatter.2.cloned.1.call-start = ((), (), s32[]{:S(2)}) async-start(), calls=%async_computation.2 | async-start | bytes 2621440 | tf_op jit(solution)/shard_map/reduce_scatter | solution.py:192
  16.4 1.2 copy-start.3
  17.9 4.8 %copy-start.5 = (s32[4096]{0:T(1024)S(1)}, s32[4096]{0:T(1024)}, u32[]{:S(2)}) copy-start(s32[4096]{0:T(1024)} %param.14) | copy-start | bytes 49156
  58.4 3.3 %copy-start.6 = (f32[30]{0:T(128)S(1)}, f32[30]{0:T(128)}, u32[]{:S(2)}) copy-start(f32[30]{0:T(128)} %param.18) | copy-start | bytes 364
  58.4 3.3 %copy-start.7 = (f32[30]{0:T(128)S(1)}, f32[30]{0:T(128)}, u32[]{:S(2)}) copy-start(f32[30]{0:T(128)} %param.17) | copy-start | bytes 364
  59.4 2.2 %copy-start = (f32[32,16384]{1,0:T(8,128)S(1)}, f32[32,16384]{1,0:T(8,128)}, u32[]{:S(2)}) copy-start(f32[32,16384]{1,0:T(8,128)} %all-gather.2.cloned.1.call-done) | copy-start | bytes 6291460
  68.1 1.2 copy-start.8
  72.8 1.5 %copy-start.1 = (f32[30,16,1024]{2,1,0:T(8,128)S(1)}, f32[30,16,1024]{2,1,0:T(8,128)}, u32[]{:S(2)}) copy-start(f32[30,16,1024]{2,1,0:T(8,128)} %param.10) | copy-start | bytes 5898244
  72.8 8.5 %copy-start.4 = (s32[4096]{0:T(1024)S(1)}, s32[4096]{0:T(1024)}, u32[]{:S(2)}) copy-start(s32[4096]{0:T(1024)} %param.16) | copy-start | bytes 49156
  74.6 59.3 %collective-permute-start = (f32[31,1,1024]{2,1,0:T(1,128)S(1)}, f32[31,1,1024]{2,1,0:T(1,128)S(1)}, u32[]{:S(2)}, u32[]{:S(2)}) collective-permute-start(f32[31,1,1024]{2,1,0:T(1,128)S(1)} %get-tuple-element.31), channel_id=1, source_target_pairs={{1,0},{2,1},{3,2},{4,3},{5,4},{6,5},{7,6},{9,8},{10,9},{11,10},{12... | collective-permute-start | bytes 380936 | tf_op jit(solution)/shard_map/ppermute | solution.py:23
  77.3 56.6 %collective-permute-start.1 = (f32[31,1,1024]{2,1,0:T(1,128)S(1)}, f32[31,1,1024]{2,1,0:T(1,128)S(1)}, u32[]{:S(2)}, u32[]{:S(2)}) collective-permute-start(f32[31,1,1024]{2,1,0:T(1,128)S(1)} %get-tuple-element.30), channel_id=1, source_target_pairs={{0,1},{1,2},{2,3},{3,4},{4,5},{5,6},{6,7},{8,9},{9,10},{10,11},{11... | collective-permute-start | bytes 380936 | tf_op jit(solution)/shard_map/ppermute | solution.py:20
  125.9 10.4 %collective-permute-start.5 = (f32[31,1024]{1,0:T(8,128)S(1)}, f32[31,1024]{1,0:T(8,128)S(1)}, u32[]{:S(2)}, u32[]{:S(2)}) collective-permute-start(f32[31,1024]{1,0:T(8,128)S(1)} %slice_add_fusion.2), channel_id=1, source_target_pairs={{0,1},{1,2},{2,3},{3,4},{4,5},{5,6},{6,7},{8,9},{9,10},{10,11},{11... | collective-permute-start | bytes 380936 | tf_op jit(solution)/shard_map/ppermute | solution.py:31
  128.1 5.8 %copy-start.2 = (f32[31,16,1024]{2,1,0:T(8,128)S(1)}, f32[31,16,1024]{2,1,0:T(8,128)}, u32[]{:S(2)}) copy-start(f32[31,16,1024]{2,1,0:T(8,128)} %copy.26) | copy-start | bytes 6094852
  131.8 7.2 %collective-permute-start.6 = (f32[31,1024]{1,0:T(8,128)S(1)}, f32[31,1024]{1,0:T(8,128)S(1)}, u32[]{:S(2)}, u32[]{:S(2)}) collective-permute-start(f32[31,1024]{1,0:T(8,128)S(1)} %slice_add_fusion), channel_id=1, source_target_pairs={{1,0},{2,1},{3,2},{4,3},{5,4},{6,5},{7,6},{9,8},{10,9},{11,10},{12... | collective-permute-start | bytes 380936 | tf_op jit(solution)/shard_map/ppermute | solution.py:31
Sparse Core Ops, SparseCore 0:
  14.7 44.6 all-gather.1
  72.9 42.1 reduce-scatter.1

commit v9 on v8

--- a/solution.py
+++ b/solution.py
@@ -166,7 +166,7 @@
     parcel_in = jnp.concatenate(
         [masses, drop_temp[None], flags.astype(jnp.float32)[None]], axis=0
     )
-    all_in = field_major(lax.all_gather(field_major(parcel_in), "sect", axis=1, tiled=True))
+    all_in = plane_major(lax.all_gather(field_major(parcel_in), "sect", axis=0, tiled=False))
     all_cells = gather_sect(cells)
     n_all = all_cells.shape[0]
     cell_row = all_cells // plane
@@ -181,22 +181,27 @@
     )
     count = jnp.sum(owned.astype(jnp.int32)).reshape(1)
     table = gas_block.reshape(fields, n_cells).T
-    at_parcel = jnp.where(
-        owned[None, :], row_gather(count, order, local_sorted, table).T, 0.0
-    )
-    state_all, terms_all = parcel_update(
-        all_in[:NC], all_in[NC], all_in[NC + 1], at_parcel[:NC], at_parcel[NC],
+    blocks = all_in.shape[0]
+    owned_blocks = owned.reshape(blocks, 1, -1)
+    gathered = row_gather(count, order, local_sorted, table)
+    gathered = gathered.reshape(blocks, -1, fields).transpose(0, 2, 1)
+    at_parcel = plane_major(jnp.where(owned_blocks, gathered, 0.0))
+    state_all, terms_all = jax.vmap(
+        parcel_update, in_axes=(0, 0, 0, 0, 0, None, None, None)
+    )(
+        all_in[:, :NC], all_in[:, NC], all_in[:, NC + 1], at_parcel[:, :NC], at_parcel[:, NC],
         volat_a, volat_b, latent,
     )
-    state_own = field_major(jnp.where(owned[None, :], state_all, 0.0))
-    state = field_major(lax.psum_scatter(state_own, "sect", scatter_dimension=1, tiled=True))
+    state_own = plane_major(jnp.where(owned_blocks, state_all, 0.0))
+    state = field_major(lax.psum_scatter(state_own, "sect", scatter_dimension=0, tiled=False))
     padded = with_halo(gas_block, (("slab", 1),), 1)
     down = padded[:, :-2]
     upper = padded[:, 2:]
     flowed = plane_major(
         gas_block + 0.2 * (upper - 2.0 * gas_block + down) - 0.3 * (gas_block - down)
     )
-    summed = row_scatter_add(count, order, seg_sorted, terms_all.T, n_cells)
+    terms_rows = terms_all.transpose(0, 2, 1).reshape(-1, fields)
+    summed = row_scatter_add(count, order, seg_sorted, terms_rows, n_cells)
     source = plane_major(summed.T.reshape(fields, width_x, width_yz))
     gas_next = plane_major(flowed + source)
     kept = jnp.where(moves[None] == 0, state, 0.0)

time: 147 us -> 148 us (level)
    reshape x0 -> x2, local copies, waits for them, and re-layouts: none -> 12.6 us  [the longest x1 6.35 us: body(): gathered = gathered.reshape(blocks, -1, fields).transpose(0, 2, 1)]
    pallas_call x1 -> x0, local copies, waits for them, and re-layouts: 6.37 us -> none  [row_gather(): pl.pallas_call(_gather_kernel, grid_spec=spec, out_shape=jax.ShapeDtypeSt...]
    transpose x1 -> x0, local copies, waits for them, and re-layouts: 6.3 us -> none  [body(): summed = row_scatter_add(count, order, seg_sorted, terms_all.T, n_cells)]
    unnamed x22 -> x23, local copies, waits for them, and re-layouts: 4.83 us -> 4.89 us
where the time goes in v9:
time: 148 us; the launch traced here: 147 us
  Pallas kernels  39.5 us (27%)
  other arithmetic  36.7 us (25%)
  local copies, waits for them, and re-layouts  29.7 us (20%)
  starting transfers between devices  15.8 us (11%)
  between operations  14.4 us (10%)
  matrix products  7.2 us (5%)
  waiting for transfers between devices  3.43 us (2%)
    pallas_call x1, Pallas kernels, row_scatter_add(): pl.pallas_call(_scatter_kernel, grid_spec=spec, out_shape=jax.ShapeDtypeS...  21.9 us
    pallas_call x1, Pallas kernels, row_gather(): pl.pallas_call(_gather_kernel, grid_spec=spec, out_shape=jax.ShapeDtypeSt...  17.5 us
    sort x1, other arithmetic, body(): lax.sort((keys, position, local_cell, seg), num_keys=1)  8.29 us
    dot_general x2, matrix products, pack_slots(): out = jnp.dot(parts, onehot, preferred_element_type=jnp.float32)  7.2 us
    reshape x1, local copies, waits for them, and re-layouts, body(): source = plane_major(summed.T.reshape(fields, width_x, width_yz))  6.48 us
    reshape x1, local copies, waits for them, and re-layouts, body(): gathered = gathered.reshape(blocks, -1, fields).transpose(0, 2, 1)  6.35 us
    reshape x1, local copies, waits for them, and re-layouts, body(): terms_rows = terms_all.transpose(0, 2, 1).reshape(-1, fields)  6.3 us
    reduce_sum x4, other arithmetic, parcel_update(): slope = jnp.sum(frac * excess * excess / (denom * denom), axis=0) + 0.1  6.15 us
  transfers between devices with their start and end apart: 9, of which 2 were waited for; matrix products, arithmetic and copies ran while one was open for 39% of the time, Pallas kernels for 27%

profile of v9, /device:TPU:3, one launch (start us, length us, event | category | flops | bytes accessed | tf_op | source)
XLA Modules:
  0.0 146.8 jit_solution(8821186351274901210)
XLA Ops:
  8.6 2.3 %collective-permute-start.3 = (s32[4096]{0:T(1024)}, s32[4096]{0:T(1024)S(1)}, u32[]{:S(2)}, u32[]{:S(2)}) collective-permute-start(s32[4096]{0:T(1024)} %param.14), channel_id=1, source_target_pairs={{0,16},{8,24},{16,0},{24,8},{1,17},{9,25},{17,1},{25,9},{2,18},{10... | collective-permute-start | bytes 49160 | tf_op jit(solution)/shard_map/ppermute | solution.py:143
  12.7 1.9 %pad_maximum_fusion.7 = f32[32,4096]{1,0:T(8,128)} fusion(f32[1,4096]{1,0:T(1,128)S(1)} %bitcast.79, f32[1,4096]{1,0:T(1,128)} %bitcast.80, f32[30,4096]{1,0:T(8,128)} %param.12), kind=kLoop, calls=%fused_computation.59 | loop fusion | flops 262144 | bytes 1048576 | tf_op jit(solution)/shard_map/concatenate | solution.py:166
  14.6 1.7 %pad.33 = f32[32,16,1024]{2,1,0:T(8,128)S(1)} pad(f32[30,16,1024]{2,1,0:T(8,128)} %param.10, f32[]{:T(128)} %constant.118.clone.1), padding=0_2x0_0x0_0 | pad | bytes 4063236
  17.9 4.8 %copy.26 = f32[31,16384]{0,1:T(8,128)} copy(f32[31,16384]{1,0:T(8,128)S(1)} %pad_maximum_fusion.1) | data formatting | bytes 4063232 | tf_op jit(solution)/shard_map/concatenate | solution.py:160
  24.5 8.3 %sort.27 = (s32[16384]{0:T(1024)}, s32[16384]{0:T(1024)}, s32[16384]{0:T(1024)}, s32[16384]{0:T(1024)}) sort(s32[16384]{0:T(1024)S(1)} %iota_add_fusion, s32[16384]{0:T(1024)S(1)} %iota.19, s32[16384]{0:T(1024)S(1)} %get-tuple-element.24, s32[16384]{0:T(1024)S(1)} %get-tuple-element.23), dimensions={0}, to_apply=%region_1.2 | sort | flops 229376 | bytes 524288 | tf_op jit(solution)/shard_map/sort | solution.py:179
  32.8 17.5 %shard_map.121 = f32[16384,31]{1,0:T(8,128)} custom-call(s32[1]{0:T(128)} %bitcast.6.count_ref, s32[16384]{0:T(1024)} %get-tuple-element.6.dst_ref.src_ref, s32[16384]{0:T(1024)} %get-tuple-element.8.src_ref, f32[16384,31]{1,0:T(8,128)} %bitcast.63), custom_call_target="tpu_custom_call" | custom-call | tf_op jit(solution)/shard_map/pallas_call | solution.py:116
  50.3 6.4 %copy.28 = f32[4,4096,31]{1,2,0:T(8,128)} copy(f32[4,4096,31]{2,1,0:T(8,128)} %bitcast.66) | data formatting | bytes 4063232 | tf_op jit(solution)/shard_map/reshape | solution.py:187
  56.7 1.8 %select_bitcast_fusion = f32[4,31,4096]{2,1,0:T(8,128)S(1)} fusion(f32[4,4096,31]{1,2,0:T(8,128)} %copy.28, pred[4,4096]{1,0:T(4,128)(4,1)S(1)} %get-tuple-element.27), kind=kLoop, calls=%fused_computation.26 | loop fusion | flops 507904 | bytes 4079616 | tf_op jit(solution)/shard_map/jit(_where)/select_n | solution.py:188
  59.4 2.0 %slice_reduce_fusion = f32[4,4096]{1,0:T(4,128)S(1)} fusion(f32[4,32,4096]{2,1,0:T(8,128)} %bitcast.55), kind=kLoop, calls=%fused_computation.51 | loop fusion | flops 475136 | bytes 2031616 | tf_op jit(solution)/shard_map/vmap()/reduce_sum | solution.py:35
  69.5 1.7 %multiply_reduce_fusion = (f32[4,4096]{1,0:T(4,128)S(1)}, f32[4,30,4096]{2,1,0:T(8,128)}) fusion(f32[4,30,4096]{2,1,0:T(8,128)S(1)} %get-tuple-element.22, f32[30]{0:T(128)S(1)} %copy-done.8), kind=kLoop, calls=%fused_computation.17 | loop fusion | flops 1458176 | bytes 3997816 | tf_op jit(solution)/shard_map/vmap()/reduce_sum | solution.py:53
  71.5 1.6 %maximum_select_fusion = f32[4,31,4096]{2,1,0:T(8,128)} fusion(f32[4,1,4096]{2,1,0:T(1,128)S(1)} %get-tuple-element.28, f32[4,30,4096]{2,1,0:T(8,128)S(1)} %get-tuple-element.21, pred[4,4096]{1,0:T(4,128)(4,1)S(1)} %get-tuple-element.27), kind=kLoop, calls=%fused_computation.16 | loop fusion | flops 1015808 | bytes 4079616 | tf_op jit(solution)/shard_map/jit(_where)/select_n | solution.py:195
  74.9 2.7 %collective-permute-start = (f32[31,1,1024]{2,1,0:T(1,128)S(1)}, f32[31,1,1024]{2,1,0:T(1,128)S(1)}, u32[]{:S(2)}, u32[]{:S(2)}) collective-permute-start(f32[31,1,1024]{2,1,0:T(1,128)S(1)} %get-tuple-element.35), channel_id=1, source_target_pairs={{1,0},{2,1},{3,2},{4,3},{5,4},{6,5},{7,6},{9,8},{10,9},{11,10},{12... | collective-permute-start | bytes 380936 | tf_op jit(solution)/shard_map/ppermute | solution.py:23
  77.6 3.9 %collective-permute-start.1 = (f32[31,1,1024]{2,1,0:T(1,128)S(1)}, f32[31,1,1024]{2,1,0:T(1,128)S(1)}, u32[]{:S(2)}, u32[]{:S(2)}) collective-permute-start(f32[31,1,1024]{2,1,0:T(1,128)S(1)} %get-tuple-element.34), channel_id=1, source_target_pairs={{0,1},{1,2},{2,3},{3,4},{4,5},{5,6},{6,7},{8,9},{9,10},{10,11},{11... | collective-permute-start | bytes 380936 | tf_op jit(solution)/shard_map/ppermute | solution.py:20
  82.8 3.2 %maximum_bitcast_fusion = f32[4,4096,31]{1,2,0:T(8,128)} fusion(f32[4,1,4096]{2,1,0:T(1,128)S(1)} %get-tuple-element.29, f32[4,30,4096]{2,1,0:T(8,128)} %get-tuple-element.31), kind=kLoop, calls=%fused_computation.15 | loop fusion | flops 507904 | bytes 4063232 | tf_op jit(solution)/shard_map/transpose | solution.py:203
  86.0 6.3 %copy.36 = f32[4,4096,31]{2,1,0:T(8,128)} copy(f32[4,4096,31]{1,2,0:T(8,128)} %maximum_bitcast_fusion) | data formatting | bytes 4063232 | tf_op jit(solution)/shard_map/reshape | solution.py:203
  92.3 21.9 %shard_map.122 = f32[16384,31]{1,0:T(8,128)} custom-call(s32[1]{0:T(128)} %bitcast.6.count_ref, s32[16384]{0:T(1024)} %get-tuple-element.6.dst_ref.src_ref, s32[16384]{0:T(1024)} %get-tuple-element.7.seg_ref, f32[16384,31]{1,0:T(8,128)} %bitcast.64), custom_call_target="tpu_custom_call" | custom-call | tf_op jit(solution)/shard_map/pallas_call | solution.py:132
  114.2 6.5 %copy.37 = f32[31,16,1024]{2,1,0:T(8,128)} copy(f32[31,16,1024]{0,2,1:T(8,128)} %bitcast.65) | data formatting | bytes 4063232 | tf_op jit(solution)/shard_map/reshape | solution.py:205
  120.7 2.0 %reduce-precision_convert_fusion.1 = (bf16[31,4096]{1,0:T(8,128)(2,1)S(1)}, bf16[31,4096]{1,0:T(8,128)(2,1)S(1)}, f32[31,4096]{1,0:T(8,128)}, bf16[31,4096]{1,0:T(8,128)(2,1)S(1)}) fusion(f32[1,31,4096]{2,1,0:T(8,128)} %reduce-scatter.2.cloned.1.call-done, pred[4096]{0:T(1024)(128)(4,1)S(1)} %get-tuple-element.41), kind=kLoop, calls=%fused_computation.57 | loop fusion | flops 1015808 | bytes 1781760 | tf_op jit(solution)/shard_map/convert.2
  122.7 3.6 %fusion = f32[93,1024]{1,0:T(8,128)S(1)} fusion(s32[4096]{0:T(1024)S(1)} %get-tuple-element.45, bf16[31,4096]{1,0:T(8,128)(2,1)S(1)} %get-tuple-element.37, bf16[31,4096]{1,0:T(8,128)(2,1)S(1)} %get-tuple-element.39, bf16[31,4096]{1,0:T(8,128)(2,1)S(1)} %get-tuple-element.36), kind=kOutput, calls=%fused_computation.3 | convolution fusion | flops 786620416 | bytes 1159168 | tf_op jit(solution)/shard_map/dot_general | solution.py:69
  126.3 2.1 %collective-permute-start.5 = (f32[31,1024]{1,0:T(8,128)S(1)}, f32[31,1024]{1,0:T(8,128)S(1)}, u32[]{:S(2)}, u32[]{:S(2)}) collective-permute-start(f32[31,1024]{1,0:T(8,128)S(1)} %slice_add_fusion.2), channel_id=1, source_target_pairs={{0,1},{1,2},{2,3},{3,4},{4,5},{5,6},{6,7},{8,9},{9,10},{10,11},{11... | collective-permute-start | bytes 380936 | tf_op jit(solution)/shard_map/ppermute | solution.py:31
  128.4 3.6 %fusion.1 = f32[93,1024]{1,0:T(8,128)S(1)} fusion(s32[4096]{0:T(1024)S(1)} %get-tuple-element.44, bf16[31,4096]{1,0:T(8,128)(2,1)S(1)} %get-tuple-element.37, bf16[31,4096]{1,0:T(8,128)(2,1)S(1)} %get-tuple-element.39, bf16[31,4096]{1,0:T(8,128)(2,1)S(1)} %get-tuple-element.36), kind=kOutput, calls=%fused_computation.4 | convolution fusion | flops 786620416 | bytes 1159168 | tf_op jit(solution)/shard_map/dot_general | solution.py:69
  132.1 2.2 %collective-permute-start.6 = (f32[31,1024]{1,0:T(8,128)S(1)}, f32[31,1024]{1,0:T(8,128)S(1)}, u32[]{:S(2)}, u32[]{:S(2)}) collective-permute-start(f32[31,1024]{1,0:T(8,128)S(1)} %slice_add_fusion), channel_id=1, source_target_pairs={{1,0},{2,1},{3,2},{4,3},{5,4},{6,5},{7,6},{9,8},{10,9},{11,10},{12... | collective-permute-start | bytes 380936 | tf_op jit(solution)/shard_map/ppermute | solution.py:31
  134.3 2.4 %fusion.15 = f32[31,16,1024]{2,1,0:T(8,128)} fusion(f32[31,16,1024]{2,1,0:T(8,128)S(1)} %copy-done.2, f32[31,1,1024]{2,1,0:T(1,128)S(1)} %collective-permute-done, f32[1,16,1024]{2,1,0:T(8,128)S(1)} %bitcast.76, f32[30,16,1024]{2,1,0:T(8,128)S(1)} %copy-done.1, f32[31,1,1024]{2,1,0:T(1,128)S(1)} %collective-permute-done.1), kind=kLoop, calls=%fused_computation.43 | loop fusion | flops 7110656 | bytes 6348800 | tf_op jit(solution)/shard_map/add | solution.py:206
  136.7 2.5 %collective-permute-done.6 = f32[31,1024]{1,0:T(8,128)S(1)} collective-permute-done((f32[31,1024]{1,0:T(8,128)S(1)}, f32[31,1024]{1,0:T(8,128)S(1)}, u32[]{:S(2)}, u32[]{:S(2)}) %collective-permute-start.6) | collective-permute-done | bytes 127008 | tf_op jit(solution)/shard_map/ppermute | solution.py:31
  (74 shorter events, 19.4 us)
Async XLA Ops:
  7.2 52.2 %all-gather.3.cloned.1.call-start = ((), (), s32[]{:S(2)}) async-start(), calls=%async_computation.2 | async-start | bytes 2621440 | tf_op jit(solution)/shard_map/all_gather | solution.py:169
  7.2 15.5 %collective-permute-start.2 = (s32[4096]{0:T(1024)}, s32[4096]{0:T(1024)S(1)}, u32[]{:S(2)}, u32[]{:S(2)}) collective-permute-start(s32[4096]{0:T(1024)} %param.14), channel_id=1, source_target_pairs={{0,8},{8,16},{16,24},{24,0},{1,9},{9,17},{17,25},{25,1},{2,10},{10... | collective-permute-start | bytes 49160 | tf_op jit(solution)/shard_map/ppermute | solution.py:143
  8.6 14.2 %collective-permute-start.3 = (s32[4096]{0:T(1024)}, s32[4096]{0:T(1024)S(1)}, u32[]{:S(2)}, u32[]{:S(2)}) collective-permute-start(s32[4096]{0:T(1024)} %param.14), channel_id=1, source_target_pairs={{0,16},{8,24},{16,0},{24,8},{1,17},{9,25},{17,1},{25,9},{2,18},{10... | collective-permute-start | bytes 49160 | tf_op jit(solution)/shard_map/ppermute | solution.py:143
  10.9 11.9 %collective-permute-start.4 = (s32[4096]{0:T(1024)}, s32[4096]{0:T(1024)S(1)}, u32[]{:S(2)}, u32[]{:S(2)}) collective-permute-start(s32[4096]{0:T(1024)} %param.14), channel_id=1, source_target_pairs={{0,24},{8,0},{16,8},{24,16},{1,25},{9,1},{17,9},{25,17},{2,26},{10... | collective-permute-start | bytes 49160 | tf_op jit(solution)/shard_map/ppermute | solution.py:143
  14.6 106.1 %reduce-scatter.2.cloned.1.call-start = ((), (), s32[]{:S(2)}) async-start(), calls=%async_computation.1 | async-start | bytes 2621440 | tf_op jit(solution)/shard_map/reduce_scatter | solution.py:196
  16.4 1.2 copy-start.3
  17.9 4.8 %copy-start.5 = (s32[4096]{0:T(1024)S(1)}, s32[4096]{0:T(1024)}, u32[]{:S(2)}) copy-start(s32[4096]{0:T(1024)} %param.14) | copy-start | bytes 49156
  58.5 3.3 %copy-start.6 = (f32[30]{0:T(128)S(1)}, f32[30]{0:T(128)}, u32[]{:S(2)}) copy-start(f32[30]{0:T(128)} %param.18) | copy-start | bytes 364
  58.5 3.3 %copy-start.7 = (f32[30]{0:T(128)S(1)}, f32[30]{0:T(128)}, u32[]{:S(2)}) copy-start(f32[30]{0:T(128)} %param.17) | copy-start | bytes 364
  59.4 2.2 %copy-start = (f32[128,4096]{1,0:T(8,128)S(1)}, f32[128,4096]{1,0:T(8,128)}, u32[]{:S(2)}) copy-start(f32[128,4096]{1,0:T(8,128)} %all-gather.3.cloned.1.call-done) | copy-start | bytes 6291460
  68.3 1.2 copy-start.8
  73.1 1.5 %copy-start.1 = (f32[30,16,1024]{2,1,0:T(8,128)S(1)}, f32[30,16,1024]{2,1,0:T(8,128)}, u32[]{:S(2)}) copy-start(f32[30,16,1024]{2,1,0:T(8,128)} %param.10) | copy-start | bytes 5898244
  73.1 8.5 %copy-start.4 = (s32[4096]{0:T(1024)S(1)}, s32[4096]{0:T(1024)}, u32[]{:S(2)}) copy-start(s32[4096]{0:T(1024)} %param.16) | copy-start | bytes 49156
  74.9 59.4 %collective-permute-start = (f32[31,1,1024]{2,1,0:T(1,128)S(1)}, f32[31,1,1024]{2,1,0:T(1,128)S(1)}, u32[]{:S(2)}, u32[]{:S(2)}) collective-permute-start(f32[31,1,1024]{2,1,0:T(1,128)S(1)} %get-tuple-element.35), channel_id=1, source_target_pairs={{1,0},{2,1},{3,2},{4,3},{5,4},{6,5},{7,6},{9,8},{10,9},{11,10},{12... | collective-permute-start | bytes 380936 | tf_op jit(solution)/shard_map/ppermute | solution.py:23
  77.6 56.7 %collective-permute-start.1 = (f32[31,1,1024]{2,1,0:T(1,128)S(1)}, f32[31,1,1024]{2,1,0:T(1,128)S(1)}, u32[]{:S(2)}, u32[]{:S(2)}) collective-permute-start(f32[31,1,1024]{2,1,0:T(1,128)S(1)} %get-tuple-element.34), channel_id=1, source_target_pairs={{0,1},{1,2},{2,3},{3,4},{4,5},{5,6},{6,7},{8,9},{9,10},{10,11},{11... | collective-permute-start | bytes 380936 | tf_op jit(solution)/shard_map/ppermute | solution.py:20
  126.3 10.4 %collective-permute-start.5 = (f32[31,1024]{1,0:T(8,128)S(1)}, f32[31,1024]{1,0:T(8,128)S(1)}, u32[]{:S(2)}, u32[]{:S(2)}) collective-permute-start(f32[31,1024]{1,0:T(8,128)S(1)} %slice_add_fusion.2), channel_id=1, source_target_pairs={{0,1},{1,2},{2,3},{3,4},{4,5},{5,6},{6,7},{8,9},{9,10},{10,11},{11... | collective-permute-start | bytes 380936 | tf_op jit(solution)/shard_map/ppermute | solution.py:31
  128.4 5.9 %copy-start.2 = (f32[31,16,1024]{2,1,0:T(8,128)S(1)}, f32[31,16,1024]{2,1,0:T(8,128)}, u32[]{:S(2)}) copy-start(f32[31,16,1024]{2,1,0:T(8,128)} %copy.37) | copy-start | bytes 6094852
  132.1 7.2 %collective-permute-start.6 = (f32[31,1024]{1,0:T(8,128)S(1)}, f32[31,1024]{1,0:T(8,128)S(1)}, u32[]{:S(2)}, u32[]{:S(2)}) collective-permute-start(f32[31,1024]{1,0:T(8,128)S(1)} %slice_add_fusion), channel_id=1, source_target_pairs={{1,0},{2,1},{3,2},{4,3},{5,4},{6,5},{7,6},{9,8},{10,9},{11,10},{12... | collective-permute-start | bytes 380936 | tf_op jit(solution)/shard_map/ppermute | solution.py:31
Sparse Core Ops, SparseCore 0:
  14.7 44.6 all-gather.2
  73.3 42.1 reduce-scatter.1

commit v10 on v9

--- a/solution.py
+++ b/solution.py
@@ -33,15 +33,18 @@
 
 def parcel_update(masses, drop_temp, flags, vap_p, temp_p, volat_a, volat_b, latent):
     total = jnp.sum(masses, axis=0)
-    frac = masses / total[None]
+    inv_total = 1.0 / total
+    frac = masses * inv_total[None]
     surf = 0.5 * (drop_temp + temp_p)
     ratio = jnp.exp(volat_a[:, None] - volat_b[:, None] / surf[None])
     excess = ratio - 1.0
+    weighted = frac * excess
     share = jnp.full(total.shape, 0.5, jnp.float32)
     for sweep in range(RR_ITERS):
-        denom = 1.0 + share[None] * excess
-        residue = jnp.sum(frac * excess / denom, axis=0)
-        slope = jnp.sum(frac * excess * excess / (denom * denom), axis=0) + 0.1
+        inv_denom = 1.0 / (1.0 + share[None] * excess)
+        part = weighted * inv_denom
+        residue = jnp.sum(part, axis=0)
+        slope = jnp.sum(part * excess * inv_denom, axis=0) + 0.1
         share = jnp.clip(share + residue / slope, 0.02, 0.98)
     effect = flags.astype(jnp.float32) * share
     vap_eq = frac * ratio / (1.0 + effect[None] * excess)
@@ -50,7 +53,7 @@
     new_temp = (
         drop_temp
         + 0.2 * (temp_p - drop_temp)
-        - 0.5 * jnp.sum(latent[:, None] * evap, axis=0) / total
+        - 0.5 * jnp.sum(latent[:, None] * evap, axis=0) * inv_total
     )
     heat = total * (drop_temp - temp_p)
     state = jnp.concatenate([new_mass, new_temp[None]], axis=0)

time: 148 us -> 147 us (level)
  no operation moved by 1% of the time
where the time goes in v10:
time: 147 us; the launch traced here: 146 us
  Pallas kernels  39.7 us (27%)
  other arithmetic  36.4 us (25%)
  local copies, waits for them, and re-layouts  29.8 us (20%)
  starting transfers between devices  15.8 us (11%)
  between operations  14.4 us (10%)
  matrix products  7.2 us (5%)
  waiting for transfers between devices  3.25 us (2%)
    pallas_call x1, Pallas kernels, row_scatter_add(): pl.pallas_call(_scatter_kernel, grid_spec=spec, out_shape=jax.ShapeDtypeS...  22.1 us
    pallas_call x1, Pallas kernels, row_gather(): pl.pallas_call(_gather_kernel, grid_spec=spec, out_shape=jax.ShapeDtypeSt...  17.6 us
    sort x1, other arithmetic, body(): lax.sort((keys, position, local_cell, seg), num_keys=1)  8.29 us
    dot_general x2, matrix products, pack_slots(): out = jnp.dot(parts, onehot, preferred_element_type=jnp.float32)  7.2 us
    reshape x1, local copies, waits for them, and re-layouts, body(): source = plane_major(summed.T.reshape(fields, width_x, width_yz))  6.49 us
    reshape x1, local copies, waits for them, and re-layouts, body(): gathered = gathered.reshape(blocks, -1, fields).transpose(0, 2, 1)  6.35 us
    reshape x1, local copies, waits for them, and re-layouts, body(): terms_rows = terms_all.transpose(0, 2, 1).reshape(-1, fields)  6.3 us
    reduce_sum x4, other arithmetic, parcel_update(): slope = jnp.sum(part * excess * inv_denom, axis=0) + 0.1  5.81 us
  transfers between devices with their start and end apart: 9, of which 2 were waited for; matrix products, arithmetic and copies ran while one was open for 39% of the time, Pallas kernels for 27%

profile of v10, /device:TPU:3, one launch (start us, length us, event | category | flops | bytes accessed | tf_op | source)
XLA Modules:
  0.0 146.4 jit_solution(3048304278783671026)
XLA Ops:
  8.6 2.3 %collective-permute-start.3 = (s32[4096]{0:T(1024)}, s32[4096]{0:T(1024)S(1)}, u32[]{:S(2)}, u32[]{:S(2)}) collective-permute-start(s32[4096]{0:T(1024)} %param.14), channel_id=1, source_target_pairs={{0,16},{8,24},{16,0},{24,8},{1,17},{9,25},{17,1},{25,9},{2,18},{10... | collective-permute-start | bytes 49160 | tf_op jit(solution)/shard_map/ppermute | solution.py:146
  12.7 1.9 %pad_maximum_fusion.7 = f32[32,4096]{1,0:T(8,128)} fusion(f32[1,4096]{1,0:T(1,128)S(1)} %bitcast.79, f32[1,4096]{1,0:T(1,128)} %bitcast.80, f32[30,4096]{1,0:T(8,128)} %param.12), kind=kLoop, calls=%fused_computation.54 | loop fusion | flops 262144 | bytes 1048576 | tf_op jit(solution)/shard_map/concatenate | solution.py:169
  14.6 1.7 %pad.33 = f32[32,16,1024]{2,1,0:T(8,128)S(1)} pad(f32[30,16,1024]{2,1,0:T(8,128)} %param.10, f32[]{:T(128)} %constant.119.clone.1), padding=0_2x0_0x0_0 | pad | bytes 4063236
  17.9 4.8 %copy.26 = f32[31,16384]{0,1:T(8,128)} copy(f32[31,16384]{1,0:T(8,128)S(1)} %pad_maximum_fusion.1) | data formatting | bytes 4063232 | tf_op jit(solution)/shard_map/concatenate | solution.py:163
  24.5 8.3 %sort.27 = (s32[16384]{0:T(1024)}, s32[16384]{0:T(1024)}, s32[16384]{0:T(1024)}, s32[16384]{0:T(1024)}) sort(s32[16384]{0:T(1024)S(1)} %iota_add_fusion, s32[16384]{0:T(1024)S(1)} %iota.19, s32[16384]{0:T(1024)S(1)} %get-tuple-element.24, s32[16384]{0:T(1024)S(1)} %get-tuple-element.23), dimensions={0}, to_apply=%region_1.2 | sort | flops 229376 | bytes 524288 | tf_op jit(solution)/shard_map/sort | solution.py:182
  32.8 17.6 %shard_map.121 = f32[16384,31]{1,0:T(8,128)} custom-call(s32[1]{0:T(128)} %bitcast.6.count_ref, s32[16384]{0:T(1024)} %get-tuple-element.6.dst_ref.src_ref, s32[16384]{0:T(1024)} %get-tuple-element.8.src_ref, f32[16384,31]{1,0:T(8,128)} %bitcast.63), custom_call_target="tpu_custom_call" | custom-call | tf_op jit(solution)/shard_map/pallas_call | solution.py:119
  50.4 6.4 %copy.28 = f32[4,4096,31]{1,2,0:T(8,128)} copy(f32[4,4096,31]{2,1,0:T(8,128)} %bitcast.66) | data formatting | bytes 4063232 | tf_op jit(solution)/shard_map/reshape | solution.py:190
  56.8 1.8 %select_bitcast_fusion = f32[4,31,4096]{2,1,0:T(8,128)S(1)} fusion(f32[4,4096,31]{1,2,0:T(8,128)} %copy.28, pred[4,4096]{1,0:T(4,128)(4,1)S(1)} %get-tuple-element.27), kind=kLoop, calls=%fused_computation.26 | loop fusion | flops 507904 | bytes 4079616 | tf_op jit(solution)/shard_map/jit(_where)/select_n | solution.py:191
  59.4 2.0 %slice_reduce_fusion = f32[4,4096]{1,0:T(4,128)S(1)} fusion(f32[4,32,4096]{2,1,0:T(8,128)} %bitcast.55), kind=kLoop, calls=%fused_computation.41 | loop fusion | flops 475136 | bytes 2031616 | tf_op jit(solution)/shard_map/vmap()/reduce_sum | solution.py:35
  69.1 1.7 %multiply_reduce_fusion = (f32[4,4096]{1,0:T(4,128)S(1)}, f32[4,30,4096]{2,1,0:T(8,128)}) fusion(f32[4,30,4096]{2,1,0:T(8,128)S(1)} %get-tuple-element.22, f32[30]{0:T(128)S(1)} %copy-done.8), kind=kLoop, calls=%fused_computation.17 | loop fusion | flops 1458176 | bytes 3997816 | tf_op jit(solution)/shard_map/vmap()/reduce_sum | solution.py:56
  71.1 1.6 %maximum_select_fusion = f32[4,31,4096]{2,1,0:T(8,128)} fusion(f32[4,1,4096]{2,1,0:T(1,128)S(1)} %get-tuple-element.28, f32[4,30,4096]{2,1,0:T(8,128)S(1)} %get-tuple-element.21, pred[4,4096]{1,0:T(4,128)(4,1)S(1)} %get-tuple-element.27), kind=kLoop, calls=%fused_computation.16 | loop fusion | flops 1015808 | bytes 4079616 | tf_op jit(solution)/shard_map/jit(_where)/select_n | solution.py:198
  74.5 2.7 %collective-permute-start = (f32[31,1,1024]{2,1,0:T(1,128)S(1)}, f32[31,1,1024]{2,1,0:T(1,128)S(1)}, u32[]{:S(2)}, u32[]{:S(2)}) collective-permute-start(f32[31,1,1024]{2,1,0:T(1,128)S(1)} %get-tuple-element.35), channel_id=1, source_target_pairs={{1,0},{2,1},{3,2},{4,3},{5,4},{6,5},{7,6},{9,8},{10,9},{11,10},{12... | collective-permute-start | bytes 380936 | tf_op jit(solution)/shard_map/ppermute | solution.py:23
  77.3 3.9 %collective-permute-start.1 = (f32[31,1,1024]{2,1,0:T(1,128)S(1)}, f32[31,1,1024]{2,1,0:T(1,128)S(1)}, u32[]{:S(2)}, u32[]{:S(2)}) collective-permute-start(f32[31,1,1024]{2,1,0:T(1,128)S(1)} %get-tuple-element.34), channel_id=1, source_target_pairs={{0,1},{1,2},{2,3},{3,4},{4,5},{5,6},{6,7},{8,9},{9,10},{10,11},{11... | collective-permute-start | bytes 380936 | tf_op jit(solution)/shard_map/ppermute | solution.py:20
  82.4 3.2 %maximum_bitcast_fusion = f32[4,4096,31]{1,2,0:T(8,128)} fusion(f32[4,1,4096]{2,1,0:T(1,128)S(1)} %get-tuple-element.29, f32[4,30,4096]{2,1,0:T(8,128)} %get-tuple-element.31), kind=kLoop, calls=%fused_computation.15 | loop fusion | flops 507904 | bytes 4063232 | tf_op jit(solution)/shard_map/transpose | solution.py:206
  85.6 6.3 %copy.36 = f32[4,4096,31]{2,1,0:T(8,128)} copy(f32[4,4096,31]{1,2,0:T(8,128)} %maximum_bitcast_fusion) | data formatting | bytes 4063232 | tf_op jit(solution)/shard_map/reshape | solution.py:206
  91.9 22.1 %shard_map.122 = f32[16384,31]{1,0:T(8,128)} custom-call(s32[1]{0:T(128)} %bitcast.6.count_ref, s32[16384]{0:T(1024)} %get-tuple-element.6.dst_ref.src_ref, s32[16384]{0:T(1024)} %get-tuple-element.7.seg_ref, f32[16384,31]{1,0:T(8,128)} %bitcast.64), custom_call_target="tpu_custom_call" | custom-call | tf_op jit(solution)/shard_map/pallas_call | solution.py:135
  114.0 6.5 %copy.37 = f32[31,16,1024]{2,1,0:T(8,128)} copy(f32[31,16,1024]{0,2,1:T(8,128)} %bitcast.65) | data formatting | bytes 4063232 | tf_op jit(solution)/shard_map/reshape | solution.py:208
  120.4 2.0 %reduce-precision_convert_fusion.1 = (bf16[31,4096]{1,0:T(8,128)(2,1)S(1)}, bf16[31,4096]{1,0:T(8,128)(2,1)S(1)}, f32[31,4096]{1,0:T(8,128)}, bf16[31,4096]{1,0:T(8,128)(2,1)S(1)}) fusion(f32[1,31,4096]{2,1,0:T(8,128)} %reduce-scatter.2.cloned.1.call-done, pred[4096]{0:T(1024)(128)(4,1)S(1)} %get-tuple-element.43), kind=kLoop, calls=%fused_computation.52 | loop fusion | flops 1015808 | bytes 1781760 | tf_op jit(solution)/shard_map/convert.2
  122.4 3.6 %fusion = f32[93,1024]{1,0:T(8,128)S(1)} fusion(s32[4096]{0:T(1024)S(1)} %get-tuple-element.47, bf16[31,4096]{1,0:T(8,128)(2,1)S(1)} %get-tuple-element.37, bf16[31,4096]{1,0:T(8,128)(2,1)S(1)} %get-tuple-element.39, bf16[31,4096]{1,0:T(8,128)(2,1)S(1)} %get-tuple-element.36), kind=kOutput, calls=%fused_computation.3 | convolution fusion | flops 786620416 | bytes 1159168 | tf_op jit(solution)/shard_map/dot_general | solution.py:72
  126.1 2.0 %collective-permute-start.5 = (f32[31,1024]{1,0:T(8,128)S(1)}, f32[31,1024]{1,0:T(8,128)S(1)}, u32[]{:S(2)}, u32[]{:S(2)}) collective-permute-start(f32[31,1024]{1,0:T(8,128)S(1)} %slice_add_fusion.2), channel_id=1, source_target_pairs={{0,1},{1,2},{2,3},{3,4},{4,5},{5,6},{6,7},{8,9},{9,10},{10,11},{11... | collective-permute-start | bytes 380936 | tf_op jit(solution)/shard_map/ppermute | solution.py:31
  128.1 3.6 %fusion.1 = f32[93,1024]{1,0:T(8,128)S(1)} fusion(s32[4096]{0:T(1024)S(1)} %get-tuple-element.46, bf16[31,4096]{1,0:T(8,128)(2,1)S(1)} %get-tuple-element.37, bf16[31,4096]{1,0:T(8,128)(2,1)S(1)} %get-tuple-element.39, bf16[31,4096]{1,0:T(8,128)(2,1)S(1)} %get-tuple-element.36), kind=kOutput, calls=%fused_computation.4 | convolution fusion | flops 786620416 | bytes 1159168 | tf_op jit(solution)/shard_map/dot_general | solution.py:72
  131.7 2.3 %collective-permute-start.6 = (f32[31,1024]{1,0:T(8,128)S(1)}, f32[31,1024]{1,0:T(8,128)S(1)}, u32[]{:S(2)}, u32[]{:S(2)}) collective-permute-start(f32[31,1024]{1,0:T(8,128)S(1)} %slice_add_fusion), channel_id=1, source_target_pairs={{1,0},{2,1},{3,2},{4,3},{5,4},{6,5},{7,6},{9,8},{10,9},{11,10},{12... | collective-permute-start | bytes 380936 | tf_op jit(solution)/shard_map/ppermute | solution.py:31
  134.1 2.4 %fusion.11 = f32[31,16,1024]{2,1,0:T(8,128)} fusion(f32[31,16,1024]{2,1,0:T(8,128)S(1)} %copy-done.2, f32[31,1,1024]{2,1,0:T(1,128)S(1)} %collective-permute-done, f32[1,16,1024]{2,1,0:T(8,128)S(1)} %bitcast.76, f32[30,16,1024]{2,1,0:T(8,128)S(1)} %copy-done.1, f32[31,1,1024]{2,1,0:T(1,128)S(1)} %collective-permute-done.1), kind=kLoop, calls=%fused_computation.35 | loop fusion | flops 7110656 | bytes 6348800 | tf_op jit(solution)/shard_map/add | solution.py:209
  136.5 2.4 %collective-permute-done.6 = f32[31,1024]{1,0:T(8,128)S(1)} collective-permute-done((f32[31,1024]{1,0:T(8,128)S(1)}, f32[31,1024]{1,0:T(8,128)S(1)}, u32[]{:S(2)}, u32[]{:S(2)}) %collective-permute-start.6) | collective-permute-done | bytes 127008 | tf_op jit(solution)/shard_map/ppermute | solution.py:31
  (74 shorter events, 18.9 us)
Async XLA Ops:
  7.2 52.2 %all-gather.3.cloned.1.call-start = ((), (), s32[]{:S(2)}) async-start(), calls=%async_computation.2 | async-start | bytes 2621440 | tf_op jit(solution)/shard_map/all_gather | solution.py:172
  7.2 15.5 %collective-permute-start.2 = (s32[4096]{0:T(1024)}, s32[4096]{0:T(1024)S(1)}, u32[]{:S(2)}, u32[]{:S(2)}) collective-permute-start(s32[4096]{0:T(1024)} %param.14), channel_id=1, source_target_pairs={{0,8},{8,16},{16,24},{24,0},{1,9},{9,17},{17,25},{25,1},{2,10},{10... | collective-permute-start | bytes 49160 | tf_op jit(solution)/shard_map/ppermute | solution.py:146
  8.6 14.2 %collective-permute-start.3 = (s32[4096]{0:T(1024)}, s32[4096]{0:T(1024)S(1)}, u32[]{:S(2)}, u32[]{:S(2)}) collective-permute-start(s32[4096]{0:T(1024)} %param.14), channel_id=1, source_target_pairs={{0,16},{8,24},{16,0},{24,8},{1,17},{9,25},{17,1},{25,9},{2,18},{10... | collective-permute-start | bytes 49160 | tf_op jit(solution)/shard_map/ppermute | solution.py:146
  10.9 11.9 %collective-permute-start.4 = (s32[4096]{0:T(1024)}, s32[4096]{0:T(1024)S(1)}, u32[]{:S(2)}, u32[]{:S(2)}) collective-permute-start(s32[4096]{0:T(1024)} %param.14), channel_id=1, source_target_pairs={{0,24},{8,0},{16,8},{24,16},{1,25},{9,1},{17,9},{25,17},{2,26},{10... | collective-permute-start | bytes 49160 | tf_op jit(solution)/shard_map/ppermute | solution.py:146
  14.6 105.8 %reduce-scatter.2.cloned.1.call-start = ((), (), s32[]{:S(2)}) async-start(), calls=%async_computation.1 | async-start | bytes 2621440 | tf_op jit(solution)/shard_map/reduce_scatter | solution.py:199
  16.4 1.2 copy-start.3
  17.9 4.8 %copy-start.5 = (s32[4096]{0:T(1024)S(1)}, s32[4096]{0:T(1024)}, u32[]{:S(2)}) copy-start(s32[4096]{0:T(1024)} %param.14) | copy-start | bytes 49156
  58.6 3.3 %copy-start.6 = (f32[30]{0:T(128)S(1)}, f32[30]{0:T(128)}, u32[]{:S(2)}) copy-start(f32[30]{0:T(128)} %param.18) | copy-start | bytes 364
  58.6 3.3 %copy-start.7 = (f32[30]{0:T(128)S(1)}, f32[30]{0:T(128)}, u32[]{:S(2)}) copy-start(f32[30]{0:T(128)} %param.17) | copy-start | bytes 364
  59.4 2.2 %copy-start = (f32[128,4096]{1,0:T(8,128)S(1)}, f32[128,4096]{1,0:T(8,128)}, u32[]{:S(2)}) copy-start(f32[128,4096]{1,0:T(8,128)} %all-gather.3.cloned.1.call-done) | copy-start | bytes 6291460
  67.9 1.2 copy-start.8
  72.8 1.5 %copy-start.1 = (f32[30,16,1024]{2,1,0:T(8,128)S(1)}, f32[30,16,1024]{2,1,0:T(8,128)}, u32[]{:S(2)}) copy-start(f32[30,16,1024]{2,1,0:T(8,128)} %param.10) | copy-start | bytes 5898244
  72.8 8.5 %copy-start.4 = (s32[4096]{0:T(1024)S(1)}, s32[4096]{0:T(1024)}, u32[]{:S(2)}) copy-start(s32[4096]{0:T(1024)} %param.16) | copy-start | bytes 49156
  74.5 59.5 %collective-permute-start = (f32[31,1,1024]{2,1,0:T(1,128)S(1)}, f32[31,1,1024]{2,1,0:T(1,128)S(1)}, u32[]{:S(2)}, u32[]{:S(2)}) collective-permute-start(f32[31,1,1024]{2,1,0:T(1,128)S(1)} %get-tuple-element.35), channel_id=1, source_target_pairs={{1,0},{2,1},{3,2},{4,3},{5,4},{6,5},{7,6},{9,8},{10,9},{11,10},{12... | collective-permute-start | bytes 380936 | tf_op jit(solution)/shard_map/ppermute | solution.py:23
  77.3 56.8 %collective-permute-start.1 = (f32[31,1,1024]{2,1,0:T(1,128)S(1)}, f32[31,1,1024]{2,1,0:T(1,128)S(1)}, u32[]{:S(2)}, u32[]{:S(2)}) collective-permute-start(f32[31,1,1024]{2,1,0:T(1,128)S(1)} %get-tuple-element.34), channel_id=1, source_target_pairs={{0,1},{1,2},{2,3},{3,4},{4,5},{5,6},{6,7},{8,9},{9,10},{10,11},{11... | collective-permute-start | bytes 380936 | tf_op jit(solution)/shard_map/ppermute | solution.py:20
  126.1 10.4 %collective-permute-start.5 = (f32[31,1024]{1,0:T(8,128)S(1)}, f32[31,1024]{1,0:T(8,128)S(1)}, u32[]{:S(2)}, u32[]{:S(2)}) collective-permute-start(f32[31,1024]{1,0:T(8,128)S(1)} %slice_add_fusion.2), channel_id=1, source_target_pairs={{0,1},{1,2},{2,3},{3,4},{4,5},{5,6},{6,7},{8,9},{9,10},{10,11},{11... | collective-permute-start | bytes 380936 | tf_op jit(solution)/shard_map/ppermute | solution.py:31
  128.0 6.0 %copy-start.2 = (f32[31,16,1024]{2,1,0:T(8,128)S(1)}, f32[31,16,1024]{2,1,0:T(8,128)}, u32[]{:S(2)}) copy-start(f32[31,16,1024]{2,1,0:T(8,128)} %copy.37) | copy-start | bytes 6094852
  131.7 7.2 %collective-permute-start.6 = (f32[31,1024]{1,0:T(8,128)S(1)}, f32[31,1024]{1,0:T(8,128)S(1)}, u32[]{:S(2)}, u32[]{:S(2)}) collective-permute-start(f32[31,1024]{1,0:T(8,128)S(1)} %slice_add_fusion), channel_id=1, source_target_pairs={{1,0},{2,1},{3,2},{4,3},{5,4},{6,5},{7,6},{9,8},{10,9},{11,10},{12... | collective-permute-start | bytes 380936 | tf_op jit(solution)/shard_map/ppermute | solution.py:31
Sparse Core Ops, SparseCore 0:
  14.7 44.6 all-gather.2
  72.9 42.1 reduce-scatter.1

commit v11 on v10

--- a/solution.py
+++ b/solution.py
@@ -61,6 +61,67 @@
     return (state, terms)
 
 
+def _update_kernel(in_ref, at_ref, own_ref, va_ref, vb_ref, lat_ref, state_ref, terms_ref):
+    masses = in_ref[0, 0:NC, :]
+    drop_temp = in_ref[0, NC:NC + 1, :]
+    flags = in_ref[0, NC + 1:NC + 2, :]
+    vap_p = at_ref[0, 0:NC, :]
+    temp_p = at_ref[0, NC:NC + 1, :]
+    own = own_ref[0] > 0.0
+    total = jnp.sum(masses, axis=0, keepdims=True)
+    inv_total = 1.0 / total
+    frac = masses * inv_total
+    surf = 0.5 * (drop_temp + temp_p)
+    ratio = jnp.exp(va_ref[...] - vb_ref[...] / surf)
+    excess = ratio - 1.0
+    weighted = frac * excess
+    share = jnp.full(total.shape, 0.5, jnp.float32)
+    for sweep in range(RR_ITERS):
+        inv_denom = 1.0 / (1.0 + share * excess)
+        part = weighted * inv_denom
+        residue = jnp.sum(part, axis=0, keepdims=True)
+        slope = jnp.sum(part * excess * inv_denom, axis=0, keepdims=True) + 0.1
+        share = jnp.clip(share + residue / slope, 0.02, 0.98)
+    effect = flags * share
+    vap_eq = frac * ratio / (1.0 + effect * excess)
+    evap = 0.02 * total * (vap_eq - vap_p)
+    new_temp = (
+        drop_temp
+        + 0.2 * (temp_p - drop_temp)
+        - 0.5 * jnp.sum(lat_ref[...] * evap, axis=0, keepdims=True) * inv_total
+    )
+    state_ref[0, 0:NC, :] = jnp.where(own, masses - evap, 0.0)
+    state_ref[0, NC:NC + 1, :] = jnp.where(own, new_temp, 0.0)
+    terms_ref[0, 0:NC, :] = 0.1 * evap
+    terms_ref[0, NC:NC + 1, :] = 0.05 * (total * (drop_temp - temp_p))
+
+
+def owner_update(all_in, at_parcel, owned, volat_a, volat_b, latent, tile=512):
+    blocks, rows_in, width = all_in.shape
+    fields = at_parcel.shape[1]
+    grid = (blocks, width // tile)
+    column = lambda b, t: (b, 0, t)
+    param = lambda b, t: (0, 0)
+    out = jax.ShapeDtypeStruct((blocks, fields, width), jnp.float32)
+    return pl.pallas_call(
+        _update_kernel,
+        grid=grid,
+        in_specs=[
+            pl.BlockSpec((1, rows_in, tile), column),
+            pl.BlockSpec((1, fields, tile), column),
+            pl.BlockSpec((1, 1, tile), column),
+            pl.BlockSpec((NC, 1), param),
+            pl.BlockSpec((NC, 1), param),
+            pl.BlockSpec((NC, 1), param),
+        ],
+        out_specs=[pl.BlockSpec((1, fields, tile), column)] * 2,
+        out_shape=[out, out],
+    )(
+        all_in, at_parcel, owned.astype(jnp.float32).reshape(blocks, 1, width),
+        volat_a.reshape(NC, 1), volat_b.reshape(NC, 1), latent.reshape(NC, 1),
+    )
+
+
 def pack_slots(state, chosen):
     slot = jnp.where(chosen, jnp.cumsum(chosen.astype(jnp.int32)) - 1, -1)
     onehot = (slot[:, None] == jnp.arange(MOVE_CAP, dtype=jnp.int32)[None, :]).astype(jnp.bfloat16)
@@ -189,13 +250,7 @@
     gathered = row_gather(count, order, local_sorted, table)
     gathered = gathered.reshape(blocks, -1, fields).transpose(0, 2, 1)
     at_parcel = plane_major(jnp.where(owned_blocks, gathered, 0.0))
-    state_all, terms_all = jax.vmap(
-        parcel_update, in_axes=(0, 0, 0, 0, 0, None, None, None)
-    )(
-        all_in[:, :NC], all_in[:, NC], all_in[:, NC + 1], at_parcel[:, :NC], at_parcel[:, NC],
-        volat_a, volat_b, latent,
-    )
-    state_own = plane_major(jnp.where(owned_blocks, state_all, 0.0))
+    state_own, terms_all = owner_update(all_in, at_parcel, owned, volat_a, volat_b, latent)
     state = field_major(lax.psum_scatter(state_own, "sect", scatter_dimension=0, tiled=False))
     padded = with_halo(gas_block, (("slab", 1),), 1)
     down = padded[:, :-2]

time: 147 us -> 155 us (1.054); the launches traced: 146 us -> 152 us
  Pallas kernels: 39.7 us -> 60.5 us
  other arithmetic: 36.4 us -> 21.1 us
    pallas_call x0 -> x1, Pallas kernels: none -> 20.9 us  [owner_update(): pl.pallas_call(_update_kernel, grid=grid, in_specs=[pl.BlockSpec((1, rows...]
    reduce_sum x6 -> x0, other arithmetic: 9.47 us -> none  [the longest x4 5.81 us: parcel_update(): slope = jnp.sum(part * excess * inv_denom, axis=0) + 0.1]
    transpose x0 -> x1, local copies, waits for them, and re-layouts: none -> 6.33 us  [body(): terms_rows = terms_all.transpose(0, 2, 1).reshape(-1, fields)]
    reshape x1 -> x3, local copies, waits for them, and re-layouts: 6.3 us -> 2.07 us  [the longest x1 0.69 us: owner_update(): latent.reshape(NC, 1)]
    transpose x1 -> x0, other arithmetic: 3.21 us -> none  [body(): terms_rows = terms_all.transpose(0, 2, 1).reshape(-1, fields)]
    select_n x1 -> x0, other arithmetic: 1.63 us -> none  [body(): state_own = plane_major(jnp.where(owned_blocks, state_all, 0.0))]
    unnamed x23 -> x20, local copies, waits for them, and re-layouts: 4.89 us -> 4.58 us
  transfers between devices with their start and end apart: 9 -> 9, of which waited for: 2 -> 1; matrix products, arithmetic and copies ran while one was open for 39% -> 37% of each run, Pallas kernels for 27% -> 26%
where the time goes in v11:
time: 155 us; the launch traced here: 152 us
  Pallas kernels  60.5 us (39%)
  local copies, waits for them, and re-layouts  30.4 us (20%)
  other arithmetic  21.1 us (14%)
  starting transfers between devices  16 us (10%)
  between operations  14.3 us (9%)
  matrix products  7.2 us (5%)
  waiting for transfers between devices  2.89 us (2%)
    pallas_call x1, Pallas kernels, row_scatter_add(): pl.pallas_call(_scatter_kernel, grid_spec=spec, out_shape=jax.ShapeDtypeS...  22 us
    pallas_call x1, Pallas kernels, owner_update(): pl.pallas_call(_update_kernel, grid=grid, in_specs=[pl.BlockSpec((1, rows...  20.9 us
    pallas_call x1, Pallas kernels, row_gather(): pl.pallas_call(_gather_kernel, grid_spec=spec, out_shape=jax.ShapeDtypeSt...  17.5 us
    sort x1, other arithmetic, body(): lax.sort((keys, position, local_cell, seg), num_keys=1)  8.32 us
    dot_general x2, matrix products, pack_slots(): out = jnp.dot(parts, onehot, preferred_element_type=jnp.float32)  7.2 us
    reshape x1, local copies, waits for them, and re-layouts, body(): source = plane_major(summed.T.reshape(fields, width_x, width_yz))  6.47 us
    transpose x1, local copies, waits for them, and re-layouts, body(): terms_rows = terms_all.transpose(0, 2, 1).reshape(-1, fields)  6.33 us
    reshape x1, local copies, waits for them, and re-layouts, body(): gathered = gathered.reshape(blocks, -1, fields).transpose(0, 2, 1)  5.25 us
  transfers between devices with their start and end apart: 9, of which 1 were waited for; matrix products, arithmetic and copies ran while one was open for 37% of the time, Pallas kernels for 26%

profile of v11, /device:TPU:3, one launch (start us, length us, event | category | flops | bytes accessed | tf_op | source)
XLA Modules:
  0.0 152.5 jit_solution(17505647742744505157)
XLA Ops:
  7.2 1.3 collective-permute-start.2
  8.6 2.3 %collective-permute-start.3 = (s32[4096]{0:T(1024)}, s32[4096]{0:T(1024)S(1)}, u32[]{:S(2)}, u32[]{:S(2)}) collective-permute-start(s32[4096]{0:T(1024)} %param.14), channel_id=1, source_target_pairs={{0,16},{8,24},{16,0},{24,8},{1,17},{9,25},{17,1},{25,9},{2,18},{10... | collective-permute-start | bytes 49160 | tf_op jit(solution)/shard_map/ppermute | solution.py:207
  12.7 1.9 %pad_maximum_fusion.7 = f32[32,4096]{1,0:T(8,128)} fusion(f32[1,4096]{1,0:T(1,128)S(1)} %bitcast.61, f32[1,4096]{1,0:T(1,128)} %bitcast.62, f32[30,4096]{1,0:T(8,128)} %param.12), kind=kLoop, calls=%fused_computation.30 | loop fusion | flops 262144 | bytes 1048576 | tf_op jit(solution)/shard_map/concatenate | solution.py:230
  14.7 1.7 %pad.29 = f32[32,16,1024]{2,1,0:T(8,128)S(1)} pad(f32[30,16,1024]{2,1,0:T(8,128)} %param.10, f32[]{:T(128)} %constant.107.clone.1), padding=0_2x0_0x0_0 | pad | bytes 4063236
  18.0 4.8 %copy.28 = f32[31,16384]{0,1:T(8,128)} copy(f32[31,16384]{1,0:T(8,128)S(1)} %pad_maximum_fusion.1) | data formatting | bytes 4063232 | tf_op jit(solution)/shard_map/concatenate | solution.py:224
  26.6 8.3 %sort.27 = (s32[16384]{0:T(1024)}, s32[16384]{0:T(1024)}, s32[16384]{0:T(1024)}, s32[16384]{0:T(1024)}) sort(s32[16384]{0:T(1024)S(1)} %iota_add_fusion, s32[16384]{0:T(1024)S(1)} %iota.19, s32[16384]{0:T(1024)S(1)} %get-tuple-element.18, s32[16384]{0:T(1024)S(1)} %get-tuple-element.17), dimensions={0}, to_apply=%region_1.2 | sort | flops 229376 | bytes 524288 | tf_op jit(solution)/shard_map/sort | solution.py:243
  34.9 17.5 %shard_map.121 = f32[16384,31]{1,0:T(8,128)} custom-call(s32[1]{0:T(128)} %bitcast.6.count_ref, s32[16384]{0:T(1024)} %get-tuple-element.8.dst_ref.src_ref, s32[16384]{0:T(1024)} %get-tuple-element.10.src_ref, f32[16384,31]{1,0:T(8,128)} %bitcast.48), custom_call_target="tpu_custom_call" | custom-call | tf_op jit(solution)/shard_map/pallas_call | solution.py:180
  52.4 5.2 %copy.30 = f32[4,4096,31]{1,2,0:T(8,128)S(1)} copy(f32[4,4096,31]{2,1,0:T(8,128)} %bitcast.51) | data formatting | bytes 4063232 | tf_op jit(solution)/shard_map/reshape | solution.py:251
  57.7 1.2 compare_convert_fusion.own_ref
  58.9 1.5 select_bitcast_fusion.at_ref
  60.4 20.9 %shard_map.122 = (f32[4,31,4096]{2,1,0:T(8,128)}, f32[4,31,4096]{2,1,0:T(8,128)}) custom-call(f32[4,32,4096]{2,1,0:T(8,128)} %bitcast.55, f32[4,31,4096]{2,1,0:T(8,128)} %select_bitcast_fusion.at_ref, f32[4,1,4096]{2,1,0:T(1,128)} %compare_convert_fusion.own_ref, f32[30,1]{1,0:T(8,128)} %copy.31.va_ref, f32[30,1]{1,0:T(8,128)} %copy.32.vb_ref, ...), custom_call_target="tpu_custom_call" | custom-call | tf_op jit(solution)/shard_map/pallas_call | solution.py:106
  81.4 1.5 copy-done
  83.1 3.2 %collective-permute-start = (f32[31,1,1024]{2,1,0:T(1,128)S(1)}, f32[31,1,1024]{2,1,0:T(1,128)S(1)}, u32[]{:S(2)}, u32[]{:S(2)}) collective-permute-start(f32[31,1,1024]{2,1,0:T(1,128)S(1)} %get-tuple-element.23), channel_id=1, source_target_pairs={{1,0},{2,1},{3,2},{4,3},{5,4},{6,5},{7,6},{9,8},{10,9},{11,10},{12... | collective-permute-start | bytes 380936 | tf_op jit(solution)/shard_map/ppermute | solution.py:23
  86.3 3.3 %collective-permute-start.1 = (f32[31,1,1024]{2,1,0:T(1,128)S(1)}, f32[31,1,1024]{2,1,0:T(1,128)S(1)}, u32[]{:S(2)}, u32[]{:S(2)}) collective-permute-start(f32[31,1,1024]{2,1,0:T(1,128)S(1)} %get-tuple-element.22), channel_id=1, source_target_pairs={{0,1},{1,2},{2,3},{3,4},{4,5},{5,6},{6,7},{8,9},{9,10},{10,11},{11... | collective-permute-start | bytes 380936 | tf_op jit(solution)/shard_map/ppermute | solution.py:20
  90.8 6.3 %copy.34 = f32[4,4096,31]{2,1,0:T(8,128)} copy(f32[4,4096,31]{1,2,0:T(8,128)} %bitcast.54) | data formatting | bytes 4063232 | tf_op jit(solution)/shard_map/transpose | solution.py:261
  97.2 22.0 %shard_map.123 = f32[16384,31]{1,0:T(8,128)} custom-call(s32[1]{0:T(128)} %bitcast.6.count_ref, s32[16384]{0:T(1024)} %get-tuple-element.8.dst_ref.src_ref, s32[16384]{0:T(1024)} %get-tuple-element.9.seg_ref, f32[16384,31]{1,0:T(8,128)} %bitcast.49), custom_call_target="tpu_custom_call" | custom-call | tf_op jit(solution)/shard_map/pallas_call | solution.py:196
  119.2 6.5 %copy.38 = f32[31,16,1024]{2,1,0:T(8,128)} copy(f32[31,16,1024]{0,2,1:T(8,128)} %bitcast.50) | data formatting | bytes 4063232 | tf_op jit(solution)/shard_map/reshape | solution.py:263
  125.7 2.0 %reduce-precision_convert_fusion.1 = (bf16[31,4096]{1,0:T(8,128)(2,1)S(1)}, bf16[31,4096]{1,0:T(8,128)(2,1)S(1)}, f32[31,4096]{1,0:T(8,128)}, bf16[31,4096]{1,0:T(8,128)(2,1)S(1)}) fusion(f32[1,31,4096]{2,1,0:T(8,128)} %reduce-scatter.2.cloned.1.call-done, pred[4096]{0:T(1024)(128)(4,1)S(1)} %get-tuple-element.29), kind=kLoop, calls=%fused_computation.28 | loop fusion | flops 1015808 | bytes 1781760 | tf_op jit(solution)/shard_map/convert.2
  127.6 3.6 %fusion = f32[93,1024]{1,0:T(8,128)S(1)} fusion(s32[4096]{0:T(1024)S(1)} %get-tuple-element.33, bf16[31,4096]{1,0:T(8,128)(2,1)S(1)} %get-tuple-element.25, bf16[31,4096]{1,0:T(8,128)(2,1)S(1)} %get-tuple-element.27, bf16[31,4096]{1,0:T(8,128)(2,1)S(1)} %get-tuple-element.24), kind=kOutput, calls=%fused_computation.3 | convolution fusion | flops 786620416 | bytes 1159168 | tf_op jit(solution)/shard_map/dot_general | solution.py:133
  131.3 2.8 %collective-permute-start.5 = (f32[31,1024]{1,0:T(8,128)S(1)}, f32[31,1024]{1,0:T(8,128)S(1)}, u32[]{:S(2)}, u32[]{:S(2)}) collective-permute-start(f32[31,1024]{1,0:T(8,128)S(1)} %slice_add_fusion.2), channel_id=1, source_target_pairs={{0,1},{1,2},{2,3},{3,4},{4,5},{5,6},{6,7},{8,9},{9,10},{10,11},{11... | collective-permute-start | bytes 380936 | tf_op jit(solution)/shard_map/ppermute | solution.py:31
  134.1 3.6 %fusion.1 = f32[93,1024]{1,0:T(8,128)S(1)} fusion(s32[4096]{0:T(1024)S(1)} %get-tuple-element.32, bf16[31,4096]{1,0:T(8,128)(2,1)S(1)} %get-tuple-element.25, bf16[31,4096]{1,0:T(8,128)(2,1)S(1)} %get-tuple-element.27, bf16[31,4096]{1,0:T(8,128)(2,1)S(1)} %get-tuple-element.24), kind=kOutput, calls=%fused_computation.4 | convolution fusion | flops 786620416 | bytes 1159168 | tf_op jit(solution)/shard_map/dot_general | solution.py:133
  137.7 1.9 %collective-permute-start.6 = (f32[31,1024]{1,0:T(8,128)S(1)}, f32[31,1024]{1,0:T(8,128)S(1)}, u32[]{:S(2)}, u32[]{:S(2)}) collective-permute-start(f32[31,1024]{1,0:T(8,128)S(1)} %slice_add_fusion), channel_id=1, source_target_pairs={{1,0},{2,1},{3,2},{4,3},{5,4},{6,5},{7,6},{9,8},{10,9},{11,10},{12... | collective-permute-start | bytes 380936 | tf_op jit(solution)/shard_map/ppermute | solution.py:31
  139.7 2.4 %fusion.9 = f32[31,16,1024]{2,1,0:T(8,128)} fusion(f32[31,16,1024]{2,1,0:T(8,128)S(1)} %copy-done.1, f32[31,1,1024]{2,1,0:T(1,128)S(1)} %collective-permute-done, f32[1,16,1024]{2,1,0:T(8,128)S(1)} %bitcast.58, f32[30,16,1024]{2,1,0:T(8,128)S(1)} %copy-done, f32[31,1,1024]{2,1,0:T(1,128)S(1)} %collective-permute-done.1), kind=kLoop, calls=%fused_computation.20 | loop fusion | flops 7110656 | bytes 6348800 | tf_op jit(solution)/shard_map/add | solution.py:264
  142.1 2.8 %collective-permute-done.6 = f32[31,1024]{1,0:T(8,128)S(1)} collective-permute-done((f32[31,1024]{1,0:T(8,128)S(1)}, f32[31,1024]{1,0:T(8,128)S(1)}, u32[]{:S(2)}, u32[]{:S(2)}) %collective-permute-start.6) | collective-permute-done | bytes 127008 | tf_op jit(solution)/shard_map/ppermute | solution.py:31
  (59 shorter events, 9.4 us)
Async XLA Ops:
  7.2 53.3 %all-gather.3.cloned.1.call-start = ((), (), s32[]{:S(2)}) async-start(), calls=%async_computation.2 | async-start | bytes 2621440 | tf_op jit(solution)/shard_map/all_gather | solution.py:233
  7.2 17.6 %collective-permute-start.2 = (s32[4096]{0:T(1024)}, s32[4096]{0:T(1024)S(1)}, u32[]{:S(2)}, u32[]{:S(2)}) collective-permute-start(s32[4096]{0:T(1024)} %param.14), channel_id=1, source_target_pairs={{0,8},{8,16},{16,24},{24,0},{1,9},{9,17},{17,25},{25,1},{2,10},{10... | collective-permute-start | bytes 49160 | tf_op jit(solution)/shard_map/ppermute | solution.py:207
  8.6 16.3 %collective-permute-start.3 = (s32[4096]{0:T(1024)}, s32[4096]{0:T(1024)S(1)}, u32[]{:S(2)}, u32[]{:S(2)}) collective-permute-start(s32[4096]{0:T(1024)} %param.14), channel_id=1, source_target_pairs={{0,16},{8,24},{16,0},{24,8},{1,17},{9,25},{17,1},{25,9},{2,18},{10... | collective-permute-start | bytes 49160 | tf_op jit(solution)/shard_map/ppermute | solution.py:207
  10.9 14.0 %collective-permute-start.4 = (s32[4096]{0:T(1024)}, s32[4096]{0:T(1024)S(1)}, u32[]{:S(2)}, u32[]{:S(2)}) collective-permute-start(s32[4096]{0:T(1024)} %param.14), channel_id=1, source_target_pairs={{0,24},{8,0},{16,8},{24,16},{1,25},{9,1},{17,9},{25,17},{2,26},{10... | collective-permute-start | bytes 49160 | tf_op jit(solution)/shard_map/ppermute | solution.py:207
  14.6 111.1 %reduce-scatter.2.cloned.1.call-start = ((), (), s32[]{:S(2)}) async-start(), calls=%async_computation.1 | async-start | bytes 2621440 | tf_op jit(solution)/shard_map/reduce_scatter | solution.py:254
  16.4 1.2 copy-start.2
  17.9 4.8 %copy-start.5 = (f32[30]{0:T(128)S(1)}, f32[30]{0:T(128)}, u32[]{:S(2)}) copy-start(f32[30]{0:T(128)} %param.17) | copy-start | bytes 364
  17.9 5.5 %copy-start.6 = (f32[30]{0:T(128)S(1)}, f32[30]{0:T(128)}, u32[]{:S(2)}) copy-start(f32[30]{0:T(128)} %param.18) | copy-start | bytes 364
  18.0 6.2 %copy-start.7 = (f32[30]{0:T(128)S(1)}, f32[30]{0:T(128)}, u32[]{:S(2)}) copy-start(f32[30]{0:T(128)} %param.19) | copy-start | bytes 364
  18.0 6.9 %copy-start.4 = (s32[4096]{0:T(1024)S(1)}, s32[4096]{0:T(1024)}, u32[]{:S(2)}) copy-start(s32[4096]{0:T(1024)} %param.14) | copy-start | bytes 49156
  81.3 1.5 %copy-start = (f32[30,16,1024]{2,1,0:T(8,128)S(1)}, f32[30,16,1024]{2,1,0:T(8,128)}, u32[]{:S(2)}) copy-start(f32[30,16,1024]{2,1,0:T(8,128)} %param.10) | copy-start | bytes 5898244
  81.4 8.3 %copy-start.3 = (s32[4096]{0:T(1024)S(1)}, s32[4096]{0:T(1024)}, u32[]{:S(2)}) copy-start(s32[4096]{0:T(1024)} %param.16) | copy-start | bytes 49156
  83.1 56.5 %collective-permute-start = (f32[31,1,1024]{2,1,0:T(1,128)S(1)}, f32[31,1,1024]{2,1,0:T(1,128)S(1)}, u32[]{:S(2)}, u32[]{:S(2)}) collective-permute-start(f32[31,1,1024]{2,1,0:T(1,128)S(1)} %get-tuple-element.23), channel_id=1, source_target_pairs={{1,0},{2,1},{3,2},{4,3},{5,4},{6,5},{7,6},{9,8},{10,9},{11,10},{12... | collective-permute-start | bytes 380936 | tf_op jit(solution)/shard_map/ppermute | solution.py:23
  86.3 53.4 %collective-permute-start.1 = (f32[31,1,1024]{2,1,0:T(1,128)S(1)}, f32[31,1,1024]{2,1,0:T(1,128)S(1)}, u32[]{:S(2)}, u32[]{:S(2)}) collective-permute-start(f32[31,1,1024]{2,1,0:T(1,128)S(1)} %get-tuple-element.22), channel_id=1, source_target_pairs={{0,1},{1,2},{2,3},{3,4},{4,5},{5,6},{6,7},{8,9},{9,10},{10,11},{11... | collective-permute-start | bytes 380936 | tf_op jit(solution)/shard_map/ppermute | solution.py:20
  131.3 10.8 %collective-permute-start.5 = (f32[31,1024]{1,0:T(8,128)S(1)}, f32[31,1024]{1,0:T(8,128)S(1)}, u32[]{:S(2)}, u32[]{:S(2)}) collective-permute-start(f32[31,1024]{1,0:T(8,128)S(1)} %slice_add_fusion.2), channel_id=1, source_target_pairs={{0,1},{1,2},{2,3},{3,4},{4,5},{5,6},{6,7},{8,9},{9,10},{10,11},{11... | collective-permute-start | bytes 380936 | tf_op jit(solution)/shard_map/ppermute | solution.py:31
  134.1 5.6 %copy-start.1 = (f32[31,16,1024]{2,1,0:T(8,128)S(1)}, f32[31,16,1024]{2,1,0:T(8,128)}, u32[]{:S(2)}) copy-start(f32[31,16,1024]{2,1,0:T(8,128)} %copy.38) | copy-start | bytes 6094852
  137.7 7.2 %collective-permute-start.6 = (f32[31,1024]{1,0:T(8,128)S(1)}, f32[31,1024]{1,0:T(8,128)S(1)}, u32[]{:S(2)}, u32[]{:S(2)}) collective-permute-start(f32[31,1024]{1,0:T(8,128)S(1)} %slice_add_fusion), channel_id=1, source_target_pairs={{1,0},{2,1},{3,2},{4,3},{5,4},{6,5},{7,6},{9,8},{10,9},{11,10},{12... | collective-permute-start | bytes 380936 | tf_op jit(solution)/shard_map/ppermute | solution.py:31
Sparse Core Ops, SparseCore 0:
  14.7 44.6 all-gather.2
  81.5 42.3 reduce-scatter.1

commit v12 on v10

--- a/solution.py
+++ b/solution.py
@@ -61,9 +61,13 @@
     return (state, terms)
 
 
-def pack_slots(state, chosen):
-    slot = jnp.where(chosen, jnp.cumsum(chosen.astype(jnp.int32)) - 1, -1)
-    onehot = (slot[:, None] == jnp.arange(MOVE_CAP, dtype=jnp.int32)[None, :]).astype(jnp.bfloat16)
+def pack_slots(state, chosen_sets):
+    slot = jnp.full(chosen_sets[0].shape, -1, jnp.int32)
+    for i, chosen in enumerate(chosen_sets):
+        rank = jnp.cumsum(chosen.astype(jnp.int32)) - 1 + i * MOVE_CAP
+        slot = jnp.where(chosen, rank, slot)
+    columns = jnp.arange(len(chosen_sets) * MOVE_CAP, dtype=jnp.int32)
+    onehot = (slot[:, None] == columns[None, :]).astype(jnp.bfloat16)
     high = lax.reduce_precision(state, exponent_bits=8, mantissa_bits=7)
     rest = state - high
     middle = lax.reduce_precision(rest, exponent_bits=8, mantissa_bits=7)
@@ -71,7 +75,8 @@
     parts = jnp.concatenate([high, middle, low], axis=0).astype(jnp.bfloat16)
     out = jnp.dot(parts, onehot, preferred_element_type=jnp.float32)
     rows = state.shape[0]
-    return (out[:rows] + out[rows : 2 * rows]) + out[2 * rows :]
+    out = (out[:rows] + out[rows : 2 * rows]) + out[2 * rows :]
+    return [out[:, i * MOVE_CAP : (i + 1) * MOVE_CAP] for i in range(len(chosen_sets))]
 
 
 def _gather_kernel(count_ref, dst_ref, src_ref, table_ref, out_ref):
@@ -208,8 +213,9 @@
     source = plane_major(summed.T.reshape(fields, width_x, width_yz))
     gas_next = plane_major(flowed + source)
     kept = jnp.where(moves[None] == 0, state, 0.0)
-    from_prev = shifted(pack_slots(state, moves == 2), "slab", 1)
-    from_next = shifted(pack_slots(state, moves == 1), "slab", -1)
+    rightward, leftward = pack_slots(state, (moves == 2, moves == 1))
+    from_prev = shifted(rightward, "slab", 1)
+    from_next = shifted(leftward, "slab", -1)
     arrivals = jnp.concatenate([from_prev, from_next], axis=1)
     return (gas_next, kept, arrivals)
 

time: 147 us -> 147 us (level)
    dot_general x2 -> x1, matrix products: 7.2 us -> 6.91 us  [pack_slots(): out = jnp.dot(parts, onehot, preferred_element_type=jnp.float32)]
where the time goes in v12:
time: 147 us; the launch traced here: 146 us
  Pallas kernels  39.4 us (27%)
  other arithmetic  36.4 us (25%)
  local copies, waits for them, and re-layouts  29.6 us (20%)
  starting transfers between devices  15.8 us (11%)
  between operations  14.4 us (10%)
  matrix products  6.91 us (5%)
  waiting for transfers between devices  3.56 us (2%)
    pallas_call x1, Pallas kernels, row_scatter_add(): pl.pallas_call(_scatter_kernel, grid_spec=spec, out_shape=jax.ShapeDtypeS...  21.9 us
    pallas_call x1, Pallas kernels, row_gather(): pl.pallas_call(_gather_kernel, grid_spec=spec, out_shape=jax.ShapeDtypeSt...  17.5 us
    sort x1, other arithmetic, body(): lax.sort((keys, position, local_cell, seg), num_keys=1)  8.29 us
    dot_general x1, matrix products, pack_slots(): out = jnp.dot(parts, onehot, preferred_element_type=jnp.float32)  6.91 us
    reshape x1, local copies, waits for them, and re-layouts, body(): source = plane_major(summed.T.reshape(fields, width_x, width_yz))  6.47 us
    reshape x1, local copies, waits for them, and re-layouts, body(): gathered = gathered.reshape(blocks, -1, fields).transpose(0, 2, 1)  6.35 us
    reshape x1, local copies, waits for them, and re-layouts, body(): terms_rows = terms_all.transpose(0, 2, 1).reshape(-1, fields)  6.3 us
    reduce_sum x4, other arithmetic, parcel_update(): slope = jnp.sum(part * excess * inv_denom, axis=0) + 0.1  5.81 us
  transfers between devices with their start and end apart: 9, of which 2 were waited for; matrix products, arithmetic and copies ran while one was open for 39% of the time, Pallas kernels for 27%

profile of v12, /device:TPU:3, one launch (start us, length us, event | category | flops | bytes accessed | tf_op | source)
XLA Modules:
  0.0 146.0 jit_solution(14035270143494166085)
XLA Ops:
  8.6 2.3 %collective-permute-start.3 = (s32[4096]{0:T(1024)}, s32[4096]{0:T(1024)S(1)}, u32[]{:S(2)}, u32[]{:S(2)}) collective-permute-start(s32[4096]{0:T(1024)} %param.14), channel_id=1, source_target_pairs={{0,16},{8,24},{16,0},{24,8},{1,17},{9,25},{17,1},{25,9},{2,18},{10... | collective-permute-start | bytes 49160 | tf_op jit(solution)/shard_map/ppermute | solution.py:151
  12.7 1.9 %pad_maximum_fusion.6 = f32[32,4096]{1,0:T(8,128)} fusion(f32[1,4096]{1,0:T(1,128)S(1)} %bitcast.81, f32[1,4096]{1,0:T(1,128)} %bitcast.82, f32[30,4096]{1,0:T(8,128)} %param.12), kind=kLoop, calls=%fused_computation.55 | loop fusion | flops 262144 | bytes 1048576 | tf_op jit(solution)/shard_map/concatenate | solution.py:174
  14.6 1.7 %pad.33 = f32[32,16,1024]{2,1,0:T(8,128)S(1)} pad(f32[30,16,1024]{2,1,0:T(8,128)} %param.10, f32[]{:T(128)} %constant.121.clone.1), padding=0_2x0_0x0_0 | pad | bytes 4063236
  17.9 4.8 %copy.26 = f32[31,16384]{0,1:T(8,128)} copy(f32[31,16384]{1,0:T(8,128)S(1)} %pad_maximum_fusion.1) | data formatting | bytes 4063232 | tf_op jit(solution)/shard_map/concatenate | solution.py:168
  24.5 8.3 %sort.27 = (s32[16384]{0:T(1024)}, s32[16384]{0:T(1024)}, s32[16384]{0:T(1024)}, s32[16384]{0:T(1024)}) sort(s32[16384]{0:T(1024)S(1)} %iota_add_fusion, s32[16384]{0:T(1024)S(1)} %iota.18, s32[16384]{0:T(1024)S(1)} %get-tuple-element.24, s32[16384]{0:T(1024)S(1)} %get-tuple-element.23), dimensions={0}, to_apply=%region_1.2 | sort | flops 229376 | bytes 524288 | tf_op jit(solution)/shard_map/sort | solution.py:187
  32.8 17.5 %shard_map.121 = f32[16384,31]{1,0:T(8,128)} custom-call(s32[1]{0:T(128)} %bitcast.6.count_ref, s32[16384]{0:T(1024)} %get-tuple-element.6.dst_ref.src_ref, s32[16384]{0:T(1024)} %get-tuple-element.8.src_ref, f32[16384,31]{1,0:T(8,128)} %bitcast.65), custom_call_target="tpu_custom_call" | custom-call | tf_op jit(solution)/shard_map/pallas_call | solution.py:124
  50.3 6.4 %copy.28 = f32[4,4096,31]{1,2,0:T(8,128)} copy(f32[4,4096,31]{2,1,0:T(8,128)} %bitcast.68) | data formatting | bytes 4063232 | tf_op jit(solution)/shard_map/reshape | solution.py:195
  56.6 1.8 %select_bitcast_fusion = f32[4,31,4096]{2,1,0:T(8,128)S(1)} fusion(f32[4,4096,31]{1,2,0:T(8,128)} %copy.28, pred[4,4096]{1,0:T(4,128)(4,1)S(1)} %get-tuple-element.27), kind=kLoop, calls=%fused_computation.23 | loop fusion | flops 507904 | bytes 4079616 | tf_op jit(solution)/shard_map/jit(_where)/select_n | solution.py:196
  59.4 2.0 %slice_reduce_fusion = f32[4,4096]{1,0:T(4,128)S(1)} fusion(f32[4,32,4096]{2,1,0:T(8,128)} %bitcast.57), kind=kLoop, calls=%fused_computation.38 | loop fusion | flops 475136 | bytes 2031616 | tf_op jit(solution)/shard_map/vmap()/reduce_sum | solution.py:35
  69.1 1.7 %multiply_reduce_fusion = (f32[4,4096]{1,0:T(4,128)S(1)}, f32[4,30,4096]{2,1,0:T(8,128)}) fusion(f32[4,30,4096]{2,1,0:T(8,128)S(1)} %get-tuple-element.22, f32[30]{0:T(128)S(1)} %copy-done.8), kind=kLoop, calls=%fused_computation.14 | loop fusion | flops 1458176 | bytes 3997816 | tf_op jit(solution)/shard_map/vmap()/reduce_sum | solution.py:56
  71.1 1.6 %maximum_select_fusion = f32[4,31,4096]{2,1,0:T(8,128)} fusion(f32[4,1,4096]{2,1,0:T(1,128)S(1)} %get-tuple-element.28, f32[4,30,4096]{2,1,0:T(8,128)S(1)} %get-tuple-element.21, pred[4,4096]{1,0:T(4,128)(4,1)S(1)} %get-tuple-element.27), kind=kLoop, calls=%fused_computation.13 | loop fusion | flops 1015808 | bytes 4079616 | tf_op jit(solution)/shard_map/jit(_where)/select_n | solution.py:203
  72.8 1.5 %copy-done.1 = f32[30,16,1024]{2,1,0:T(8,128)S(1)} copy-done((f32[30,16,1024]{2,1,0:T(8,128)S(1)}, f32[30,16,1024]{2,1,0:T(8,128)}, u32[]{:S(2)}) %copy-start.1) | copy-done | bytes 1966104
  74.5 2.8 %collective-permute-start = (f32[31,1,1024]{2,1,0:T(1,128)S(1)}, f32[31,1,1024]{2,1,0:T(1,128)S(1)}, u32[]{:S(2)}, u32[]{:S(2)}) collective-permute-start(f32[31,1,1024]{2,1,0:T(1,128)S(1)} %get-tuple-element.35), channel_id=1, source_target_pairs={{1,0},{2,1},{3,2},{4,3},{5,4},{6,5},{7,6},{9,8},{10,9},{11,10},{12... | collective-permute-start | bytes 380936 | tf_op jit(solution)/shard_map/ppermute | solution.py:23
  77.3 3.9 %collective-permute-start.1 = (f32[31,1,1024]{2,1,0:T(1,128)S(1)}, f32[31,1,1024]{2,1,0:T(1,128)S(1)}, u32[]{:S(2)}, u32[]{:S(2)}) collective-permute-start(f32[31,1,1024]{2,1,0:T(1,128)S(1)} %get-tuple-element.34), channel_id=1, source_target_pairs={{0,1},{1,2},{2,3},{3,4},{4,5},{5,6},{6,7},{8,9},{9,10},{10,11},{11... | collective-permute-start | bytes 380936 | tf_op jit(solution)/shard_map/ppermute | solution.py:20
  82.3 3.2 %maximum_bitcast_fusion = f32[4,4096,31]{1,2,0:T(8,128)} fusion(f32[4,1,4096]{2,1,0:T(1,128)S(1)} %get-tuple-element.29, f32[4,30,4096]{2,1,0:T(8,128)} %get-tuple-element.31), kind=kLoop, calls=%fused_computation.12 | loop fusion | flops 507904 | bytes 4063232 | tf_op jit(solution)/shard_map/transpose | solution.py:211
  85.5 6.3 %copy.36 = f32[4,4096,31]{2,1,0:T(8,128)} copy(f32[4,4096,31]{1,2,0:T(8,128)} %maximum_bitcast_fusion) | data formatting | bytes 4063232 | tf_op jit(solution)/shard_map/reshape | solution.py:211
  91.8 21.9 %shard_map.122 = f32[16384,31]{1,0:T(8,128)} custom-call(s32[1]{0:T(128)} %bitcast.6.count_ref, s32[16384]{0:T(1024)} %get-tuple-element.6.dst_ref.src_ref, s32[16384]{0:T(1024)} %get-tuple-element.7.seg_ref, f32[16384,31]{1,0:T(8,128)} %bitcast.66), custom_call_target="tpu_custom_call" | custom-call | tf_op jit(solution)/shard_map/pallas_call | solution.py:140
  113.7 6.5 %copy.37 = f32[31,16,1024]{2,1,0:T(8,128)} copy(f32[31,16,1024]{0,2,1:T(8,128)} %bitcast.67) | data formatting | bytes 4063232 | tf_op jit(solution)/shard_map/reshape | solution.py:213
  120.1 2.0 %reduce-precision_convert_fusion.1 = (bf16[31,4096]{1,0:T(8,128)(2,1)S(1)}, bf16[31,4096]{1,0:T(8,128)(2,1)S(1)}, f32[31,4096]{1,0:T(8,128)}, bf16[31,4096]{1,0:T(8,128)(2,1)S(1)}) fusion(f32[1,31,4096]{2,1,0:T(8,128)} %reduce-scatter.2.cloned.1.call-done, pred[4096]{0:T(1024)(128)(4,1)S(1)} %get-tuple-element.45), kind=kLoop, calls=%fused_computation.53 | loop fusion | flops 1015808 | bytes 1781760 | tf_op jit(solution)/shard_map/convert.2
  122.1 6.9 %fusion = f32[93,2048]{1,0:T(8,128)S(1)} fusion(s32[4096]{0:T(1024)S(1)} %fusion.36, bf16[31,4096]{1,0:T(8,128)(2,1)S(1)} %get-tuple-element.37, bf16[31,4096]{1,0:T(8,128)(2,1)S(1)} %get-tuple-element.39, bf16[31,4096]{1,0:T(8,128)(2,1)S(1)} %get-tuple-element.36), kind=kOutput, calls=%fused_computation.2 | convolution fusion | flops 1570955264 | bytes 1540096 | tf_op jit(solution)/shard_map/dot_general | solution.py:76
  129.1 2.2 %collective-permute-start.5 = (f32[31,1024]{1,0:T(8,128)S(1)}, f32[31,1024]{1,0:T(8,128)S(1)}, u32[]{:S(2)}, u32[]{:S(2)}) collective-permute-start(f32[31,1024]{1,0:T(8,128)S(1)} %get-tuple-element.40), channel_id=1, source_target_pairs={{0,1},{1,2},{2,3},{3,4},{4,5},{5,6},{6,7},{8,9},{9,10},{10,11},{11... | collective-permute-start | bytes 380936 | tf_op jit(solution)/shard_map/ppermute | solution.py:31
  131.3 2.2 %collective-permute-start.6 = (f32[31,1024]{1,0:T(8,128)S(1)}, f32[31,1024]{1,0:T(8,128)S(1)}, u32[]{:S(2)}, u32[]{:S(2)}) collective-permute-start(f32[31,1024]{1,0:T(8,128)S(1)} %get-tuple-element.41), channel_id=1, source_target_pairs={{1,0},{2,1},{3,2},{4,3},{5,4},{6,5},{7,6},{9,8},{10,9},{11,10},{12... | collective-permute-start | bytes 380936 | tf_op jit(solution)/shard_map/ppermute | solution.py:31
  133.5 2.4 %fusion.9 = f32[31,16,1024]{2,1,0:T(8,128)} fusion(f32[31,16,1024]{2,1,0:T(8,128)S(1)} %copy-done.2, f32[31,1,1024]{2,1,0:T(1,128)S(1)} %collective-permute-done, f32[1,16,1024]{2,1,0:T(8,128)S(1)} %bitcast.78, f32[30,16,1024]{2,1,0:T(8,128)S(1)} %copy-done.1, f32[31,1,1024]{2,1,0:T(1,128)S(1)} %collective-permute-done.1), kind=kLoop, calls=%fused_computation.32 | loop fusion | flops 7110656 | bytes 6348800 | tf_op jit(solution)/shard_map/add | solution.py:214
  135.9 2.6 %collective-permute-done.6 = f32[31,1024]{1,0:T(8,128)S(1)} collective-permute-done((f32[31,1024]{1,0:T(8,128)S(1)}, f32[31,1024]{1,0:T(8,128)S(1)}, u32[]{:S(2)}, u32[]{:S(2)}) %collective-permute-start.6) | collective-permute-done | bytes 127008 | tf_op jit(solution)/shard_map/ppermute | solution.py:31
  (72 shorter events, 17.4 us)
Async XLA Ops:
  7.2 52.2 %all-gather.3.cloned.1.call-start = ((), (), s32[]{:S(2)}) async-start(), calls=%async_computation.2 | async-start | bytes 2621440 | tf_op jit(solution)/shard_map/all_gather | solution.py:177
  7.2 15.5 %collective-permute-start.2 = (s32[4096]{0:T(1024)}, s32[4096]{0:T(1024)S(1)}, u32[]{:S(2)}, u32[]{:S(2)}) collective-permute-start(s32[4096]{0:T(1024)} %param.14), channel_id=1, source_target_pairs={{0,8},{8,16},{16,24},{24,0},{1,9},{9,17},{17,25},{25,1},{2,10},{10... | collective-permute-start | bytes 49160 | tf_op jit(solution)/shard_map/ppermute | solution.py:151
  8.6 14.2 %collective-permute-start.3 = (s32[4096]{0:T(1024)}, s32[4096]{0:T(1024)S(1)}, u32[]{:S(2)}, u32[]{:S(2)}) collective-permute-start(s32[4096]{0:T(1024)} %param.14), channel_id=1, source_target_pairs={{0,16},{8,24},{16,0},{24,8},{1,17},{9,25},{17,1},{25,9},{2,18},{10... | collective-permute-start | bytes 49160 | tf_op jit(solution)/shard_map/ppermute | solution.py:151
  10.9 11.9 %collective-permute-start.4 = (s32[4096]{0:T(1024)}, s32[4096]{0:T(1024)S(1)}, u32[]{:S(2)}, u32[]{:S(2)}) collective-permute-start(s32[4096]{0:T(1024)} %param.14), channel_id=1, source_target_pairs={{0,24},{8,0},{16,8},{24,16},{1,25},{9,1},{17,9},{25,17},{2,26},{10... | collective-permute-start | bytes 49160 | tf_op jit(solution)/shard_map/ppermute | solution.py:151
  14.6 105.5 %reduce-scatter.2.cloned.1.call-start = ((), (), s32[]{:S(2)}) async-start(), calls=%async_computation.1 | async-start | bytes 2621440 | tf_op jit(solution)/shard_map/reduce_scatter | solution.py:204
  16.4 1.2 copy-start.3
  17.9 4.8 %copy-start.5 = (s32[4096]{0:T(1024)S(1)}, s32[4096]{0:T(1024)}, u32[]{:S(2)}) copy-start(s32[4096]{0:T(1024)} %param.14) | copy-start | bytes 49156
  58.4 3.4 %copy-start.6 = (f32[30]{0:T(128)S(1)}, f32[30]{0:T(128)}, u32[]{:S(2)}) copy-start(f32[30]{0:T(128)} %param.18) | copy-start | bytes 364
  58.5 3.4 %copy-start.7 = (f32[30]{0:T(128)S(1)}, f32[30]{0:T(128)}, u32[]{:S(2)}) copy-start(f32[30]{0:T(128)} %param.17) | copy-start | bytes 364
  59.4 2.2 %copy-start = (f32[128,4096]{1,0:T(8,128)S(1)}, f32[128,4096]{1,0:T(8,128)}, u32[]{:S(2)}) copy-start(f32[128,4096]{1,0:T(8,128)} %all-gather.3.cloned.1.call-done) | copy-start | bytes 6291460
  67.9 1.2 copy-start.8
  72.8 1.5 %copy-start.1 = (f32[30,16,1024]{2,1,0:T(8,128)S(1)}, f32[30,16,1024]{2,1,0:T(8,128)}, u32[]{:S(2)}) copy-start(f32[30,16,1024]{2,1,0:T(8,128)} %param.10) | copy-start | bytes 5898244
  72.8 8.5 %copy-start.4 = (s32[4096]{0:T(1024)S(1)}, s32[4096]{0:T(1024)}, u32[]{:S(2)}) copy-start(s32[4096]{0:T(1024)} %param.16) | copy-start | bytes 49156
  74.5 58.9 %collective-permute-start = (f32[31,1,1024]{2,1,0:T(1,128)S(1)}, f32[31,1,1024]{2,1,0:T(1,128)S(1)}, u32[]{:S(2)}, u32[]{:S(2)}) collective-permute-start(f32[31,1,1024]{2,1,0:T(1,128)S(1)} %get-tuple-element.35), channel_id=1, source_target_pairs={{1,0},{2,1},{3,2},{4,3},{5,4},{6,5},{7,6},{9,8},{10,9},{11,10},{12... | collective-permute-start | bytes 380936 | tf_op jit(solution)/shard_map/ppermute | solution.py:23
  77.3 56.1 %collective-permute-start.1 = (f32[31,1,1024]{2,1,0:T(1,128)S(1)}, f32[31,1,1024]{2,1,0:T(1,128)S(1)}, u32[]{:S(2)}, u32[]{:S(2)}) collective-permute-start(f32[31,1,1024]{2,1,0:T(1,128)S(1)} %get-tuple-element.34), channel_id=1, source_target_pairs={{0,1},{1,2},{2,3},{3,4},{4,5},{5,6},{6,7},{8,9},{9,10},{10,11},{11... | collective-permute-start | bytes 380936 | tf_op jit(solution)/shard_map/ppermute | solution.py:20
  122.1 11.4 %copy-start.2 = (f32[31,16,1024]{2,1,0:T(8,128)S(1)}, f32[31,16,1024]{2,1,0:T(8,128)}, u32[]{:S(2)}) copy-start(f32[31,16,1024]{2,1,0:T(8,128)} %copy.37) | copy-start | bytes 6094852
  129.1 6.8 %collective-permute-start.5 = (f32[31,1024]{1,0:T(8,128)S(1)}, f32[31,1024]{1,0:T(8,128)S(1)}, u32[]{:S(2)}, u32[]{:S(2)}) collective-permute-start(f32[31,1024]{1,0:T(8,128)S(1)} %get-tuple-element.40), channel_id=1, source_target_pairs={{0,1},{1,2},{2,3},{3,4},{4,5},{5,6},{6,7},{8,9},{9,10},{10,11},{11... | collective-permute-start | bytes 380936 | tf_op jit(solution)/shard_map/ppermute | solution.py:31
  131.3 7.2 %collective-permute-start.6 = (f32[31,1024]{1,0:T(8,128)S(1)}, f32[31,1024]{1,0:T(8,128)S(1)}, u32[]{:S(2)}, u32[]{:S(2)}) collective-permute-start(f32[31,1024]{1,0:T(8,128)S(1)} %get-tuple-element.41), channel_id=1, source_target_pairs={{1,0},{2,1},{3,2},{4,3},{5,4},{6,5},{7,6},{9,8},{10,9},{11,10},{12... | collective-permute-start | bytes 380936 | tf_op jit(solution)/shard_map/ppermute | solution.py:31
Sparse Core Ops, SparseCore 0:
  14.7 44.6 all-gather.2
  72.9 42.1 reduce-scatter.1

commit v13 on v12

--- a/solution.py
+++ b/solution.py
@@ -153,7 +153,7 @@
     ]
     stacked = jnp.stack(parts)
     where = (own - jnp.arange(count, dtype=jnp.int32)) % count
-    return jnp.take(stacked, where, axis=0).reshape(-1)
+    return jnp.take(stacked, where, axis=0)
 
 
 def field_major(x):
@@ -171,11 +171,10 @@
     sections = lax.axis_size("sect")
     own_sect = lax.axis_index("sect")
     plane = sections * width_yz
-    parcel_in = jnp.concatenate(
-        [masses, drop_temp[None], flags.astype(jnp.float32)[None]], axis=0
-    )
-    all_in = plane_major(lax.all_gather(field_major(parcel_in), "sect", axis=0, tiled=False))
-    all_cells = gather_sect(cells)
+    all_masses = plane_major(lax.all_gather(masses, "sect", axis=0, tiled=False))
+    side = jnp.stack([cells.astype(jnp.float32), drop_temp, flags.astype(jnp.float32)])
+    all_side = gather_sect(side)
+    all_cells = all_side[:, 0].reshape(-1).astype(jnp.int32)
     n_all = all_cells.shape[0]
     cell_row = all_cells // plane
     cell_col = all_cells % plane
@@ -189,7 +188,7 @@
     )
     count = jnp.sum(owned.astype(jnp.int32)).reshape(1)
     table = gas_block.reshape(fields, n_cells).T
-    blocks = all_in.shape[0]
+    blocks = all_masses.shape[0]
     owned_blocks = owned.reshape(blocks, 1, -1)
     gathered = row_gather(count, order, local_sorted, table)
     gathered = gathered.reshape(blocks, -1, fields).transpose(0, 2, 1)
@@ -197,7 +196,7 @@
     state_all, terms_all = jax.vmap(
         parcel_update, in_axes=(0, 0, 0, 0, 0, None, None, None)
     )(
-        all_in[:, :NC], all_in[:, NC], all_in[:, NC + 1], at_parcel[:, :NC], at_parcel[:, NC],
+        all_masses, all_side[:, 1], all_side[:, 2], at_parcel[:, :NC], at_parcel[:, NC],
         volat_a, volat_b, latent,
     )
     state_own = plane_major(jnp.where(owned_blocks, state_all, 0.0))

time: 147 us -> 146 us (level)
  other arithmetic: 36.4 us -> 34.9 us
    concatenate x1 -> x0, other arithmetic: 1.91 us -> none  [body(): jnp.concatenate([masses, drop_temp[None], flags.astype(jnp.float32)[None]...]
    select_n x1, other arithmetic: 1.81 us -> 0.22 us  [body(): at_parcel = plane_major(jnp.where(owned_blocks, gathered, 0.0))]
    unnamed x23 -> x26, local copies, waits for them, and re-layouts: 4.89 us -> 6.2 us
  transfers between devices with their start and end apart: 9 -> 9, of which waited for: 2 -> 2; matrix products, arithmetic and copies ran while one was open for 39% -> 36% of each run, Pallas kernels for 27% -> 27%
where the time goes in v13:
time: 146 us; the launch traced here: 145 us
  Pallas kernels  39.2 us (27%)
  other arithmetic  34.9 us (24%)
  local copies, waits for them, and re-layouts  30 us (21%)
  starting transfers between devices  15.8 us (11%)
  between operations  14.4 us (10%)
  matrix products  6.9 us (5%)
  waiting for transfers between devices  4.12 us (3%)
    pallas_call x1, Pallas kernels, row_scatter_add(): pl.pallas_call(_scatter_kernel, grid_spec=spec, out_shape=jax.ShapeDtypeS...  21.8 us
    pallas_call x1, Pallas kernels, row_gather(): pl.pallas_call(_gather_kernel, grid_spec=spec, out_shape=jax.ShapeDtypeSt...  17.4 us
    sort x1, other arithmetic, body(): lax.sort((keys, position, local_cell, seg), num_keys=1)  8.29 us
    dot_general x1, matrix products, pack_slots(): out = jnp.dot(parts, onehot, preferred_element_type=jnp.float32)  6.9 us
    reshape x1, local copies, waits for them, and re-layouts, body(): source = plane_major(summed.T.reshape(fields, width_x, width_yz))  6.46 us
    reshape x1, local copies, waits for them, and re-layouts, body(): terms_rows = terms_all.transpose(0, 2, 1).reshape(-1, fields)  6.3 us
    unnamed x26, local copies, waits for them, and re-layouts  6.2 us
    reduce_sum x4, other arithmetic, parcel_update(): slope = jnp.sum(part * excess * inv_denom, axis=0) + 0.1  5.83 us
  transfers between devices with their start and end apart: 9, of which 2 were waited for; matrix products, arithmetic and copies ran while one was open for 36% of the time, Pallas kernels for 27%

profile of v13, /device:TPU:3, one launch (start us, length us, event | category | flops | bytes accessed | tf_op | source)
XLA Modules:
  0.0 145.4 jit_solution(18231760712484895883)
XLA Ops:
  10.8 2.3 %collective-permute-start.3 = (f32[3,4096]{1,0:T(4,128)S(1)}, f32[3,4096]{1,0:T(4,128)S(1)}, u32[]{:S(2)}, u32[]{:S(2)}) collective-permute-start(f32[3,4096]{1,0:T(4,128)S(1)} %get-tuple-element.43), channel_id=1, source_target_pairs={{0,16},{8,24},{16,0},{24,8},{1,17},{9,25},{17,1},{25,9},{2,18},{10... | collective-permute-start | bytes 147464 | tf_op jit(solution)/shard_map/ppermute | solution.py:151
  14.3 1.7 %pad.33 = f32[32,16,1024]{2,1,0:T(8,128)S(1)} pad(f32[30,16,1024]{2,1,0:T(8,128)} %param.10, f32[]{:T(128)} %constant.119.clone.1), padding=0_2x0_0x0_0 | pad | bytes 4063236
  17.5 4.8 %copy.24 = f32[31,16384]{0,1:T(8,128)} copy(f32[31,16384]{1,0:T(8,128)S(1)} %pad_maximum_fusion.1) | data formatting | bytes 4063232 | tf_op jit(solution)/shard_map/concatenate | solution.py:168
  23.5 8.3 %sort.27 = (s32[16384]{0:T(1024)}, s32[16384]{0:T(1024)}, s32[16384]{0:T(1024)}, s32[16384]{0:T(1024)}) sort(s32[16384]{0:T(1024)S(1)} %iota_add_fusion, s32[16384]{0:T(1024)S(1)} %iota.18, s32[16384]{0:T(1024)S(1)} %get-tuple-element.24, s32[16384]{0:T(1024)S(1)} %get-tuple-element.23), dimensions={0}, to_apply=%region_1.2 | sort | flops 229376 | bytes 524288 | tf_op jit(solution)/shard_map/sort | solution.py:186
  33.0 17.4 %shard_map.121 = f32[16384,31]{1,0:T(8,128)} custom-call(s32[1]{0:T(128)} %bitcast.9.count_ref, s32[16384]{0:T(1024)} %get-tuple-element.6.dst_ref.src_ref, s32[16384]{0:T(1024)} %get-tuple-element.8.src_ref, f32[16384,31]{1,0:T(8,128)} %bitcast.59), custom_call_target="tpu_custom_call" | custom-call | tf_op jit(solution)/shard_map/pallas_call | solution.py:124
  50.4 5.2 %copy.26 = f32[4,4096,31]{1,2,0:T(8,128)S(1)} copy(f32[4,4096,31]{2,1,0:T(8,128)} %bitcast.62) | data formatting | bytes 4063232 | tf_op jit(solution)/shard_map/reshape | solution.py:194
  57.5 1.5 %all-gather.4.cloned.1.call-done = f32[4,30,4096]{2,1,0:T(8,128)} async-done(((f32[1,30,4096]{2,1,0:T(8,128)}), f32[4,30,4096]{2,1,0:T(8,128)}) %all-gather.4.cloned.1.call-update) | async-done | bytes 1966096 | tf_op jit(solution)/shard_map/all_gather | solution.py:174
  59.0 2.0 %reduce_sum.102 = f32[4,4096]{1,0:T(4,128)S(1)} reduce(f32[4,30,4096]{2,1,0:T(8,128)} %all-gather.4.cloned.1.call-done, f32[]{:T(128)} %constant.119.clone.1), dimensions={1}, to_apply=%region_2.3 | reduce | flops 475136 | bytes 2031620 | tf_op jit(solution)/shard_map/vmap()/reduce_sum | solution.py:35
  62.7 1.5 %multiply_reduce_fusion.3 = (f32[4,4096]{1,0:T(4,128)S(1)}, f32[4,4096]{1,0:T(4,128)S(1)}) fusion(f32[4,4096]{1,0:T(4,128)S(1)} %add_clamp_fusion.3, f32[4,4096]{1,0:T(4,128)S(1)} %bitcast.66, f32[30]{0:T(128)S(1)} %copy-done.7, f32[30]{0:T(128)S(1)} %copy-done.8, f32[4,30,4096]{2,1,0:T(8,128)S(1)} %copy-done, f32[4,4096]{1,0:T(4,128)S(1)} %get-tuple-element.41), kind=kLoop, calls=%fused_computation.19 | loop fusion | flops 6356992 | bytes 2294000 | tf_op jit(solution)/shard_map/vmap()/reduce_sum | solution.py:47
  68.6 1.7 %multiply_reduce_fusion = (f32[4,4096]{1,0:T(4,128)S(1)}, f32[4,30,4096]{2,1,0:T(8,128)}) fusion(f32[4,30,4096]{2,1,0:T(8,128)S(1)} %get-tuple-element.22, f32[30]{0:T(128)S(1)} %copy-done.9), kind=kLoop, calls=%fused_computation.14 | loop fusion | flops 1458176 | bytes 3997816 | tf_op jit(solution)/shard_map/vmap()/reduce_sum | solution.py:56
  70.6 1.6 %maximum_select_fusion = f32[4,31,4096]{2,1,0:T(8,128)} fusion(f32[4,1,4096]{2,1,0:T(1,128)S(1)} %get-tuple-element.28, f32[4,30,4096]{2,1,0:T(8,128)S(1)} %get-tuple-element.21, pred[4,4096]{1,0:T(4,128)(4,1)S(1)} %bitcast.78), kind=kLoop, calls=%fused_computation.13 | loop fusion | flops 1015808 | bytes 4079616 | tf_op jit(solution)/shard_map/jit(_where)/select_n | solution.py:202
  72.2 1.5 %copy-done.1 = f32[30,16,1024]{2,1,0:T(8,128)S(1)} copy-done((f32[30,16,1024]{2,1,0:T(8,128)S(1)}, f32[30,16,1024]{2,1,0:T(8,128)}, u32[]{:S(2)}) %copy-start.1) | copy-done | bytes 1966104
  74.0 2.7 %collective-permute-start = (f32[31,1,1024]{2,1,0:T(1,128)S(1)}, f32[31,1,1024]{2,1,0:T(1,128)S(1)}, u32[]{:S(2)}, u32[]{:S(2)}) collective-permute-start(f32[31,1,1024]{2,1,0:T(1,128)S(1)} %get-tuple-element.33), channel_id=1, source_target_pairs={{1,0},{2,1},{3,2},{4,3},{5,4},{6,5},{7,6},{9,8},{10,9},{11,10},{12... | collective-permute-start | bytes 380936 | tf_op jit(solution)/shard_map/ppermute | solution.py:23
  76.7 3.9 %collective-permute-start.1 = (f32[31,1,1024]{2,1,0:T(1,128)S(1)}, f32[31,1,1024]{2,1,0:T(1,128)S(1)}, u32[]{:S(2)}, u32[]{:S(2)}) collective-permute-start(f32[31,1,1024]{2,1,0:T(1,128)S(1)} %get-tuple-element.32), channel_id=1, source_target_pairs={{0,1},{1,2},{2,3},{3,4},{4,5},{5,6},{6,7},{8,9},{9,10},{10,11},{11... | collective-permute-start | bytes 380936 | tf_op jit(solution)/shard_map/ppermute | solution.py:20
  81.7 3.2 %maximum_bitcast_fusion = f32[4,4096,31]{1,2,0:T(8,128)} fusion(f32[4,1,4096]{2,1,0:T(1,128)S(1)} %get-tuple-element.29, f32[4,30,4096]{2,1,0:T(8,128)} %get-tuple-element.31), kind=kLoop, calls=%fused_computation.12 | loop fusion | flops 507904 | bytes 4063232 | tf_op jit(solution)/shard_map/transpose | solution.py:210
  85.0 6.3 %copy.33 = f32[4,4096,31]{2,1,0:T(8,128)} copy(f32[4,4096,31]{1,2,0:T(8,128)} %maximum_bitcast_fusion) | data formatting | bytes 4063232 | tf_op jit(solution)/shard_map/reshape | solution.py:210
  91.2 21.8 %shard_map.122 = f32[16384,31]{1,0:T(8,128)} custom-call(s32[1]{0:T(128)} %bitcast.9.count_ref, s32[16384]{0:T(1024)} %get-tuple-element.6.dst_ref.src_ref, s32[16384]{0:T(1024)} %get-tuple-element.7.seg_ref, f32[16384,31]{1,0:T(8,128)} %bitcast.60), custom_call_target="tpu_custom_call" | custom-call | tf_op jit(solution)/shard_map/pallas_call | solution.py:140
  113.0 6.5 %copy.34 = f32[31,16,1024]{2,1,0:T(8,128)} copy(f32[31,16,1024]{0,2,1:T(8,128)} %bitcast.61) | data formatting | bytes 4063232 | tf_op jit(solution)/shard_map/reshape | solution.py:212
  119.5 2.0 %reduce-precision_convert_fusion.1 = (bf16[31,4096]{1,0:T(8,128)(2,1)S(1)}, bf16[31,4096]{1,0:T(8,128)(2,1)S(1)}, f32[31,4096]{1,0:T(8,128)}, bf16[31,4096]{1,0:T(8,128)(2,1)S(1)}) fusion(f32[1,31,4096]{2,1,0:T(8,128)} %reduce-scatter.2.cloned.1.call-done, pred[4096]{0:T(1024)(128)(4,1)S(1)} %get-tuple-element.44), kind=kLoop, calls=%fused_computation.51 | loop fusion | flops 1015808 | bytes 1781760 | tf_op jit(solution)/shard_map/convert.2
  121.5 6.9 %fusion = f32[93,2048]{1,0:T(8,128)S(1)} fusion(s32[4096]{0:T(1024)S(1)} %fusion.33, bf16[31,4096]{1,0:T(8,128)(2,1)S(1)} %get-tuple-element.35, bf16[31,4096]{1,0:T(8,128)(2,1)S(1)} %get-tuple-element.37, bf16[31,4096]{1,0:T(8,128)(2,1)S(1)} %get-tuple-element.34), kind=kOutput, calls=%fused_computation.2 | convolution fusion | flops 1570955264 | bytes 1540096 | tf_op jit(solution)/shard_map/dot_general | solution.py:76
  128.5 2.2 %collective-permute-start.5 = (f32[31,1024]{1,0:T(8,128)S(1)}, f32[31,1024]{1,0:T(8,128)S(1)}, u32[]{:S(2)}, u32[]{:S(2)}) collective-permute-start(f32[31,1024]{1,0:T(8,128)S(1)} %get-tuple-element.38), channel_id=1, source_target_pairs={{0,1},{1,2},{2,3},{3,4},{4,5},{5,6},{6,7},{8,9},{9,10},{10,11},{11... | collective-permute-start | bytes 380936 | tf_op jit(solution)/shard_map/ppermute | solution.py:31
  130.7 2.1 %collective-permute-start.6 = (f32[31,1024]{1,0:T(8,128)S(1)}, f32[31,1024]{1,0:T(8,128)S(1)}, u32[]{:S(2)}, u32[]{:S(2)}) collective-permute-start(f32[31,1024]{1,0:T(8,128)S(1)} %get-tuple-element.39), channel_id=1, source_target_pairs={{1,0},{2,1},{3,2},{4,3},{5,4},{6,5},{7,6},{9,8},{10,9},{11,10},{12... | collective-permute-start | bytes 380936 | tf_op jit(solution)/shard_map/ppermute | solution.py:31
  132.9 2.4 %fusion.9 = f32[31,16,1024]{2,1,0:T(8,128)} fusion(f32[31,16,1024]{2,1,0:T(8,128)S(1)} %copy-done.4, f32[31,1,1024]{2,1,0:T(1,128)S(1)} %collective-permute-done, f32[1,16,1024]{2,1,0:T(8,128)S(1)} %bitcast.72, f32[30,16,1024]{2,1,0:T(8,128)S(1)} %copy-done.1, f32[31,1,1024]{2,1,0:T(1,128)S(1)} %collective-permute-done.1), kind=kLoop, calls=%fused_computation.32 | loop fusion | flops 7110656 | bytes 6348800 | tf_op jit(solution)/shard_map/add | solution.py:213
  135.2 2.6 %collective-permute-done.6 = f32[31,1024]{1,0:T(8,128)S(1)} collective-permute-done((f32[31,1024]{1,0:T(8,128)S(1)}, f32[31,1024]{1,0:T(8,128)S(1)}, u32[]{:S(2)}, u32[]{:S(2)}) %collective-permute-start.6) | collective-permute-done | bytes 127008 | tf_op jit(solution)/shard_map/ppermute | solution.py:31
  (79 shorter events, 18.7 us)
Async XLA Ops:
  7.2 51.8 %all-gather.4.cloned.1.call-start = ((), (), s32[]{:S(2)}) async-start(), calls=%async_computation.2 | async-start | bytes 2621440 | tf_op jit(solution)/shard_map/all_gather | solution.py:174
  9.4 12.9 %collective-permute-start.2 = (f32[3,4096]{1,0:T(4,128)S(1)}, f32[3,4096]{1,0:T(4,128)S(1)}, u32[]{:S(2)}, u32[]{:S(2)}) collective-permute-start(f32[3,4096]{1,0:T(4,128)S(1)} %get-tuple-element.43), channel_id=1, source_target_pairs={{0,8},{8,16},{16,24},{24,0},{1,9},{9,17},{17,25},{25,1},{2,10},{10... | collective-permute-start | bytes 147464 | tf_op jit(solution)/shard_map/ppermute | solution.py:151
  10.8 11.5 %collective-permute-start.3 = (f32[3,4096]{1,0:T(4,128)S(1)}, f32[3,4096]{1,0:T(4,128)S(1)}, u32[]{:S(2)}, u32[]{:S(2)}) collective-permute-start(f32[3,4096]{1,0:T(4,128)S(1)} %get-tuple-element.43), channel_id=1, source_target_pairs={{0,16},{8,24},{16,0},{24,8},{1,17},{9,25},{17,1},{25,9},{2,18},{10... | collective-permute-start | bytes 147464 | tf_op jit(solution)/shard_map/ppermute | solution.py:151
  13.1 9.2 %collective-permute-start.4 = (f32[3,4096]{1,0:T(4,128)S(1)}, f32[3,4096]{1,0:T(4,128)S(1)}, u32[]{:S(2)}, u32[]{:S(2)}) collective-permute-start(f32[3,4096]{1,0:T(4,128)S(1)} %get-tuple-element.43), channel_id=1, source_target_pairs={{0,24},{8,0},{16,8},{24,16},{1,25},{9,1},{17,9},{25,17},{2,26},{10... | collective-permute-start | bytes 147464 | tf_op jit(solution)/shard_map/ppermute | solution.py:151
  14.2 105.3 %reduce-scatter.2.cloned.1.call-start = ((), (), s32[]{:S(2)}) async-start(), calls=%async_computation.1 | async-start | bytes 2621440 | tf_op jit(solution)/shard_map/reduce_scatter | solution.py:203
  16.0 1.2 copy-start.5
  56.0 1.4 copy-start.2
  57.3 3.7 %copy-start.7 = (f32[30]{0:T(128)S(1)}, f32[30]{0:T(128)}, u32[]{:S(2)}) copy-start(f32[30]{0:T(128)} %param.18) | copy-start | bytes 364
  57.3 3.7 %copy-start.8 = (f32[30]{0:T(128)S(1)}, f32[30]{0:T(128)}, u32[]{:S(2)}) copy-start(f32[30]{0:T(128)} %param.17) | copy-start | bytes 364
  59.0 2.2 %copy-start = (f32[4,30,4096]{2,1,0:T(8,128)S(1)}, f32[4,30,4096]{2,1,0:T(8,128)}, u32[]{:S(2)}) copy-start(f32[4,30,4096]{2,1,0:T(8,128)} %all-gather.4.cloned.1.call-done) | copy-start | bytes 5898244
  65.7 1.7 %copy-start.3 = (f32[4,31,4096]{2,1,0:T(8,128)S(1)}, f32[4,31,4096]{2,1,0:T(8,128)}, u32[]{:S(2)}) copy-start(f32[4,31,4096]{2,1,0:T(8,128)} %copy-done.2) | copy-start | bytes 6094852
  67.4 1.2 copy-start.9
  72.2 1.5 %copy-start.1 = (f32[30,16,1024]{2,1,0:T(8,128)S(1)}, f32[30,16,1024]{2,1,0:T(8,128)}, u32[]{:S(2)}) copy-start(f32[30,16,1024]{2,1,0:T(8,128)} %param.10) | copy-start | bytes 5898244
  72.2 8.5 %copy-start.6 = (s32[4096]{0:T(1024)S(1)}, s32[4096]{0:T(1024)}, u32[]{:S(2)}) copy-start(s32[4096]{0:T(1024)} %param.16) | copy-start | bytes 49156
  74.0 58.8 %collective-permute-start = (f32[31,1,1024]{2,1,0:T(1,128)S(1)}, f32[31,1,1024]{2,1,0:T(1,128)S(1)}, u32[]{:S(2)}, u32[]{:S(2)}) collective-permute-start(f32[31,1,1024]{2,1,0:T(1,128)S(1)} %get-tuple-element.33), channel_id=1, source_target_pairs={{1,0},{2,1},{3,2},{4,3},{5,4},{6,5},{7,6},{9,8},{10,9},{11,10},{12... | collective-permute-start | bytes 380936 | tf_op jit(solution)/shard_map/ppermute | solution.py:23
  76.7 56.1 %collective-permute-start.1 = (f32[31,1,1024]{2,1,0:T(1,128)S(1)}, f32[31,1,1024]{2,1,0:T(1,128)S(1)}, u32[]{:S(2)}, u32[]{:S(2)}) collective-permute-start(f32[31,1,1024]{2,1,0:T(1,128)S(1)} %get-tuple-element.32), channel_id=1, source_target_pairs={{0,1},{1,2},{2,3},{3,4},{4,5},{5,6},{6,7},{8,9},{9,10},{10,11},{11... | collective-permute-start | bytes 380936 | tf_op jit(solution)/shard_map/ppermute | solution.py:20
  121.5 11.4 %copy-start.4 = (f32[31,16,1024]{2,1,0:T(8,128)S(1)}, f32[31,16,1024]{2,1,0:T(8,128)}, u32[]{:S(2)}) copy-start(f32[31,16,1024]{2,1,0:T(8,128)} %copy.34) | copy-start | bytes 6094852
  128.5 6.8 %collective-permute-start.5 = (f32[31,1024]{1,0:T(8,128)S(1)}, f32[31,1024]{1,0:T(8,128)S(1)}, u32[]{:S(2)}, u32[]{:S(2)}) collective-permute-start(f32[31,1024]{1,0:T(8,128)S(1)} %get-tuple-element.38), channel_id=1, source_target_pairs={{0,1},{1,2},{2,3},{3,4},{4,5},{5,6},{6,7},{8,9},{9,10},{10,11},{11... | collective-permute-start | bytes 380936 | tf_op jit(solution)/shard_map/ppermute | solution.py:31
  130.7 7.2 %collective-permute-start.6 = (f32[31,1024]{1,0:T(8,128)S(1)}, f32[31,1024]{1,0:T(8,128)S(1)}, u32[]{:S(2)}, u32[]{:S(2)}) collective-permute-start(f32[31,1024]{1,0:T(8,128)S(1)} %get-tuple-element.39), channel_id=1, source_target_pairs={{1,0},{2,1},{3,2},{4,3},{5,4},{6,5},{7,6},{9,8},{10,9},{11,10},{12... | collective-permute-start | bytes 380936 | tf_op jit(solution)/shard_map/ppermute | solution.py:31
Sparse Core Ops, SparseCore 0:
  14.3 44.6 all-gather.3
  72.4 42.1 reduce-scatter.1

commit v14 on v13

--- a/solution.py
+++ b/solution.py
@@ -212,7 +212,8 @@
     source = plane_major(summed.T.reshape(fields, width_x, width_yz))
     gas_next = plane_major(flowed + source)
     kept = jnp.where(moves[None] == 0, state, 0.0)
-    rightward, leftward = pack_slots(state, (moves == 2, moves == 1))
+    state_ready = state + 0.0 * gas_next[0, 0, 0]
+    rightward, leftward = pack_slots(state_ready, (moves == 2, moves == 1))
     from_prev = shifted(rightward, "slab", 1)
     from_next = shifted(leftward, "slab", -1)
     arrivals = jnp.concatenate([from_prev, from_next], axis=1)

time: 146 us -> 152 us (1.041)
  waiting for transfers between devices: 4.12 us -> 6.17 us
  local copies, waits for them, and re-layouts: 30 us -> 31.8 us
    ppermute x2, waiting for transfers between devices: 2.61 us -> 4.82 us  [shifted(): return lax.ppermute(shard, axis, pairs)]
  transfers between devices with their start and end apart: 9 -> 9, of which waited for: 2 -> 2; matrix products, arithmetic and copies ran while one was open for 36% -> 30% of each run, Pallas kernels for 27% -> 26%
where the time goes in v14:
time: 152 us; the launch traced here: 151 us
  Pallas kernels  39.7 us (26%)
  other arithmetic  35.2 us (23%)
  local copies, waits for them, and re-layouts  31.8 us (21%)
  starting transfers between devices  15.8 us (10%)
  between operations  15.1 us (10%)
  matrix products  6.91 us (5%)
  waiting for transfers between devices  6.17 us (4%)
    pallas_call x1, Pallas kernels, row_scatter_add(): pl.pallas_call(_scatter_kernel, grid_spec=spec, out_shape=jax.ShapeDtypeS...  22.1 us
    pallas_call x1, Pallas kernels, row_gather(): pl.pallas_call(_gather_kernel, grid_spec=spec, out_shape=jax.ShapeDtypeSt...  17.6 us
    sort x1, other arithmetic, body(): lax.sort((keys, position, local_cell, seg), num_keys=1)  8.29 us
    unnamed x26, local copies, waits for them, and re-layouts  7.48 us
    dot_general x1, matrix products, pack_slots(): out = jnp.dot(parts, onehot, preferred_element_type=jnp.float32)  6.91 us
    reshape x1, local copies, waits for them, and re-layouts, body(): source = plane_major(summed.T.reshape(fields, width_x, width_yz))  6.48 us
    reshape x1, local copies, waits for them, and re-layouts, body(): terms_rows = terms_all.transpose(0, 2, 1).reshape(-1, fields)  6.3 us
    reduce_sum x4, other arithmetic, parcel_update(): slope = jnp.sum(part * excess * inv_denom, axis=0) + 0.1  5.83 us
  transfers between devices with their start and end apart: 9, of which 2 were waited for; matrix products, arithmetic and copies ran while one was open for 30% of the time, Pallas kernels for 26%

profile of v14, /device:TPU:3, one launch (start us, length us, event | category | flops | bytes accessed | tf_op | source)
XLA Modules:
  0.0 150.7 jit_solution(7853996679429750758)
XLA Ops:
  10.8 2.3 %collective-permute-start.3 = (f32[3,4096]{1,0:T(4,128)S(1)}, f32[3,4096]{1,0:T(4,128)S(1)}, u32[]{:S(2)}, u32[]{:S(2)}) collective-permute-start(f32[3,4096]{1,0:T(4,128)S(1)} %get-tuple-element.43), channel_id=1, source_target_pairs={{0,16},{8,24},{16,0},{24,8},{1,17},{9,25},{17,1},{25,9},{2,18},{10... | collective-permute-start | bytes 147464 | tf_op jit(solution)/shard_map/ppermute | solution.py:151
  14.3 1.7 %pad.33 = f32[32,16,1024]{2,1,0:T(8,128)S(1)} pad(f32[30,16,1024]{2,1,0:T(8,128)} %param.10, f32[]{:T(128)} %constant.120.clone.1), padding=0_2x0_0x0_0 | pad | bytes 4063236
  17.5 4.8 %copy.24 = f32[31,16384]{0,1:T(8,128)} copy(f32[31,16384]{1,0:T(8,128)S(1)} %pad_maximum_fusion.1) | data formatting | bytes 4063232 | tf_op jit(solution)/shard_map/concatenate | solution.py:168
  23.5 8.3 %sort.27 = (s32[16384]{0:T(1024)}, s32[16384]{0:T(1024)}, s32[16384]{0:T(1024)}, s32[16384]{0:T(1024)}) sort(s32[16384]{0:T(1024)S(1)} %iota_add_fusion, s32[16384]{0:T(1024)S(1)} %iota.18, s32[16384]{0:T(1024)S(1)} %get-tuple-element.24, s32[16384]{0:T(1024)S(1)} %get-tuple-element.23), dimensions={0}, to_apply=%region_1.2 | sort | flops 229376 | bytes 524288 | tf_op jit(solution)/shard_map/sort | solution.py:186
  33.0 17.6 %shard_map.121 = f32[16384,31]{1,0:T(8,128)} custom-call(s32[1]{0:T(128)} %bitcast.9.count_ref, s32[16384]{0:T(1024)} %get-tuple-element.6.dst_ref.src_ref, s32[16384]{0:T(1024)} %get-tuple-element.8.src_ref, f32[16384,31]{1,0:T(8,128)} %bitcast.63), custom_call_target="tpu_custom_call" | custom-call | tf_op jit(solution)/shard_map/pallas_call | solution.py:124
  50.6 5.2 %copy.26 = f32[4,4096,31]{1,2,0:T(8,128)S(1)} copy(f32[4,4096,31]{2,1,0:T(8,128)} %bitcast.66) | data formatting | bytes 4063232 | tf_op jit(solution)/shard_map/reshape | solution.py:194
  59.0 2.0 %reduce_sum.102 = f32[4,4096]{1,0:T(4,128)S(1)} reduce(f32[4,30,4096]{2,1,0:T(8,128)} %all-gather.4.cloned.1.call-done, f32[]{:T(128)} %constant.120.clone.1), dimensions={1}, to_apply=%region_2.3 | reduce | flops 475136 | bytes 2031620 | tf_op jit(solution)/shard_map/vmap()/reduce_sum | solution.py:35
  62.7 1.5 multiply_reduce_fusion.3
  64.2 1.5 multiply_reduce_fusion.2
  68.6 1.7 %multiply_reduce_fusion = (f32[4,4096]{1,0:T(4,128)S(1)}, f32[4,30,4096]{2,1,0:T(8,128)}) fusion(f32[4,30,4096]{2,1,0:T(8,128)S(1)} %get-tuple-element.22, f32[30]{0:T(128)S(1)} %copy-done.9), kind=kLoop, calls=%fused_computation.14 | loop fusion | flops 1458176 | bytes 3997816 | tf_op jit(solution)/shard_map/vmap()/reduce_sum | solution.py:56
  70.6 1.6 %maximum_select_fusion = f32[4,31,4096]{2,1,0:T(8,128)} fusion(f32[4,1,4096]{2,1,0:T(1,128)S(1)} %get-tuple-element.28, f32[4,30,4096]{2,1,0:T(8,128)S(1)} %get-tuple-element.21, pred[4,4096]{1,0:T(4,128)(4,1)S(1)} %bitcast.82), kind=kLoop, calls=%fused_computation.13 | loop fusion | flops 1015808 | bytes 4079616 | tf_op jit(solution)/shard_map/jit(_where)/select_n | solution.py:202
  72.2 1.5 %copy-done.1 = f32[30,16,1024]{2,1,0:T(8,128)S(1)} copy-done((f32[30,16,1024]{2,1,0:T(8,128)S(1)}, f32[30,16,1024]{2,1,0:T(8,128)}, u32[]{:S(2)}) %copy-start.1) | copy-done | bytes 1966104
  74.0 2.7 %collective-permute-start = (f32[31,1,1024]{2,1,0:T(1,128)S(1)}, f32[31,1,1024]{2,1,0:T(1,128)S(1)}, u32[]{:S(2)}, u32[]{:S(2)}) collective-permute-start(f32[31,1,1024]{2,1,0:T(1,128)S(1)} %get-tuple-element.33), channel_id=1, source_target_pairs={{1,0},{2,1},{3,2},{4,3},{5,4},{6,5},{7,6},{9,8},{10,9},{11,10},{12... | collective-permute-start | bytes 380936 | tf_op jit(solution)/shard_map/ppermute | solution.py:23
  76.7 3.9 %collective-permute-start.1 = (f32[31,1,1024]{2,1,0:T(1,128)S(1)}, f32[31,1,1024]{2,1,0:T(1,128)S(1)}, u32[]{:S(2)}, u32[]{:S(2)}) collective-permute-start(f32[31,1,1024]{2,1,0:T(1,128)S(1)} %get-tuple-element.32), channel_id=1, source_target_pairs={{0,1},{1,2},{2,3},{3,4},{4,5},{5,6},{6,7},{8,9},{9,10},{10,11},{11... | collective-permute-start | bytes 380936 | tf_op jit(solution)/shard_map/ppermute | solution.py:20
  81.7 3.2 %maximum_bitcast_fusion = f32[4,4096,31]{1,2,0:T(8,128)} fusion(f32[4,1,4096]{2,1,0:T(1,128)S(1)} %get-tuple-element.29, f32[4,30,4096]{2,1,0:T(8,128)} %get-tuple-element.31), kind=kLoop, calls=%fused_computation.12 | loop fusion | flops 507904 | bytes 4063232 | tf_op jit(solution)/shard_map/transpose | solution.py:210
  85.0 6.3 %copy.33 = f32[4,4096,31]{2,1,0:T(8,128)} copy(f32[4,4096,31]{1,2,0:T(8,128)} %maximum_bitcast_fusion) | data formatting | bytes 4063232 | tf_op jit(solution)/shard_map/reshape | solution.py:210
  91.2 22.1 %shard_map.122 = f32[16384,31]{1,0:T(8,128)} custom-call(s32[1]{0:T(128)} %bitcast.9.count_ref, s32[16384]{0:T(1024)} %get-tuple-element.6.dst_ref.src_ref, s32[16384]{0:T(1024)} %get-tuple-element.7.seg_ref, f32[16384,31]{1,0:T(8,128)} %bitcast.64), custom_call_target="tpu_custom_call" | custom-call | tf_op jit(solution)/shard_map/pallas_call | solution.py:140
  113.3 6.5 %copy.34 = f32[31,16,1024]{2,1,0:T(8,128)} copy(f32[31,16,1024]{0,2,1:T(8,128)} %bitcast.65) | data formatting | bytes 4063232 | tf_op jit(solution)/shard_map/reshape | solution.py:212
  119.8 2.7 %fusion.9 = f32[31,16,1024]{2,1,0:T(8,128)S(1)} fusion(f32[31,16,1024]{2,1,0:T(8,128)} %copy.34, f32[31,1,1024]{2,1,0:T(1,128)S(1)} %collective-permute-done, f32[1,16,1024]{2,1,0:T(8,128)S(1)} %bitcast.76, f32[30,16,1024]{2,1,0:T(8,128)S(1)} %copy-done.1, f32[31,1,1024]{2,1,0:T(1,128)S(1)} %collective-permute-done.1), kind=kLoop, calls=%fused_computation.32 | loop fusion | flops 7110656 | bytes 6348800 | tf_op jit(solution)/shard_map/add | solution.py:213
  125.0 2.0 %reduce-precision_convert_fusion.1 = (bf16[31,4096]{1,0:T(8,128)(2,1)S(1)}, bf16[31,4096]{1,0:T(8,128)(2,1)S(1)}, bf16[31,4096]{1,0:T(8,128)(2,1)S(1)}, f32[31,4096]{1,0:T(8,128)}) fusion(f32[1,31,4096]{2,1,0:T(8,128)} %reduce-scatter.2.cloned.1.call-done, f32[]{:T(128)} %bitcast.21, pred[4096]{0:T(1024)(128)(4,1)S(1)} %get-tuple-element.44), kind=kLoop, calls=%fused_computation.51 | loop fusion | flops 1142784 | bytes 1781764 | tf_op jit(solution)/shard_map/convert.2
  126.9 6.9 %fusion = f32[93,2048]{1,0:T(8,128)S(1)} fusion(s32[4096]{0:T(1024)S(1)} %fusion.33, bf16[31,4096]{1,0:T(8,128)(2,1)S(1)} %get-tuple-element.35, bf16[31,4096]{1,0:T(8,128)(2,1)S(1)} %get-tuple-element.36, bf16[31,4096]{1,0:T(8,128)(2,1)S(1)} %get-tuple-element.34), kind=kOutput, calls=%fused_computation.2 | convolution fusion | flops 1570955264 | bytes 1540096 | tf_op jit(solution)/shard_map/dot_general | solution.py:76
  134.0 2.0 %collective-permute-start.5 = (f32[31,1024]{1,0:T(8,128)S(1)}, f32[31,1024]{1,0:T(8,128)S(1)}, u32[]{:S(2)}, u32[]{:S(2)}) collective-permute-start(f32[31,1024]{1,0:T(8,128)S(1)} %get-tuple-element.38), channel_id=1, source_target_pairs={{0,1},{1,2},{2,3},{3,4},{4,5},{5,6},{6,7},{8,9},{9,10},{10,11},{11... | collective-permute-start | bytes 380936 | tf_op jit(solution)/shard_map/ppermute | solution.py:31
  135.9 2.3 %collective-permute-start.6 = (f32[31,1024]{1,0:T(8,128)S(1)}, f32[31,1024]{1,0:T(8,128)S(1)}, u32[]{:S(2)}, u32[]{:S(2)}) collective-permute-start(f32[31,1024]{1,0:T(8,128)S(1)} %get-tuple-element.39), channel_id=1, source_target_pairs={{1,0},{2,1},{3,2},{4,3},{5,4},{6,5},{7,6},{9,8},{10,9},{11,10},{12... | collective-permute-start | bytes 380936 | tf_op jit(solution)/shard_map/ppermute | solution.py:31
  138.3 4.8 %collective-permute-done.6 = f32[31,1024]{1,0:T(8,128)S(1)} collective-permute-done((f32[31,1024]{1,0:T(8,128)S(1)}, f32[31,1024]{1,0:T(8,128)S(1)}, u32[]{:S(2)}, u32[]{:S(2)}) %collective-permute-start.6) | collective-permute-done | bytes 127008 | tf_op jit(solution)/shard_map/ppermute | solution.py:31
  (80 shorter events, 20.4 us)
Async XLA Ops:
  7.2 51.8 %all-gather.4.cloned.1.call-start = ((), (), s32[]{:S(2)}) async-start(), calls=%async_computation.2 | async-start | bytes 2621440 | tf_op jit(solution)/shard_map/all_gather | solution.py:174
  9.4 12.9 %collective-permute-start.2 = (f32[3,4096]{1,0:T(4,128)S(1)}, f32[3,4096]{1,0:T(4,128)S(1)}, u32[]{:S(2)}, u32[]{:S(2)}) collective-permute-start(f32[3,4096]{1,0:T(4,128)S(1)} %get-tuple-element.43), channel_id=1, source_target_pairs={{0,8},{8,16},{16,24},{24,0},{1,9},{9,17},{17,25},{25,1},{2,10},{10... | collective-permute-start | bytes 147464 | tf_op jit(solution)/shard_map/ppermute | solution.py:151
  10.8 11.5 %collective-permute-start.3 = (f32[3,4096]{1,0:T(4,128)S(1)}, f32[3,4096]{1,0:T(4,128)S(1)}, u32[]{:S(2)}, u32[]{:S(2)}) collective-permute-start(f32[3,4096]{1,0:T(4,128)S(1)} %get-tuple-element.43), channel_id=1, source_target_pairs={{0,16},{8,24},{16,0},{24,8},{1,17},{9,25},{17,1},{25,9},{2,18},{10... | collective-permute-start | bytes 147464 | tf_op jit(solution)/shard_map/ppermute | solution.py:151
  13.1 9.2 %collective-permute-start.4 = (f32[3,4096]{1,0:T(4,128)S(1)}, f32[3,4096]{1,0:T(4,128)S(1)}, u32[]{:S(2)}, u32[]{:S(2)}) collective-permute-start(f32[3,4096]{1,0:T(4,128)S(1)} %get-tuple-element.43), channel_id=1, source_target_pairs={{0,24},{8,0},{16,8},{24,16},{1,25},{9,1},{17,9},{25,17},{2,26},{10... | collective-permute-start | bytes 147464 | tf_op jit(solution)/shard_map/ppermute | solution.py:151
  14.2 110.8 %reduce-scatter.2.cloned.1.call-start = ((), (), s32[]{:S(2)}) async-start(), calls=%async_computation.1 | async-start | bytes 2621440 | tf_op jit(solution)/shard_map/reduce_scatter | solution.py:203
  16.0 1.2 copy-start.5
  56.1 1.4 copy-start.2
  57.5 3.5 %copy-start.7 = (f32[30]{0:T(128)S(1)}, f32[30]{0:T(128)}, u32[]{:S(2)}) copy-start(f32[30]{0:T(128)} %param.18) | copy-start | bytes 364
  57.5 3.5 %copy-start.8 = (f32[30]{0:T(128)S(1)}, f32[30]{0:T(128)}, u32[]{:S(2)}) copy-start(f32[30]{0:T(128)} %param.17) | copy-start | bytes 364
  59.0 2.2 %copy-start = (f32[4,30,4096]{2,1,0:T(8,128)S(1)}, f32[4,30,4096]{2,1,0:T(8,128)}, u32[]{:S(2)}) copy-start(f32[4,30,4096]{2,1,0:T(8,128)} %all-gather.4.cloned.1.call-done) | copy-start | bytes 5898244
  65.7 1.7 %copy-start.3 = (f32[4,31,4096]{2,1,0:T(8,128)S(1)}, f32[4,31,4096]{2,1,0:T(8,128)}, u32[]{:S(2)}) copy-start(f32[4,31,4096]{2,1,0:T(8,128)} %copy-done.2) | copy-start | bytes 6094852
  67.4 1.2 copy-start.9
  72.2 1.5 %copy-start.1 = (f32[30,16,1024]{2,1,0:T(8,128)S(1)}, f32[30,16,1024]{2,1,0:T(8,128)}, u32[]{:S(2)}) copy-start(f32[30,16,1024]{2,1,0:T(8,128)} %param.10) | copy-start | bytes 5898244
  72.2 8.5 %copy-start.6 = (s32[4096]{0:T(1024)S(1)}, s32[4096]{0:T(1024)}, u32[]{:S(2)}) copy-start(s32[4096]{0:T(1024)} %param.16) | copy-start | bytes 49156
  74.0 45.8 %collective-permute-start = (f32[31,1,1024]{2,1,0:T(1,128)S(1)}, f32[31,1,1024]{2,1,0:T(1,128)S(1)}, u32[]{:S(2)}, u32[]{:S(2)}) collective-permute-start(f32[31,1,1024]{2,1,0:T(1,128)S(1)} %get-tuple-element.33), channel_id=1, source_target_pairs={{1,0},{2,1},{3,2},{4,3},{5,4},{6,5},{7,6},{9,8},{10,9},{11,10},{12... | collective-permute-start | bytes 380936 | tf_op jit(solution)/shard_map/ppermute | solution.py:23
  76.7 43.1 %collective-permute-start.1 = (f32[31,1,1024]{2,1,0:T(1,128)S(1)}, f32[31,1,1024]{2,1,0:T(1,128)S(1)}, u32[]{:S(2)}, u32[]{:S(2)}) collective-permute-start(f32[31,1,1024]{2,1,0:T(1,128)S(1)} %get-tuple-element.32), channel_id=1, source_target_pairs={{0,1},{1,2},{2,3},{3,4},{4,5},{5,6},{6,7},{8,9},{9,10},{10,11},{11... | collective-permute-start | bytes 380936 | tf_op jit(solution)/shard_map/ppermute | solution.py:20
  122.5 1.3 copy-start.4
  134.0 4.3 %collective-permute-start.5 = (f32[31,1024]{1,0:T(8,128)S(1)}, f32[31,1024]{1,0:T(8,128)S(1)}, u32[]{:S(2)}, u32[]{:S(2)}) collective-permute-start(f32[31,1024]{1,0:T(8,128)S(1)} %get-tuple-element.38), channel_id=1, source_target_pairs={{0,1},{1,2},{2,3},{3,4},{4,5},{5,6},{6,7},{8,9},{9,10},{10,11},{11... | collective-permute-start | bytes 380936 | tf_op jit(solution)/shard_map/ppermute | solution.py:31
  135.9 7.2 %collective-permute-start.6 = (f32[31,1024]{1,0:T(8,128)S(1)}, f32[31,1024]{1,0:T(8,128)S(1)}, u32[]{:S(2)}, u32[]{:S(2)}) collective-permute-start(f32[31,1024]{1,0:T(8,128)S(1)} %get-tuple-element.39), channel_id=1, source_target_pairs={{1,0},{2,1},{3,2},{4,3},{5,4},{6,5},{7,6},{9,8},{10,9},{11,10},{12... | collective-permute-start | bytes 380936 | tf_op jit(solution)/shard_map/ppermute | solution.py:31
Sparse Core Ops, SparseCore 0:
  14.3 44.6 all-gather.3
  72.4 42.1 reduce-scatter.1

commit v15 on v13

--- a/solution.py
+++ b/solution.py
@@ -63,20 +63,27 @@
 
 def pack_slots(state, chosen_sets):
     slot = jnp.full(chosen_sets[0].shape, -1, jnp.int32)
-    for i, chosen in enumerate(chosen_sets):
-        rank = jnp.cumsum(chosen.astype(jnp.int32)) - 1 + i * MOVE_CAP
-        slot = jnp.where(chosen, rank, slot)
-    columns = jnp.arange(len(chosen_sets) * MOVE_CAP, dtype=jnp.int32)
-    onehot = (slot[:, None] == columns[None, :]).astype(jnp.bfloat16)
+    for chosen in chosen_sets:
+        slot = jnp.where(chosen, jnp.cumsum(chosen.astype(jnp.int32)) - 1, slot)
+    onehot = (slot[:, None] == jnp.arange(MOVE_CAP, dtype=jnp.int32)[None, :]).astype(
+        jnp.bfloat16
+    )
     high = lax.reduce_precision(state, exponent_bits=8, mantissa_bits=7)
     rest = state - high
     middle = lax.reduce_precision(rest, exponent_bits=8, mantissa_bits=7)
     low = rest - middle
-    parts = jnp.concatenate([high, middle, low], axis=0).astype(jnp.bfloat16)
-    out = jnp.dot(parts, onehot, preferred_element_type=jnp.float32)
+    parts = jnp.concatenate([high, middle, low], axis=0)
+    picked = jnp.concatenate(
+        [jnp.where(chosen[None, :], parts, 0.0) for chosen in chosen_sets], axis=0
+    ).astype(jnp.bfloat16)
+    out = jnp.dot(picked, onehot, preferred_element_type=jnp.float32)
     rows = state.shape[0]
-    out = (out[:rows] + out[rows : 2 * rows]) + out[2 * rows :]
-    return [out[:, i * MOVE_CAP : (i + 1) * MOVE_CAP] for i in range(len(chosen_sets))]
+    span = 3 * rows
+    result = []
+    for i in range(len(chosen_sets)):
+        block = out[i * span : (i + 1) * span]
+        result.append((block[:rows] + block[rows : 2 * rows]) + block[2 * rows :])
+    return result
 
 
 def _gather_kernel(count_ref, dst_ref, src_ref, table_ref, out_ref):

time: 146 us -> 147 us (level)
  matrix products: 6.9 us -> 3.66 us
  other arithmetic: 34.9 us -> 36.9 us
    dot_general x1, matrix products: 6.9 us -> 3.66 us  [pack_slots(): out = jnp.dot(picked, onehot, preferred_element_type=jnp.float32)]
    another operation x6, other arithmetic: 2.65 us -> 1.06 us
    add x1, other arithmetic: 2.39 us -> 3.94 us  [body(): gas_next = plane_major(flowed + source)]
  transfers between devices with their start and end apart: 9 -> 9, of which waited for: 2 -> 2; matrix products, arithmetic and copies ran while one was open for 36% -> 32% of each run, Pallas kernels for 27% -> 27%
where the time goes in v15:
time: 147 us; the launch traced here: 146 us
  Pallas kernels  39.7 us (27%)
  other arithmetic  36.9 us (25%)
  local copies, waits for them, and re-layouts  30 us (20%)
  starting transfers between devices  15.8 us (11%)
  between operations  14.4 us (10%)
  waiting for transfers between devices  5.26 us (4%)
  matrix products  3.66 us (2%)
    pallas_call x1, Pallas kernels, row_scatter_add(): pl.pallas_call(_scatter_kernel, grid_spec=spec, out_shape=jax.ShapeDtypeS...  22.1 us
    pallas_call x1, Pallas kernels, row_gather(): pl.pallas_call(_gather_kernel, grid_spec=spec, out_shape=jax.ShapeDtypeSt...  17.6 us
    sort x1, other arithmetic, body(): lax.sort((keys, position, local_cell, seg), num_keys=1)  8.29 us
    reshape x1, local copies, waits for them, and re-layouts, body(): source = plane_major(summed.T.reshape(fields, width_x, width_yz))  6.48 us
    reshape x1, local copies, waits for them, and re-layouts, body(): terms_rows = terms_all.transpose(0, 2, 1).reshape(-1, fields)  6.3 us
    unnamed x26, local copies, waits for them, and re-layouts  6.2 us
    reduce_sum x4, other arithmetic, parcel_update(): slope = jnp.sum(part * excess * inv_denom, axis=0) + 0.1  5.83 us
    reshape x1, local copies, waits for them, and re-layouts, body(): gathered = gathered.reshape(blocks, -1, fields).transpose(0, 2, 1)  5.25 us
  transfers between devices with their start and end apart: 9, of which 2 were waited for; matrix products, arithmetic and copies ran while one was open for 32% of the time, Pallas kernels for 27%

profile of v15, /device:TPU:3, one launch (start us, length us, event | category | flops | bytes accessed | tf_op | source)
XLA Modules:
  0.0 145.7 jit_solution(8784276282635530996)
XLA Ops:
  10.8 2.3 %collective-permute-start.3 = (f32[3,4096]{1,0:T(4,128)S(1)}, f32[3,4096]{1,0:T(4,128)S(1)}, u32[]{:S(2)}, u32[]{:S(2)}) collective-permute-start(f32[3,4096]{1,0:T(4,128)S(1)} %get-tuple-element.44), channel_id=1, source_target_pairs={{0,16},{8,24},{16,0},{24,8},{1,17},{9,25},{17,1},{25,9},{2,18},{10... | collective-permute-start | bytes 147464 | tf_op jit(solution)/shard_map/ppermute | solution.py:158
  14.3 1.7 %pad.35 = f32[32,16,1024]{2,1,0:T(8,128)S(1)} pad(f32[30,16,1024]{2,1,0:T(8,128)} %param.10, f32[]{:T(128)} %constant.117.clone.1), padding=0_2x0_0x0_0 | pad | bytes 4063236
  17.5 4.8 %copy.24 = f32[31,16384]{0,1:T(8,128)} copy(f32[31,16384]{1,0:T(8,128)S(1)} %pad_maximum_fusion.1) | data formatting | bytes 4063232 | tf_op jit(solution)/shard_map/concatenate | solution.py:175
  23.5 8.3 %sort.27 = (s32[16384]{0:T(1024)}, s32[16384]{0:T(1024)}, s32[16384]{0:T(1024)}, s32[16384]{0:T(1024)}) sort(s32[16384]{0:T(1024)S(1)} %iota_add_fusion, s32[16384]{0:T(1024)S(1)} %iota.18, s32[16384]{0:T(1024)S(1)} %get-tuple-element.24, s32[16384]{0:T(1024)S(1)} %get-tuple-element.23), dimensions={0}, to_apply=%region_1.2 | sort | flops 229376 | bytes 524288 | tf_op jit(solution)/shard_map/sort | solution.py:193
  33.0 17.6 %shard_map.121 = f32[16384,31]{1,0:T(8,128)} custom-call(s32[1]{0:T(128)} %bitcast.9.count_ref, s32[16384]{0:T(1024)} %get-tuple-element.6.dst_ref.src_ref, s32[16384]{0:T(1024)} %get-tuple-element.8.src_ref, f32[16384,31]{1,0:T(8,128)} %bitcast.65), custom_call_target="tpu_custom_call" | custom-call | tf_op jit(solution)/shard_map/pallas_call | solution.py:131
  50.6 5.2 %copy.26 = f32[4,4096,31]{1,2,0:T(8,128)S(1)} copy(f32[4,4096,31]{2,1,0:T(8,128)} %bitcast.68) | data formatting | bytes 4063232 | tf_op jit(solution)/shard_map/reshape | solution.py:201
  59.0 2.0 %reduce_sum.102 = f32[4,4096]{1,0:T(4,128)S(1)} reduce(f32[4,30,4096]{2,1,0:T(8,128)} %all-gather.4.cloned.1.call-done, f32[]{:T(128)} %constant.117.clone.1), dimensions={1}, to_apply=%region_2.3 | reduce | flops 475136 | bytes 2031620 | tf_op jit(solution)/shard_map/vmap()/reduce_sum | solution.py:35
  62.7 1.5 %multiply_reduce_fusion.3 = (f32[4,4096]{1,0:T(4,128)S(1)}, f32[4,4096]{1,0:T(4,128)S(1)}) fusion(f32[4,4096]{1,0:T(4,128)S(1)} %add_clamp_fusion.3, f32[4,4096]{1,0:T(4,128)S(1)} %bitcast.72, f32[30]{0:T(128)S(1)} %copy-done.7, f32[30]{0:T(128)S(1)} %copy-done.8, f32[4,30,4096]{2,1,0:T(8,128)S(1)} %copy-done, f32[4,4096]{1,0:T(4,128)S(1)} %get-tuple-element.42), kind=kLoop, calls=%fused_computation.19 | loop fusion | flops 6356992 | bytes 2294000 | tf_op jit(solution)/shard_map/vmap()/reduce_sum | solution.py:47
  64.2 1.5 %multiply_reduce_fusion.2 = (f32[4,4096]{1,0:T(4,128)S(1)}, f32[4,4096]{1,0:T(4,128)S(1)}) fusion(f32[4,4096]{1,0:T(4,128)S(1)} %add_clamp_fusion.2, f32[4,4096]{1,0:T(4,128)S(1)} %bitcast.73, f32[30]{0:T(128)S(1)} %copy-done.7, f32[30]{0:T(128)S(1)} %copy-done.8, f32[4,30,4096]{2,1,0:T(8,128)S(1)} %copy-done, f32[4,4096]{1,0:T(4,128)S(1)} %get-tuple-element.42), kind=kLoop, calls=%fused_computation.17 | loop fusion | flops 6356992 | bytes 2294000 | tf_op jit(solution)/shard_map/vmap()/reduce_sum | solution.py:47
  65.7 1.5 %multiply_reduce_fusion.1 = (f32[4,4096]{1,0:T(4,128)S(1)}, f32[4,4096]{1,0:T(4,128)S(1)}) fusion(f32[4,4096]{1,0:T(4,128)S(1)} %add_clamp_fusion.1, f32[4,4096]{1,0:T(4,128)S(1)} %bitcast.74, f32[30]{0:T(128)S(1)} %copy-done.7, f32[30]{0:T(128)S(1)} %copy-done.8, f32[4,30,4096]{2,1,0:T(8,128)S(1)} %copy-done, f32[4,4096]{1,0:T(4,128)S(1)} %get-tuple-element.42), kind=kLoop, calls=%fused_computation.15 | loop fusion | flops 6356992 | bytes 2294000 | tf_op jit(solution)/shard_map/vmap()/reduce_sum | solution.py:47
  68.6 1.7 %multiply_reduce_fusion = (f32[4,4096]{1,0:T(4,128)S(1)}, f32[4,30,4096]{2,1,0:T(8,128)}) fusion(f32[4,30,4096]{2,1,0:T(8,128)S(1)} %get-tuple-element.22, f32[30]{0:T(128)S(1)} %copy-done.9), kind=kLoop, calls=%fused_computation.14 | loop fusion | flops 1458176 | bytes 3997816 | tf_op jit(solution)/shard_map/vmap()/reduce_sum | solution.py:56
  70.6 1.6 %maximum_select_fusion = f32[4,31,4096]{2,1,0:T(8,128)} fusion(f32[4,1,4096]{2,1,0:T(1,128)S(1)} %get-tuple-element.28, f32[4,30,4096]{2,1,0:T(8,128)S(1)} %get-tuple-element.21, pred[4,4096]{1,0:T(4,128)(4,1)S(1)} %bitcast.84), kind=kLoop, calls=%fused_computation.13 | loop fusion | flops 1015808 | bytes 4079616 | tf_op jit(solution)/shard_map/jit(_where)/select_n | solution.py:209
  72.2 1.5 %copy-done.1 = f32[30,16,1024]{2,1,0:T(8,128)S(1)} copy-done((f32[30,16,1024]{2,1,0:T(8,128)S(1)}, f32[30,16,1024]{2,1,0:T(8,128)}, u32[]{:S(2)}) %copy-start.1) | copy-done | bytes 1966104
  74.0 2.7 %collective-permute-start = (f32[31,1,1024]{2,1,0:T(1,128)S(1)}, f32[31,1,1024]{2,1,0:T(1,128)S(1)}, u32[]{:S(2)}, u32[]{:S(2)}) collective-permute-start(f32[31,1,1024]{2,1,0:T(1,128)S(1)} %get-tuple-element.33), channel_id=1, source_target_pairs={{1,0},{2,1},{3,2},{4,3},{5,4},{6,5},{7,6},{9,8},{10,9},{11,10},{12... | collective-permute-start | bytes 380936 | tf_op jit(solution)/shard_map/ppermute | solution.py:23
  76.7 3.9 %collective-permute-start.1 = (f32[31,1,1024]{2,1,0:T(1,128)S(1)}, f32[31,1,1024]{2,1,0:T(1,128)S(1)}, u32[]{:S(2)}, u32[]{:S(2)}) collective-permute-start(f32[31,1,1024]{2,1,0:T(1,128)S(1)} %get-tuple-element.32), channel_id=1, source_target_pairs={{0,1},{1,2},{2,3},{3,4},{4,5},{5,6},{6,7},{8,9},{9,10},{10,11},{11... | collective-permute-start | bytes 380936 | tf_op jit(solution)/shard_map/ppermute | solution.py:20
  81.7 3.2 %maximum_bitcast_fusion = f32[4,4096,31]{1,2,0:T(8,128)} fusion(f32[4,1,4096]{2,1,0:T(1,128)S(1)} %get-tuple-element.29, f32[4,30,4096]{2,1,0:T(8,128)} %get-tuple-element.31), kind=kLoop, calls=%fused_computation.12 | loop fusion | flops 507904 | bytes 4063232 | tf_op jit(solution)/shard_map/transpose | solution.py:217
  85.0 6.3 %copy.33 = f32[4,4096,31]{2,1,0:T(8,128)} copy(f32[4,4096,31]{1,2,0:T(8,128)} %maximum_bitcast_fusion) | data formatting | bytes 4063232 | tf_op jit(solution)/shard_map/reshape | solution.py:217
  91.2 22.1 %shard_map.122 = f32[16384,31]{1,0:T(8,128)} custom-call(s32[1]{0:T(128)} %bitcast.9.count_ref, s32[16384]{0:T(1024)} %get-tuple-element.6.dst_ref.src_ref, s32[16384]{0:T(1024)} %get-tuple-element.7.seg_ref, f32[16384,31]{1,0:T(8,128)} %bitcast.66), custom_call_target="tpu_custom_call" | custom-call | tf_op jit(solution)/shard_map/pallas_call | solution.py:147
  113.3 6.5 %copy.34 = f32[31,16,1024]{2,1,0:T(8,128)} copy(f32[31,16,1024]{0,2,1:T(8,128)} %bitcast.67) | data formatting | bytes 4063232 | tf_op jit(solution)/shard_map/reshape | solution.py:219
  119.8 3.9 %fusion.9 = f32[31,16,1024]{2,1,0:T(8,128)} fusion(f32[31,16,1024]{2,1,0:T(8,128)} %copy.34, f32[31,1,1024]{2,1,0:T(1,128)S(1)} %collective-permute-done, f32[1,16,1024]{2,1,0:T(8,128)S(1)} %bitcast.78, f32[30,16,1024]{2,1,0:T(8,128)S(1)} %copy-done.1, f32[31,1,1024]{2,1,0:T(1,128)S(1)} %collective-permute-done.1), kind=kLoop, calls=%fused_computation.32 | loop fusion | flops 7110656 | bytes 6348800 | tf_op jit(solution)/shard_map/add | solution.py:220
  125.3 3.7 %fusion = f32[186,1024]{1,0:T(8,128)S(1)} fusion(s32[4096]{0:T(1024)S(1)} %fusion.32, bf16[93,4096]{1,0:T(8,128)(2,1)S(1)} %get-tuple-element.37, bf16[93,4096]{1,0:T(8,128)(2,1)S(1)} %get-tuple-element.36), kind=kOutput, calls=%fused_computation.2 | convolution fusion | flops 1567522816 | bytes 2301952 | tf_op jit(solution)/shard_map/dot_general | solution.py:79
  129.0 1.9 %collective-permute-start.5 = (f32[31,1024]{1,0:T(8,128)S(1)}, f32[31,1024]{1,0:T(8,128)S(1)}, u32[]{:S(2)}, u32[]{:S(2)}) collective-permute-start(f32[31,1024]{1,0:T(8,128)S(1)} %get-tuple-element.34), channel_id=1, source_target_pairs={{0,1},{1,2},{2,3},{3,4},{4,5},{5,6},{6,7},{8,9},{9,10},{10,11},{11... | collective-permute-start | bytes 380936 | tf_op jit(solution)/shard_map/ppermute | solution.py:31
  131.0 2.4 %collective-permute-start.6 = (f32[31,1024]{1,0:T(8,128)S(1)}, f32[31,1024]{1,0:T(8,128)S(1)}, u32[]{:S(2)}, u32[]{:S(2)}) collective-permute-start(f32[31,1024]{1,0:T(8,128)S(1)} %get-tuple-element.35), channel_id=1, source_target_pairs={{1,0},{2,1},{3,2},{4,3},{5,4},{6,5},{7,6},{9,8},{10,9},{11,10},{12... | collective-permute-start | bytes 380936 | tf_op jit(solution)/shard_map/ppermute | solution.py:31
  134.2 3.9 %collective-permute-done.6 = f32[31,1024]{1,0:T(8,128)S(1)} collective-permute-done((f32[31,1024]{1,0:T(8,128)S(1)}, f32[31,1024]{1,0:T(8,128)S(1)}, u32[]{:S(2)}, u32[]{:S(2)}) %collective-permute-start.6) | collective-permute-done | bytes 127008 | tf_op jit(solution)/shard_map/ppermute | solution.py:31
  (80 shorter events, 19.4 us)
Async XLA Ops:
  7.2 51.8 %all-gather.4.cloned.1.call-start = ((), (), s32[]{:S(2)}) async-start(), calls=%async_computation.2 | async-start | bytes 2621440 | tf_op jit(solution)/shard_map/all_gather | solution.py:181
  9.4 12.9 %collective-permute-start.2 = (f32[3,4096]{1,0:T(4,128)S(1)}, f32[3,4096]{1,0:T(4,128)S(1)}, u32[]{:S(2)}, u32[]{:S(2)}) collective-permute-start(f32[3,4096]{1,0:T(4,128)S(1)} %get-tuple-element.44), channel_id=1, source_target_pairs={{0,8},{8,16},{16,24},{24,0},{1,9},{9,17},{17,25},{25,1},{2,10},{10... | collective-permute-start | bytes 147464 | tf_op jit(solution)/shard_map/ppermute | solution.py:158
  10.8 11.5 %collective-permute-start.3 = (f32[3,4096]{1,0:T(4,128)S(1)}, f32[3,4096]{1,0:T(4,128)S(1)}, u32[]{:S(2)}, u32[]{:S(2)}) collective-permute-start(f32[3,4096]{1,0:T(4,128)S(1)} %get-tuple-element.44), channel_id=1, source_target_pairs={{0,16},{8,24},{16,0},{24,8},{1,17},{9,25},{17,1},{25,9},{2,18},{10... | collective-permute-start | bytes 147464 | tf_op jit(solution)/shard_map/ppermute | solution.py:158
  13.1 9.2 %collective-permute-start.4 = (f32[3,4096]{1,0:T(4,128)S(1)}, f32[3,4096]{1,0:T(4,128)S(1)}, u32[]{:S(2)}, u32[]{:S(2)}) collective-permute-start(f32[3,4096]{1,0:T(4,128)S(1)} %get-tuple-element.44), channel_id=1, source_target_pairs={{0,24},{8,0},{16,8},{24,16},{1,25},{9,1},{17,9},{25,17},{2,26},{10... | collective-permute-start | bytes 147464 | tf_op jit(solution)/shard_map/ppermute | solution.py:158
  14.2 109.6 %reduce-scatter.2.cloned.1.call-start = ((), (), s32[]{:S(2)}) async-start(), calls=%async_computation.1 | async-start | bytes 2621440 | tf_op jit(solution)/shard_map/reduce_scatter | solution.py:210
  16.0 1.2 copy-start.5
  56.1 1.4 copy-start.2
  57.5 3.5 %copy-start.7 = (f32[30]{0:T(128)S(1)}, f32[30]{0:T(128)}, u32[]{:S(2)}) copy-start(f32[30]{0:T(128)} %param.18) | copy-start | bytes 364
  57.5 3.5 %copy-start.8 = (f32[30]{0:T(128)S(1)}, f32[30]{0:T(128)}, u32[]{:S(2)}) copy-start(f32[30]{0:T(128)} %param.17) | copy-start | bytes 364
  59.0 2.2 %copy-start = (f32[4,30,4096]{2,1,0:T(8,128)S(1)}, f32[4,30,4096]{2,1,0:T(8,128)}, u32[]{:S(2)}) copy-start(f32[4,30,4096]{2,1,0:T(8,128)} %all-gather.4.cloned.1.call-done) | copy-start | bytes 5898244
  65.7 1.7 %copy-start.3 = (f32[4,31,4096]{2,1,0:T(8,128)S(1)}, f32[4,31,4096]{2,1,0:T(8,128)}, u32[]{:S(2)}) copy-start(f32[4,31,4096]{2,1,0:T(8,128)} %copy-done.2) | copy-start | bytes 6094852
  67.4 1.2 copy-start.9
  72.2 1.5 %copy-start.1 = (f32[30,16,1024]{2,1,0:T(8,128)S(1)}, f32[30,16,1024]{2,1,0:T(8,128)}, u32[]{:S(2)}) copy-start(f32[30,16,1024]{2,1,0:T(8,128)} %param.10) | copy-start | bytes 5898244
  72.2 8.5 %copy-start.6 = (s32[4096]{0:T(1024)S(1)}, s32[4096]{0:T(1024)}, u32[]{:S(2)}) copy-start(s32[4096]{0:T(1024)} %param.16) | copy-start | bytes 49156
  74.0 45.8 %collective-permute-start = (f32[31,1,1024]{2,1,0:T(1,128)S(1)}, f32[31,1,1024]{2,1,0:T(1,128)S(1)}, u32[]{:S(2)}, u32[]{:S(2)}) collective-permute-start(f32[31,1,1024]{2,1,0:T(1,128)S(1)} %get-tuple-element.33), channel_id=1, source_target_pairs={{1,0},{2,1},{3,2},{4,3},{5,4},{6,5},{7,6},{9,8},{10,9},{11,10},{12... | collective-permute-start | bytes 380936 | tf_op jit(solution)/shard_map/ppermute | solution.py:23
  76.7 43.1 %collective-permute-start.1 = (f32[31,1,1024]{2,1,0:T(1,128)S(1)}, f32[31,1,1024]{2,1,0:T(1,128)S(1)}, u32[]{:S(2)}, u32[]{:S(2)}) collective-permute-start(f32[31,1,1024]{2,1,0:T(1,128)S(1)} %get-tuple-element.32), channel_id=1, source_target_pairs={{0,1},{1,2},{2,3},{3,4},{4,5},{5,6},{6,7},{8,9},{9,10},{10,11},{11... | collective-permute-start | bytes 380936 | tf_op jit(solution)/shard_map/ppermute | solution.py:20
  125.3 8.1 %copy-start.4 = (f32[1,31,4096]{2,1,0:T(8,128)S(1)}, f32[1,31,4096]{2,1,0:T(8,128)}, u32[]{:S(2)}) copy-start(f32[1,31,4096]{2,1,0:T(8,128)} %reduce-scatter.2.cloned.1.call-done) | copy-start | bytes 1523716
  129.0 5.2 %collective-permute-start.5 = (f32[31,1024]{1,0:T(8,128)S(1)}, f32[31,1024]{1,0:T(8,128)S(1)}, u32[]{:S(2)}, u32[]{:S(2)}) collective-permute-start(f32[31,1024]{1,0:T(8,128)S(1)} %get-tuple-element.34), channel_id=1, source_target_pairs={{0,1},{1,2},{2,3},{3,4},{4,5},{5,6},{6,7},{8,9},{9,10},{10,11},{11... | collective-permute-start | bytes 380936 | tf_op jit(solution)/shard_map/ppermute | solution.py:31
  131.0 7.2 %collective-permute-start.6 = (f32[31,1024]{1,0:T(8,128)S(1)}, f32[31,1024]{1,0:T(8,128)S(1)}, u32[]{:S(2)}, u32[]{:S(2)}) collective-permute-start(f32[31,1024]{1,0:T(8,128)S(1)} %get-tuple-element.35), channel_id=1, source_target_pairs={{1,0},{2,1},{3,2},{4,3},{5,4},{6,5},{7,6},{9,8},{10,9},{11,10},{12... | collective-permute-start | bytes 380936 | tf_op jit(solution)/shard_map/ppermute | solution.py:31
Sparse Core Ops, SparseCore 0:
  14.3 44.6 all-gather.3
  72.4 42.1 reduce-scatter.1
